TPU v7x, 256 devices: a whole 4x4x8 slice. The times are simulated.
256 devices in a mesh: ctx: 32 (over z, x), tp: 8 (over y, core).
Axes of the slice: x: 4, y: 4, z: 8, core: 2. Of those that a mesh axis runs over, the one named last changes fastest.
Arguments:
- tokens: bfloat16 [16384, 3072], P(('ctx', 'tp')), may hold values from -6 to 6
- w_query: bfloat16 [3072, 4096], P(None, 'tp'), may hold values from -0.109375 to 0.109375
- w_key: bfloat16 [3072, 4096], P(None, 'tp'), may hold values from -0.109375 to 0.109375
- w_value: bfloat16 [3072, 4096], P(None, 'tp'), may hold values from -0.109375 to 0.109375
- norm_gain: float32 [4096], P('tp'), may hold values from 0.1 to 1.9
Outputs:
- attended: bfloat16 [16384, 4096], P('ctx', 'tp')
All inputs are finite; a program needn't handle non-finite values.
Results may differ from a plain program's by a relative error of at most 0.0062.
Values may be sent and summed in bfloat16 or wider, within the bound.
No kernel may reach another device: no remote copies, remote signals or barrier semaphores. Data moves between devices by JAX's collectives and lax.ppermute only.
A program may use at most 64 MiB of HBM per device.

v0:
```python
import jax
import jax.numpy as jnp
from jax import lax
from jax.sharding import PartitionSpec as P

HEAD_DIM = 128
BLOCK = 512


EPSILON = 1e-06


def from_behind(value, axis, by):
    size = lax.axis_size(axis)
    pairs = [(i, i + by) for i in range(size) if 0 <= i + by < size]
    return lax.ppermute(value, axis, pairs)


def body(tokens, w_query, w_key, w_value, norm_gain):
    local_width = w_query.shape[1]
    head_count = local_width // HEAD_DIM
    piece_rows = lax.all_gather(tokens, "tp", axis=0, tiled=True)
    query_part = jnp.dot(piece_rows, w_query, preferred_element_type=jnp.float32).astype(
        jnp.bfloat16
    )
    key_part = jnp.dot(piece_rows, w_key, preferred_element_type=jnp.float32).astype(jnp.bfloat16)
    value_part = jnp.dot(piece_rows, w_value, preferred_element_type=jnp.float32).astype(
        jnp.bfloat16
    )
    projected = jnp.concatenate([query_part, key_part, value_part], axis=1)
    group_len = projected.shape[0]
    block_count = group_len // BLOCK
    shaped = projected.reshape(block_count, BLOCK, 3, head_count, HEAD_DIM)
    query_rows = shaped[:, :, 0]
    key_rows = shaped[:, :, 1]
    value_rows = shaped[:, :, 2]
    block_states = jnp.einsum(
        "bshd,bshe->bhde", key_rows, value_rows, preferred_element_type=jnp.float32
    )
    local_state = jnp.sum(block_states, axis=0)
    empty_state = jnp.zeros_like(local_state)

    def advance(step_index, carried):
        return from_behind(carried + local_state, "ctx", 1)

    prefix_state = lax.fori_loop(0, lax.axis_size("ctx") - 1, advance, empty_state)
    running = jnp.cumsum(block_states, axis=0)
    earlier = jnp.concatenate([jnp.zeros_like(block_states), running[:-1]], axis=0)
    block_start = prefix_state[None] + earlier
    scores = jnp.einsum("bqhd,bkhd->bhqk", query_rows, key_rows, preferred_element_type=jnp.float32)
    causal = jnp.arange(BLOCK)[:, None] >= jnp.arange(BLOCK)[None, :]
    scores = jnp.where(causal[None, None], scores, jnp.float32(0.0)).astype(jnp.bfloat16)
    inner = jnp.einsum("bhqk,bkhe->bqhe", scores, value_rows, preferred_element_type=jnp.float32)
    carried_part = jnp.einsum(
        "bqhd,bhde->bqhe",
        query_rows.astype(jnp.float32),
        block_start,
        precision=lax.Precision.HIGHEST,
    )
    mixed = inner + carried_part
    mean_square = jnp.mean(mixed * mixed, axis=-1, keepdims=True)
    normed = mixed * lax.rsqrt(mean_square + EPSILON) * norm_gain.reshape(head_count, HEAD_DIM)
    return normed.reshape(group_len, local_width).astype(jnp.bfloat16)


def solution(mesh):
    placed = (P(("ctx", "tp"), None), P(None, "tp"), P(None, "tp"), P(None, "tp"), P("tp"))
    return jax.shard_map(
        body, mesh=mesh, in_specs=placed, out_specs=P("ctx", "tp"), check_vma=False
    )
```

profile of v0, /device:TPU:128, one launch (start us, length us, event | category | flops | bytes accessed | tf_op | source)
XLA Modules:
  0.0 505.0 jit_solution(23542777974359117)
XLA Ops:
  8.0 32.9 %all-gather.2.cloned.1.call-done = bf16[512,3072]{1,0:T(8,128)(2,1)} async-done(((bf16[64,3072]{1,0:T(8,128)(2,1)}), bf16[512,3072]{1,0:T(8,128)(2,1)}) %all-gather.2.cloned.1.call-update) | async-done | bytes 3145744 | tf_op jit(solution)/shard_map/all_gather | solution.py:22
  41.0 3.9 convolution_convert_fusion
  50.9 436.2 %while.10 = (s32[]{:T(128)}, f32[4,128,128]{2,1,0:T(8,128)S(1)}, f32[4,128,128]{2,1,0:T(8,128)}, s32[]{:T(128)}) while((s32[]{:T(128)}, f32[4,128,128]{2,1,0:T(8,128)S(1)}, f32[4,128,128]{2,1,0:T(8,128)}, s32[]{:T(128)}) %tuple.19), condition=%wide.region_1.0_spmd, body=%wide.region_0.0_spmd.sunk | while | flops 65538 | bytes 1835101 | solution.py:46
  52.6 3.4 collective-permute-start
  56.0 10.5 %collective-permute-done = f32[4,128,128]{2,1,0:T(8,128)S(1)} collective-permute-done((f32[4,128,128]{2,1,0:T(8,128)}, f32[4,128,128]{2,1,0:T(8,128)S(1)}, u32[]{:S(2)}, u32[]{:S(2)}) %collective-permute-start) | collective-permute-done | bytes 262176 | tf_op jit(solution)/shard_map/while/body/eval_jaxpr/ppermute | solution.py:16
  68.1 1.9 collective-permute-start
  70.0 11.1 %collective-permute-done = f32[4,128,128]{2,1,0:T(8,128)S(1)} collective-permute-done((f32[4,128,128]{2,1,0:T(8,128)}, f32[4,128,128]{2,1,0:T(8,128)S(1)}, u32[]{:S(2)}, u32[]{:S(2)}) %collective-permute-start) | collective-permute-done | bytes 262176 | tf_op jit(solution)/shard_map/while/body/eval_jaxpr/ppermute | solution.py:16
  84.7 10.2 %collective-permute-done = f32[4,128,128]{2,1,0:T(8,128)S(1)} collective-permute-done((f32[4,128,128]{2,1,0:T(8,128)}, f32[4,128,128]{2,1,0:T(8,128)S(1)}, u32[]{:S(2)}, u32[]{:S(2)}) %collective-permute-start) | collective-permute-done | bytes 262176 | tf_op jit(solution)/shard_map/while/body/eval_jaxpr/ppermute | solution.py:16
  98.5 9.9 %collective-permute-done = f32[4,128,128]{2,1,0:T(8,128)S(1)} collective-permute-done((f32[4,128,128]{2,1,0:T(8,128)}, f32[4,128,128]{2,1,0:T(8,128)S(1)}, u32[]{:S(2)}, u32[]{:S(2)}) %collective-permute-start) | collective-permute-done | bytes 262176 | tf_op jit(solution)/shard_map/while/body/eval_jaxpr/ppermute | solution.py:16
  110.1 1.9 collective-permute-start
  112.0 9.9 %collective-permute-done = f32[4,128,128]{2,1,0:T(8,128)S(1)} collective-permute-done((f32[4,128,128]{2,1,0:T(8,128)}, f32[4,128,128]{2,1,0:T(8,128)S(1)}, u32[]{:S(2)}, u32[]{:S(2)}) %collective-permute-start) | collective-permute-done | bytes 262176 | tf_op jit(solution)/shard_map/while/body/eval_jaxpr/ppermute | solution.py:16
  123.5 1.9 collective-permute-start
  125.4 9.9 %collective-permute-done = f32[4,128,128]{2,1,0:T(8,128)S(1)} collective-permute-done((f32[4,128,128]{2,1,0:T(8,128)}, f32[4,128,128]{2,1,0:T(8,128)S(1)}, u32[]{:S(2)}, u32[]{:S(2)}) %collective-permute-start) | collective-permute-done | bytes 262176 | tf_op jit(solution)/shard_map/while/body/eval_jaxpr/ppermute | solution.py:16
  137.0 1.9 collective-permute-start
  138.9 9.9 %collective-permute-done = f32[4,128,128]{2,1,0:T(8,128)S(1)} collective-permute-done((f32[4,128,128]{2,1,0:T(8,128)}, f32[4,128,128]{2,1,0:T(8,128)S(1)}, u32[]{:S(2)}, u32[]{:S(2)}) %collective-permute-start) | collective-permute-done | bytes 262176 | tf_op jit(solution)/shard_map/while/body/eval_jaxpr/ppermute | solution.py:16
  150.4 1.9 collective-permute-start
  152.3 9.9 %collective-permute-done = f32[4,128,128]{2,1,0:T(8,128)S(1)} collective-permute-done((f32[4,128,128]{2,1,0:T(8,128)}, f32[4,128,128]{2,1,0:T(8,128)S(1)}, u32[]{:S(2)}, u32[]{:S(2)}) %collective-permute-start) | collective-permute-done | bytes 262176 | tf_op jit(solution)/shard_map/while/body/eval_jaxpr/ppermute | solution.py:16
  163.9 1.9 collective-permute-start
  165.8 9.9 %collective-permute-done = f32[4,128,128]{2,1,0:T(8,128)S(1)} collective-permute-done((f32[4,128,128]{2,1,0:T(8,128)}, f32[4,128,128]{2,1,0:T(8,128)S(1)}, u32[]{:S(2)}, u32[]{:S(2)}) %collective-permute-start) | collective-permute-done | bytes 262176 | tf_op jit(solution)/shard_map/while/body/eval_jaxpr/ppermute | solution.py:16
  179.3 10.6 %collective-permute-done = f32[4,128,128]{2,1,0:T(8,128)S(1)} collective-permute-done((f32[4,128,128]{2,1,0:T(8,128)}, f32[4,128,128]{2,1,0:T(8,128)S(1)}, u32[]{:S(2)}, u32[]{:S(2)}) %collective-permute-start) | collective-permute-done | bytes 262176 | tf_op jit(solution)/shard_map/while/body/eval_jaxpr/ppermute | solution.py:16
  191.5 1.9 collective-permute-start
  193.4 11.7 %collective-permute-done = f32[4,128,128]{2,1,0:T(8,128)S(1)} collective-permute-done((f32[4,128,128]{2,1,0:T(8,128)}, f32[4,128,128]{2,1,0:T(8,128)S(1)}, u32[]{:S(2)}, u32[]{:S(2)}) %collective-permute-start) | collective-permute-done | bytes 262176 | tf_op jit(solution)/shard_map/while/body/eval_jaxpr/ppermute | solution.py:16
  206.8 1.9 collective-permute-start
  208.7 12.5 %collective-permute-done = f32[4,128,128]{2,1,0:T(8,128)S(1)} collective-permute-done((f32[4,128,128]{2,1,0:T(8,128)}, f32[4,128,128]{2,1,0:T(8,128)S(1)}, u32[]{:S(2)}, u32[]{:S(2)}) %collective-permute-start) | collective-permute-done | bytes 262176 | tf_op jit(solution)/shard_map/while/body/eval_jaxpr/ppermute | solution.py:16
  222.9 1.9 collective-permute-start
  224.8 11.6 %collective-permute-done = f32[4,128,128]{2,1,0:T(8,128)S(1)} collective-permute-done((f32[4,128,128]{2,1,0:T(8,128)}, f32[4,128,128]{2,1,0:T(8,128)S(1)}, u32[]{:S(2)}, u32[]{:S(2)}) %collective-permute-start) | collective-permute-done | bytes 262176 | tf_op jit(solution)/shard_map/while/body/eval_jaxpr/ppermute | solution.py:16
  240.0 10.8 %collective-permute-done = f32[4,128,128]{2,1,0:T(8,128)S(1)} collective-permute-done((f32[4,128,128]{2,1,0:T(8,128)}, f32[4,128,128]{2,1,0:T(8,128)S(1)}, u32[]{:S(2)}, u32[]{:S(2)}) %collective-permute-start) | collective-permute-done | bytes 262176 | tf_op jit(solution)/shard_map/while/body/eval_jaxpr/ppermute | solution.py:16
  254.4 9.9 %collective-permute-done = f32[4,128,128]{2,1,0:T(8,128)S(1)} collective-permute-done((f32[4,128,128]{2,1,0:T(8,128)}, f32[4,128,128]{2,1,0:T(8,128)S(1)}, u32[]{:S(2)}, u32[]{:S(2)}) %collective-permute-start) | collective-permute-done | bytes 262176 | tf_op jit(solution)/shard_map/while/body/eval_jaxpr/ppermute | solution.py:16
  267.9 9.9 %collective-permute-done = f32[4,128,128]{2,1,0:T(8,128)S(1)} collective-permute-done((f32[4,128,128]{2,1,0:T(8,128)}, f32[4,128,128]{2,1,0:T(8,128)S(1)}, u32[]{:S(2)}, u32[]{:S(2)}) %collective-permute-start) | collective-permute-done | bytes 262176 | tf_op jit(solution)/shard_map/while/body/eval_jaxpr/ppermute | solution.py:16
  281.3 9.9 %collective-permute-done = f32[4,128,128]{2,1,0:T(8,128)S(1)} collective-permute-done((f32[4,128,128]{2,1,0:T(8,128)}, f32[4,128,128]{2,1,0:T(8,128)S(1)}, u32[]{:S(2)}, u32[]{:S(2)}) %collective-permute-start) | collective-permute-done | bytes 262176 | tf_op jit(solution)/shard_map/while/body/eval_jaxpr/ppermute | solution.py:16
  294.8 9.9 %collective-permute-done = f32[4,128,128]{2,1,0:T(8,128)S(1)} collective-permute-done((f32[4,128,128]{2,1,0:T(8,128)}, f32[4,128,128]{2,1,0:T(8,128)S(1)}, u32[]{:S(2)}, u32[]{:S(2)}) %collective-permute-start) | collective-permute-done | bytes 262176 | tf_op jit(solution)/shard_map/while/body/eval_jaxpr/ppermute | solution.py:16
  308.3 9.9 %collective-permute-done = f32[4,128,128]{2,1,0:T(8,128)S(1)} collective-permute-done((f32[4,128,128]{2,1,0:T(8,128)}, f32[4,128,128]{2,1,0:T(8,128)S(1)}, u32[]{:S(2)}, u32[]{:S(2)}) %collective-permute-start) | collective-permute-done | bytes 262176 | tf_op jit(solution)/shard_map/while/body/eval_jaxpr/ppermute | solution.py:16
  321.7 9.9 %collective-permute-done = f32[4,128,128]{2,1,0:T(8,128)S(1)} collective-permute-done((f32[4,128,128]{2,1,0:T(8,128)}, f32[4,128,128]{2,1,0:T(8,128)S(1)}, u32[]{:S(2)}, u32[]{:S(2)}) %collective-permute-start) | collective-permute-done | bytes 262176 | tf_op jit(solution)/shard_map/while/body/eval_jaxpr/ppermute | solution.py:16
  335.2 9.9 %collective-permute-done = f32[4,128,128]{2,1,0:T(8,128)S(1)} collective-permute-done((f32[4,128,128]{2,1,0:T(8,128)}, f32[4,128,128]{2,1,0:T(8,128)S(1)}, u32[]{:S(2)}, u32[]{:S(2)}) %collective-permute-start) | collective-permute-done | bytes 262176 | tf_op jit(solution)/shard_map/while/body/eval_jaxpr/ppermute | solution.py:16
  348.6 10.9 %collective-permute-done = f32[4,128,128]{2,1,0:T(8,128)S(1)} collective-permute-done((f32[4,128,128]{2,1,0:T(8,128)}, f32[4,128,128]{2,1,0:T(8,128)S(1)}, u32[]{:S(2)}, u32[]{:S(2)}) %collective-permute-start) | collective-permute-done | bytes 262176 | tf_op jit(solution)/shard_map/while/body/eval_jaxpr/ppermute | solution.py:16
  363.1 12.0 %collective-permute-done = f32[4,128,128]{2,1,0:T(8,128)S(1)} collective-permute-done((f32[4,128,128]{2,1,0:T(8,128)}, f32[4,128,128]{2,1,0:T(8,128)S(1)}, u32[]{:S(2)}, u32[]{:S(2)}) %collective-permute-start) | collective-permute-done | bytes 262176 | tf_op jit(solution)/shard_map/while/body/eval_jaxpr/ppermute | solution.py:16
  378.7 12.2 %collective-permute-done = f32[4,128,128]{2,1,0:T(8,128)S(1)} collective-permute-done((f32[4,128,128]{2,1,0:T(8,128)}, f32[4,128,128]{2,1,0:T(8,128)S(1)}, u32[]{:S(2)}, u32[]{:S(2)}) %collective-permute-start) | collective-permute-done | bytes 262176 | tf_op jit(solution)/shard_map/while/body/eval_jaxpr/ppermute | solution.py:16
  394.5 11.3 %collective-permute-done = f32[4,128,128]{2,1,0:T(8,128)S(1)} collective-permute-done((f32[4,128,128]{2,1,0:T(8,128)}, f32[4,128,128]{2,1,0:T(8,128)S(1)}, u32[]{:S(2)}, u32[]{:S(2)}) %collective-permute-start) | collective-permute-done | bytes 262176 | tf_op jit(solution)/shard_map/while/body/eval_jaxpr/ppermute | solution.py:16
  409.4 10.5 %collective-permute-done = f32[4,128,128]{2,1,0:T(8,128)S(1)} collective-permute-done((f32[4,128,128]{2,1,0:T(8,128)}, f32[4,128,128]{2,1,0:T(8,128)S(1)}, u32[]{:S(2)}, u32[]{:S(2)}) %collective-permute-start) | collective-permute-done | bytes 262176 | tf_op jit(solution)/shard_map/while/body/eval_jaxpr/ppermute | solution.py:16
  423.4 9.9 %collective-permute-done = f32[4,128,128]{2,1,0:T(8,128)S(1)} collective-permute-done((f32[4,128,128]{2,1,0:T(8,128)}, f32[4,128,128]{2,1,0:T(8,128)S(1)}, u32[]{:S(2)}, u32[]{:S(2)}) %collective-permute-start) | collective-permute-done | bytes 262176 | tf_op jit(solution)/shard_map/while/body/eval_jaxpr/ppermute | solution.py:16
  436.9 9.9 %collective-permute-done = f32[4,128,128]{2,1,0:T(8,128)S(1)} collective-permute-done((f32[4,128,128]{2,1,0:T(8,128)}, f32[4,128,128]{2,1,0:T(8,128)S(1)}, u32[]{:S(2)}, u32[]{:S(2)}) %collective-permute-start) | collective-permute-done | bytes 262176 | tf_op jit(solution)/shard_map/while/body/eval_jaxpr/ppermute | solution.py:16
  450.3 9.9 %collective-permute-done = f32[4,128,128]{2,1,0:T(8,128)S(1)} collective-permute-done((f32[4,128,128]{2,1,0:T(8,128)}, f32[4,128,128]{2,1,0:T(8,128)S(1)}, u32[]{:S(2)}, u32[]{:S(2)}) %collective-permute-start) | collective-permute-done | bytes 262176 | tf_op jit(solution)/shard_map/while/body/eval_jaxpr/ppermute | solution.py:16
  463.8 9.9 %collective-permute-done = f32[4,128,128]{2,1,0:T(8,128)S(1)} collective-permute-done((f32[4,128,128]{2,1,0:T(8,128)}, f32[4,128,128]{2,1,0:T(8,128)S(1)}, u32[]{:S(2)}, u32[]{:S(2)}) %collective-permute-start) | collective-permute-done | bytes 262176 | tf_op jit(solution)/shard_map/while/body/eval_jaxpr/ppermute | solution.py:16
  477.3 9.9 %collective-permute-done = f32[4,128,128]{2,1,0:T(8,128)S(1)} collective-permute-done((f32[4,128,128]{2,1,0:T(8,128)}, f32[4,128,128]{2,1,0:T(8,128)S(1)}, u32[]{:S(2)}, u32[]{:S(2)}) %collective-permute-start) | collective-permute-done | bytes 262176 | tf_op jit(solution)/shard_map/while/body/eval_jaxpr/ppermute | solution.py:16
  487.1 2.6 fusion.4
  489.8 4.1 multiply_reduce_fusion
  493.9 2.2 multiply_convert_fusion
  496.1 2.0 copy.8
  (73 shorter events, 99.3 us)
Async XLA Ops:
  6.5 34.4 %copy-start = (bf16[3072,512]{1,0:T(8,128)(2,1)S(1)}, bf16[3072,512]{1,0:T(8,128)(2,1)}, u32[]{:S(2)}) copy-start(bf16[3072,512]{1,0:T(8,128)(2,1)} %param.10) | copy-start | bytes 9437188
  6.5 34.4 %all-gather.2.cloned.1.call-start = ((), (), s32[]{:S(2)}) async-start(), calls=%async_computation | async-start | bytes 3538944 | tf_op jit(solution)/shard_map/all_gather | solution.py:22
  41.0 3.9 copy-start.3
  41.0 3.9 copy-start.5
  44.9 1.9 copy-start.4
  48.7 1.1 copy-start.1
  52.6 13.9 %collective-permute-start = (f32[4,128,128]{2,1,0:T(8,128)}, f32[4,128,128]{2,1,0:T(8,128)S(1)}, u32[]{:S(2)}, u32[]{:S(2)}) collective-permute-start(f32[4,128,128]{2,1,0:T(8,128)} %add.39), channel_id=1, source_target_pairs={{0,8},{8,16},{16,24},{24,32},{32,40},{40,48},{48,56},{56,64},{64,7... | collective-permute-start | bytes 786440 | tf_op jit(solution)/shard_map/while/body/eval_jaxpr/ppermute | solution.py:16
  68.1 13.0 %collective-permute-start = (f32[4,128,128]{2,1,0:T(8,128)}, f32[4,128,128]{2,1,0:T(8,128)S(1)}, u32[]{:S(2)}, u32[]{:S(2)}) collective-permute-start(f32[4,128,128]{2,1,0:T(8,128)} %add.39), channel_id=1, source_target_pairs={{0,8},{8,16},{16,24},{24,32},{32,40},{40,48},{48,56},{56,64},{64,7... | collective-permute-start | bytes 786440 | tf_op jit(solution)/shard_map/while/body/eval_jaxpr/ppermute | solution.py:16
  82.8 12.1 %collective-permute-start = (f32[4,128,128]{2,1,0:T(8,128)}, f32[4,128,128]{2,1,0:T(8,128)S(1)}, u32[]{:S(2)}, u32[]{:S(2)}) collective-permute-start(f32[4,128,128]{2,1,0:T(8,128)} %add.39), channel_id=1, source_target_pairs={{0,8},{8,16},{16,24},{24,32},{32,40},{40,48},{48,56},{56,64},{64,7... | collective-permute-start | bytes 786440 | tf_op jit(solution)/shard_map/while/body/eval_jaxpr/ppermute | solution.py:16
  96.6 11.8 %collective-permute-start = (f32[4,128,128]{2,1,0:T(8,128)}, f32[4,128,128]{2,1,0:T(8,128)S(1)}, u32[]{:S(2)}, u32[]{:S(2)}) collective-permute-start(f32[4,128,128]{2,1,0:T(8,128)} %add.39), channel_id=1, source_target_pairs={{0,8},{8,16},{16,24},{24,32},{32,40},{40,48},{48,56},{56,64},{64,7... | collective-permute-start | bytes 786440 | tf_op jit(solution)/shard_map/while/body/eval_jaxpr/ppermute | solution.py:16
  110.1 11.8 %collective-permute-start = (f32[4,128,128]{2,1,0:T(8,128)}, f32[4,128,128]{2,1,0:T(8,128)S(1)}, u32[]{:S(2)}, u32[]{:S(2)}) collective-permute-start(f32[4,128,128]{2,1,0:T(8,128)} %add.39), channel_id=1, source_target_pairs={{0,8},{8,16},{16,24},{24,32},{32,40},{40,48},{48,56},{56,64},{64,7... | collective-permute-start | bytes 786440 | tf_op jit(solution)/shard_map/while/body/eval_jaxpr/ppermute | solution.py:16
  123.5 11.8 %collective-permute-start = (f32[4,128,128]{2,1,0:T(8,128)}, f32[4,128,128]{2,1,0:T(8,128)S(1)}, u32[]{:S(2)}, u32[]{:S(2)}) collective-permute-start(f32[4,128,128]{2,1,0:T(8,128)} %add.39), channel_id=1, source_target_pairs={{0,8},{8,16},{16,24},{24,32},{32,40},{40,48},{48,56},{56,64},{64,7... | collective-permute-start | bytes 786440 | tf_op jit(solution)/shard_map/while/body/eval_jaxpr/ppermute | solution.py:16
  137.0 11.8 %collective-permute-start = (f32[4,128,128]{2,1,0:T(8,128)}, f32[4,128,128]{2,1,0:T(8,128)S(1)}, u32[]{:S(2)}, u32[]{:S(2)}) collective-permute-start(f32[4,128,128]{2,1,0:T(8,128)} %add.39), channel_id=1, source_target_pairs={{0,8},{8,16},{16,24},{24,32},{32,40},{40,48},{48,56},{56,64},{64,7... | collective-permute-start | bytes 786440 | tf_op jit(solution)/shard_map/while/body/eval_jaxpr/ppermute | solution.py:16
  150.4 11.8 %collective-permute-start = (f32[4,128,128]{2,1,0:T(8,128)}, f32[4,128,128]{2,1,0:T(8,128)S(1)}, u32[]{:S(2)}, u32[]{:S(2)}) collective-permute-start(f32[4,128,128]{2,1,0:T(8,128)} %add.39), channel_id=1, source_target_pairs={{0,8},{8,16},{16,24},{24,32},{32,40},{40,48},{48,56},{56,64},{64,7... | collective-permute-start | bytes 786440 | tf_op jit(solution)/shard_map/while/body/eval_jaxpr/ppermute | solution.py:16
  163.9 11.8 %collective-permute-start = (f32[4,128,128]{2,1,0:T(8,128)}, f32[4,128,128]{2,1,0:T(8,128)S(1)}, u32[]{:S(2)}, u32[]{:S(2)}) collective-permute-start(f32[4,128,128]{2,1,0:T(8,128)} %add.39), channel_id=1, source_target_pairs={{0,8},{8,16},{16,24},{24,32},{32,40},{40,48},{48,56},{56,64},{64,7... | collective-permute-start | bytes 786440 | tf_op jit(solution)/shard_map/while/body/eval_jaxpr/ppermute | solution.py:16
  177.3 12.5 %collective-permute-start = (f32[4,128,128]{2,1,0:T(8,128)}, f32[4,128,128]{2,1,0:T(8,128)S(1)}, u32[]{:S(2)}, u32[]{:S(2)}) collective-permute-start(f32[4,128,128]{2,1,0:T(8,128)} %add.39), channel_id=1, source_target_pairs={{0,8},{8,16},{16,24},{24,32},{32,40},{40,48},{48,56},{56,64},{64,7... | collective-permute-start | bytes 786440 | tf_op jit(solution)/shard_map/while/body/eval_jaxpr/ppermute | solution.py:16
  191.5 13.6 %collective-permute-start = (f32[4,128,128]{2,1,0:T(8,128)}, f32[4,128,128]{2,1,0:T(8,128)S(1)}, u32[]{:S(2)}, u32[]{:S(2)}) collective-permute-start(f32[4,128,128]{2,1,0:T(8,128)} %add.39), channel_id=1, source_target_pairs={{0,8},{8,16},{16,24},{24,32},{32,40},{40,48},{48,56},{56,64},{64,7... | collective-permute-start | bytes 786440 | tf_op jit(solution)/shard_map/while/body/eval_jaxpr/ppermute | solution.py:16
  206.8 14.4 %collective-permute-start = (f32[4,128,128]{2,1,0:T(8,128)}, f32[4,128,128]{2,1,0:T(8,128)S(1)}, u32[]{:S(2)}, u32[]{:S(2)}) collective-permute-start(f32[4,128,128]{2,1,0:T(8,128)} %add.39), channel_id=1, source_target_pairs={{0,8},{8,16},{16,24},{24,32},{32,40},{40,48},{48,56},{56,64},{64,7... | collective-permute-start | bytes 786440 | tf_op jit(solution)/shard_map/while/body/eval_jaxpr/ppermute | solution.py:16
  222.9 13.6 %collective-permute-start = (f32[4,128,128]{2,1,0:T(8,128)}, f32[4,128,128]{2,1,0:T(8,128)S(1)}, u32[]{:S(2)}, u32[]{:S(2)}) collective-permute-start(f32[4,128,128]{2,1,0:T(8,128)} %add.39), channel_id=1, source_target_pairs={{0,8},{8,16},{16,24},{24,32},{32,40},{40,48},{48,56},{56,64},{64,7... | collective-permute-start | bytes 786440 | tf_op jit(solution)/shard_map/while/body/eval_jaxpr/ppermute | solution.py:16
  238.1 12.7 %collective-permute-start = (f32[4,128,128]{2,1,0:T(8,128)}, f32[4,128,128]{2,1,0:T(8,128)S(1)}, u32[]{:S(2)}, u32[]{:S(2)}) collective-permute-start(f32[4,128,128]{2,1,0:T(8,128)} %add.39), channel_id=1, source_target_pairs={{0,8},{8,16},{16,24},{24,32},{32,40},{40,48},{48,56},{56,64},{64,7... | collective-permute-start | bytes 786440 | tf_op jit(solution)/shard_map/while/body/eval_jaxpr/ppermute | solution.py:16
  252.5 11.8 %collective-permute-start = (f32[4,128,128]{2,1,0:T(8,128)}, f32[4,128,128]{2,1,0:T(8,128)S(1)}, u32[]{:S(2)}, u32[]{:S(2)}) collective-permute-start(f32[4,128,128]{2,1,0:T(8,128)} %add.39), channel_id=1, source_target_pairs={{0,8},{8,16},{16,24},{24,32},{32,40},{40,48},{48,56},{56,64},{64,7... | collective-permute-start | bytes 786440 | tf_op jit(solution)/shard_map/while/body/eval_jaxpr/ppermute | solution.py:16
  266.0 11.8 %collective-permute-start = (f32[4,128,128]{2,1,0:T(8,128)}, f32[4,128,128]{2,1,0:T(8,128)S(1)}, u32[]{:S(2)}, u32[]{:S(2)}) collective-permute-start(f32[4,128,128]{2,1,0:T(8,128)} %add.39), channel_id=1, source_target_pairs={{0,8},{8,16},{16,24},{24,32},{32,40},{40,48},{48,56},{56,64},{64,7... | collective-permute-start | bytes 786440 | tf_op jit(solution)/shard_map/while/body/eval_jaxpr/ppermute | solution.py:16
  279.4 11.8 %collective-permute-start = (f32[4,128,128]{2,1,0:T(8,128)}, f32[4,128,128]{2,1,0:T(8,128)S(1)}, u32[]{:S(2)}, u32[]{:S(2)}) collective-permute-start(f32[4,128,128]{2,1,0:T(8,128)} %add.39), channel_id=1, source_target_pairs={{0,8},{8,16},{16,24},{24,32},{32,40},{40,48},{48,56},{56,64},{64,7... | collective-permute-start | bytes 786440 | tf_op jit(solution)/shard_map/while/body/eval_jaxpr/ppermute | solution.py:16
  292.9 11.8 %collective-permute-start = (f32[4,128,128]{2,1,0:T(8,128)}, f32[4,128,128]{2,1,0:T(8,128)S(1)}, u32[]{:S(2)}, u32[]{:S(2)}) collective-permute-start(f32[4,128,128]{2,1,0:T(8,128)} %add.39), channel_id=1, source_target_pairs={{0,8},{8,16},{16,24},{24,32},{32,40},{40,48},{48,56},{56,64},{64,7... | collective-permute-start | bytes 786440 | tf_op jit(solution)/shard_map/while/body/eval_jaxpr/ppermute | solution.py:16
  306.3 11.8 %collective-permute-start = (f32[4,128,128]{2,1,0:T(8,128)}, f32[4,128,128]{2,1,0:T(8,128)S(1)}, u32[]{:S(2)}, u32[]{:S(2)}) collective-permute-start(f32[4,128,128]{2,1,0:T(8,128)} %add.39), channel_id=1, source_target_pairs={{0,8},{8,16},{16,24},{24,32},{32,40},{40,48},{48,56},{56,64},{64,7... | collective-permute-start | bytes 786440 | tf_op jit(solution)/shard_map/while/body/eval_jaxpr/ppermute | solution.py:16
  319.8 11.8 %collective-permute-start = (f32[4,128,128]{2,1,0:T(8,128)}, f32[4,128,128]{2,1,0:T(8,128)S(1)}, u32[]{:S(2)}, u32[]{:S(2)}) collective-permute-start(f32[4,128,128]{2,1,0:T(8,128)} %add.39), channel_id=1, source_target_pairs={{0,8},{8,16},{16,24},{24,32},{32,40},{40,48},{48,56},{56,64},{64,7... | collective-permute-start | bytes 786440 | tf_op jit(solution)/shard_map/while/body/eval_jaxpr/ppermute | solution.py:16
  333.2 11.8 %collective-permute-start = (f32[4,128,128]{2,1,0:T(8,128)}, f32[4,128,128]{2,1,0:T(8,128)S(1)}, u32[]{:S(2)}, u32[]{:S(2)}) collective-permute-start(f32[4,128,128]{2,1,0:T(8,128)} %add.39), channel_id=1, source_target_pairs={{0,8},{8,16},{16,24},{24,32},{32,40},{40,48},{48,56},{56,64},{64,7... | collective-permute-start | bytes 786440 | tf_op jit(solution)/shard_map/while/body/eval_jaxpr/ppermute | solution.py:16
  346.7 12.8 %collective-permute-start = (f32[4,128,128]{2,1,0:T(8,128)}, f32[4,128,128]{2,1,0:T(8,128)S(1)}, u32[]{:S(2)}, u32[]{:S(2)}) collective-permute-start(f32[4,128,128]{2,1,0:T(8,128)} %add.39), channel_id=1, source_target_pairs={{0,8},{8,16},{16,24},{24,32},{32,40},{40,48},{48,56},{56,64},{64,7... | collective-permute-start | bytes 786440 | tf_op jit(solution)/shard_map/while/body/eval_jaxpr/ppermute | solution.py:16
  361.2 13.9 %collective-permute-start = (f32[4,128,128]{2,1,0:T(8,128)}, f32[4,128,128]{2,1,0:T(8,128)S(1)}, u32[]{:S(2)}, u32[]{:S(2)}) collective-permute-start(f32[4,128,128]{2,1,0:T(8,128)} %add.39), channel_id=1, source_target_pairs={{0,8},{8,16},{16,24},{24,32},{32,40},{40,48},{48,56},{56,64},{64,7... | collective-permute-start | bytes 786440 | tf_op jit(solution)/shard_map/while/body/eval_jaxpr/ppermute | solution.py:16
  376.8 14.1 %collective-permute-start = (f32[4,128,128]{2,1,0:T(8,128)}, f32[4,128,128]{2,1,0:T(8,128)S(1)}, u32[]{:S(2)}, u32[]{:S(2)}) collective-permute-start(f32[4,128,128]{2,1,0:T(8,128)} %add.39), channel_id=1, source_target_pairs={{0,8},{8,16},{16,24},{24,32},{32,40},{40,48},{48,56},{56,64},{64,7... | collective-permute-start | bytes 786440 | tf_op jit(solution)/shard_map/while/body/eval_jaxpr/ppermute | solution.py:16
  392.5 13.2 %collective-permute-start = (f32[4,128,128]{2,1,0:T(8,128)}, f32[4,128,128]{2,1,0:T(8,128)S(1)}, u32[]{:S(2)}, u32[]{:S(2)}) collective-permute-start(f32[4,128,128]{2,1,0:T(8,128)} %add.39), channel_id=1, source_target_pairs={{0,8},{8,16},{16,24},{24,32},{32,40},{40,48},{48,56},{56,64},{64,7... | collective-permute-start | bytes 786440 | tf_op jit(solution)/shard_map/while/body/eval_jaxpr/ppermute | solution.py:16
  407.5 12.4 %collective-permute-start = (f32[4,128,128]{2,1,0:T(8,128)}, f32[4,128,128]{2,1,0:T(8,128)S(1)}, u32[]{:S(2)}, u32[]{:S(2)}) collective-permute-start(f32[4,128,128]{2,1,0:T(8,128)} %add.39), channel_id=1, source_target_pairs={{0,8},{8,16},{16,24},{24,32},{32,40},{40,48},{48,56},{56,64},{64,7... | collective-permute-start | bytes 786440 | tf_op jit(solution)/shard_map/while/body/eval_jaxpr/ppermute | solution.py:16
  421.5 11.8 %collective-permute-start = (f32[4,128,128]{2,1,0:T(8,128)}, f32[4,128,128]{2,1,0:T(8,128)S(1)}, u32[]{:S(2)}, u32[]{:S(2)}) collective-permute-start(f32[4,128,128]{2,1,0:T(8,128)} %add.39), channel_id=1, source_target_pairs={{0,8},{8,16},{16,24},{24,32},{32,40},{40,48},{48,56},{56,64},{64,7... | collective-permute-start | bytes 786440 | tf_op jit(solution)/shard_map/while/body/eval_jaxpr/ppermute | solution.py:16
  435.0 11.8 %collective-permute-start = (f32[4,128,128]{2,1,0:T(8,128)}, f32[4,128,128]{2,1,0:T(8,128)S(1)}, u32[]{:S(2)}, u32[]{:S(2)}) collective-permute-start(f32[4,128,128]{2,1,0:T(8,128)} %add.39), channel_id=1, source_target_pairs={{0,8},{8,16},{16,24},{24,32},{32,40},{40,48},{48,56},{56,64},{64,7... | collective-permute-start | bytes 786440 | tf_op jit(solution)/shard_map/while/body/eval_jaxpr/ppermute | solution.py:16
  448.4 11.8 %collective-permute-start = (f32[4,128,128]{2,1,0:T(8,128)}, f32[4,128,128]{2,1,0:T(8,128)S(1)}, u32[]{:S(2)}, u32[]{:S(2)}) collective-permute-start(f32[4,128,128]{2,1,0:T(8,128)} %add.39), channel_id=1, source_target_pairs={{0,8},{8,16},{16,24},{24,32},{32,40},{40,48},{48,56},{56,64},{64,7... | collective-permute-start | bytes 786440 | tf_op jit(solution)/shard_map/while/body/eval_jaxpr/ppermute | solution.py:16
  461.9 11.8 %collective-permute-start = (f32[4,128,128]{2,1,0:T(8,128)}, f32[4,128,128]{2,1,0:T(8,128)S(1)}, u32[]{:S(2)}, u32[]{:S(2)}) collective-permute-start(f32[4,128,128]{2,1,0:T(8,128)} %add.39), channel_id=1, source_target_pairs={{0,8},{8,16},{16,24},{24,32},{32,40},{40,48},{48,56},{56,64},{64,7... | collective-permute-start | bytes 786440 | tf_op jit(solution)/shard_map/while/body/eval_jaxpr/ppermute | solution.py:16
  475.3 11.8 %collective-permute-start = (f32[4,128,128]{2,1,0:T(8,128)}, f32[4,128,128]{2,1,0:T(8,128)S(1)}, u32[]{:S(2)}, u32[]{:S(2)}) collective-permute-start(f32[4,128,128]{2,1,0:T(8,128)} %add.39), channel_id=1, source_target_pairs={{0,8},{8,16},{16,24},{24,32},{32,40},{40,48},{48,56},{56,64},{64,7... | collective-permute-start | bytes 786440 | tf_op jit(solution)/shard_map/while/body/eval_jaxpr/ppermute | solution.py:16
  489.8 4.2 copy-start.2
Sparse Core Ops, SparseCore 0:
  9.2 31.7 all-gather.1
where the time goes:
time: 507 us; the launch traced here: 505 us
  waiting for transfers between devices  357 us (70%)
  starting transfers between devices  60.6 us (12%)
  other arithmetic  54.9 us (11%)
  matrix products  15.3 us (3%)
  between operations  13.5 us (3%)
    ppermute x31, waiting for transfers between devices, from_behind(): return lax.ppermute(value, axis, pairs)  323 us
    ppermute x31, starting transfers between devices, from_behind(): return lax.ppermute(value, axis, pairs)  60.6 us
    add x31, other arithmetic, advance(): return from_behind(carried + local_state, 'ctx', 1)  51.8 us
    all_gather x1, waiting for transfers between devices, body(): piece_rows = lax.all_gather(tokens, 'tp', axis=0, tiled=True)  32.9 us
  transfers between devices with their start and end apart: 32, of which 32 were waited for; matrix products, arithmetic and copies ran while one was open for 0% of the time, Pallas kernels for 0%

commit v1 on v0

--- a/solution.py
+++ b/solution.py
@@ -14,6 +14,20 @@
     size = lax.axis_size(axis)
     pairs = [(i, i + by) for i in range(size) if 0 <= i + by < size]
     return lax.ppermute(value, axis, pairs)
+
+
+def exclusive_scan(value, axis):
+    size = lax.axis_size(axis)
+    covered = value
+    before = None
+    by = 1
+    while by < size:
+        piece = from_behind(covered, axis, by)
+        before = piece if before is None else before + piece
+        by *= 2
+        if by < size:
+            covered = covered + piece
+    return before
 
 
 def body(tokens, w_query, w_key, w_value, norm_gain):
@@ -38,12 +52,7 @@
         "bshd,bshe->bhde", key_rows, value_rows, preferred_element_type=jnp.float32
     )
     local_state = jnp.sum(block_states, axis=0)
-    empty_state = jnp.zeros_like(local_state)
-
-    def advance(step_index, carried):
-        return from_behind(carried + local_state, "ctx", 1)
-
-    prefix_state = lax.fori_loop(0, lax.axis_size("ctx") - 1, advance, empty_state)
+    prefix_state = exclusive_scan(local_state, "ctx")
     running = jnp.cumsum(block_states, axis=0)
     earlier = jnp.concatenate([jnp.zeros_like(block_states), running[:-1]], axis=0)
     block_start = prefix_state[None] + earlier

time: 507 us -> 132 us (0.26)
  the two profiles are of different devices: /device:TPU:128 before, /device:TPU:192 now
where the time goes in v1:
time: 132 us
  waiting for transfers between devices  87.1 us (66%)
  matrix products  14 us (11%)
  between operations  13.5 us (10%)
  starting transfers between devices  11.3 us (9%)
  local copies, waits for them, and re-layouts  3.27 us (2%)
  other arithmetic  2.72 us (2%)
    ppermute x5, waiting for transfers between devices, from_behind(): return lax.ppermute(value, axis, pairs)  53.4 us
    all_gather x1, waiting for transfers between devices, body(): piece_rows = lax.all_gather(tokens, 'tp', axis=0, tiled=True)  33 us
    ppermute x5, starting transfers between devices, from_behind(): return lax.ppermute(value, axis, pairs)  11.3 us
    dot_general x1, matrix products, body(): jnp.dot(piece_rows, w_value, preferred_element_type=jnp.float32)  3.87 us
    dot_general x1, matrix products, body(): jnp.einsum('bhqk,bkhe->bqhe', scores, value_rows, preferred_element_type=...  3.8 us
  transfers between devices with their start and end apart: 6, of which 6 were waited for; matrix products, arithmetic and copies ran while one was open for 3% of the time, Pallas kernels for 0%

profile of v1, /device:TPU:192, one launch (start us, length us, event | category | flops | bytes accessed | tf_op | source)
XLA Modules:
  0.0 132.0 jit_solution(15375087548146200491)
XLA Ops:
  6.5 0.0 copy-start
  6.5 0.0 all-gather.2.cloned.1.call-start
  6.5 0.7 all-gather.2.cloned.1.call-update
  7.3 33.0 %all-gather.2.cloned.1.call-done = bf16[512,3072]{1,0:T(8,128)(2,1)} async-done(((bf16[64,3072]{1,0:T(8,128)(2,1)}), bf16[512,3072]{1,0:T(8,128)(2,1)}) %all-gather.2.cloned.1.call-update) | async-done | bytes 3145744 | tf_op jit(solution)/shard_map/all_gather | solution.py:36
  40.3 0.0 copy-done
  40.3 0.0 copy-start.6
  40.3 0.0 copy-start.8
  40.3 3.9 %convolution_convert_fusion = bf16[512,512]{0,1:T(8,128)(2,1)S(1)} fusion(bf16[512,3072]{1,0:T(8,128)(2,1)} %all-gather.2.cloned.1.call-done, bf16[3072,512]{1,0:T(8,128)(2,1)S(1)} %copy-done), kind=kOutput, calls=%fused_computation.5 | convolution fusion | flops 1610874880 | bytes 6815744 | tf_op jit(solution)/shard_map/dot_general | solution.py:41
  44.1 0.0 copy-done.6
  44.1 0.0 copy-done.8
  44.2 0.0 copy-start.7
  44.2 1.8 %convolution_convert_fusion.1 = bf16[512,512]{0,1:T(8,128)(2,1)S(1)} fusion(bf16[512,3072]{1,0:T(8,128)(2,1)S(1)} %copy-done.8, bf16[3072,512]{1,0:T(8,128)(2,1)S(1)} %copy-done.6), kind=kOutput, calls=%fused_computation.6 | convolution fusion | flops 1610874880 | bytes 6815744 | tf_op jit(solution)/shard_map/dot_general | solution.py:40
  46.0 0.0 copy-done.7
  46.1 1.8 %convolution_convert_fusion.2 = bf16[512,512]{0,1:T(8,128)(2,1)S(1)} fusion(bf16[512,3072]{1,0:T(8,128)(2,1)S(1)} %copy-done.8, bf16[3072,512]{1,0:T(8,128)(2,1)S(1)} %copy-done.7), kind=kOutput, calls=%fused_computation.7 | convolution fusion | flops 1610874880 | bytes 6815744 | tf_op jit(solution)/shard_map/dot_general | solution.py:37
  47.9 0.1 pad_maximum_fusion
  48.0 0.0 copy-start.1
  48.0 1.2 copy-done.1
  49.2 0.3 fusion.2
  49.5 3.4 %collective-permute-start = (f32[4,128,128]{2,1,0:T(8,128)S(1)}, f32[4,128,128]{2,1,0:T(8,128)S(1)}, u32[]{:S(2)}, u32[]{:S(2)}) collective-permute-start(f32[4,128,128]{2,1,0:T(8,128)S(1)} %fusion.2), channel_id=1, source_target_pairs={{0,8},{8,16},{16,24},{24,32},{32,40},{40,48},{48,56},{56,64},{64,7... | collective-permute-start | bytes 786440 | tf_op jit(solution)/shard_map/ppermute | solution.py:16
  52.8 9.1 %collective-permute-done = f32[4,128,128]{2,1,0:T(8,128)S(1)} collective-permute-done((f32[4,128,128]{2,1,0:T(8,128)S(1)}, f32[4,128,128]{2,1,0:T(8,128)S(1)}, u32[]{:S(2)}, u32[]{:S(2)}) %collective-permute-start) | collective-permute-done | bytes 262176 | tf_op jit(solution)/shard_map/ppermute | solution.py:16
  61.9 2.8 %collective-permute-start.1 = (f32[4,128,128]{2,1,0:T(8,128)S(1)}, f32[4,128,128]{2,1,0:T(8,128)S(1)}, u32[]{:S(2)}, u32[]{:S(2)}) collective-permute-start(f32[4,128,128]{2,1,0:T(8,128)S(1)} %add.44), channel_id=1, source_target_pairs={{0,16},{8,24},{16,32},{24,40},{32,48},{40,56},{48,64},{56,72},{64,... | collective-permute-start | bytes 786440 | tf_op jit(solution)/shard_map/ppermute | solution.py:16
  64.7 9.1 %collective-permute-done.1 = f32[4,128,128]{2,1,0:T(8,128)S(1)} collective-permute-done((f32[4,128,128]{2,1,0:T(8,128)S(1)}, f32[4,128,128]{2,1,0:T(8,128)S(1)}, u32[]{:S(2)}, u32[]{:S(2)}) %collective-permute-start.1) | collective-permute-done | bytes 262176 | tf_op jit(solution)/shard_map/ppermute | solution.py:16
  73.8 0.0 copy-start.2
  73.9 2.6 %collective-permute-start.2 = (f32[4,128,128]{2,1,0:T(8,128)S(1)}, f32[4,128,128]{2,1,0:T(8,128)S(1)}, u32[]{:S(2)}, u32[]{:S(2)}) collective-permute-start(f32[4,128,128]{2,1,0:T(8,128)S(1)} %add.46), channel_id=1, source_target_pairs={{0,32},{8,40},{16,48},{24,56},{32,64},{40,72},{48,80},{56,88},{64,... | collective-permute-start | bytes 786440 | tf_op jit(solution)/shard_map/ppermute | solution.py:16
  76.4 6.1 %collective-permute-done.2 = f32[4,128,128]{2,1,0:T(8,128)S(1)} collective-permute-done((f32[4,128,128]{2,1,0:T(8,128)S(1)}, f32[4,128,128]{2,1,0:T(8,128)S(1)}, u32[]{:S(2)}, u32[]{:S(2)}) %collective-permute-start.2) | collective-permute-done | bytes 262176 | tf_op jit(solution)/shard_map/ppermute | solution.py:16
  82.5 0.0 copy-start.3
  82.5 1.3 collective-permute-start.3
  83.8 0.8 iota_compare_fusion
  84.6 15.5 %collective-permute-done.3 = f32[4,128,128]{2,1,0:T(8,128)S(1)} collective-permute-done((f32[4,128,128]{2,1,0:T(8,128)S(1)}, f32[4,128,128]{2,1,0:T(8,128)S(1)}, u32[]{:S(2)}, u32[]{:S(2)}) %collective-permute-start.3) | collective-permute-done | bytes 262176 | tf_op jit(solution)/shard_map/ppermute | solution.py:16
  100.1 0.0 copy-start.4
  100.1 0.8 add.50
  100.9 0.0 copy-done.2
  100.9 0.0 copy-done.3
  100.9 0.0 copy-done.4
  100.9 1.3 collective-permute-start.4
  102.2 3.8 %fusion = f32[4,128,512]{2,1,0:T(8,128)} fusion(pred[512,512]{1,0:T(8,128)(4,1)} %iota_compare_fusion, bf16[1,512,3,4,128]{1,4,3,2,0:T(8,128)(2,1)} %bitcast.30), kind=kOutput, calls=%fused_computation.1 | convolution fusion | flops 538968064 | bytes 2883584 | tf_op jit(solution)/shard_map/bhqk,bkhe->bqhe/dot_general | solution.py:62
  106.0 0.0 copy-start.5
  106.0 13.7 %collective-permute-done.4 = f32[4,128,128]{2,1,0:T(8,128)} collective-permute-done((f32[4,128,128]{2,1,0:T(8,128)}, f32[4,128,128]{2,1,0:T(8,128)}, u32[]{:S(2)}, u32[]{:S(2)}) %collective-permute-start.4) | collective-permute-done | bytes 262176 | tf_op jit(solution)/shard_map/ppermute | solution.py:16
  119.7 2.4 %multiply_reduce_fusion = (f32[512,4]{0,1:T(4,128)S(1)}, f32[1,512,4,128]{1,3,2,0:T(8,128)S(1)}) fusion(f32[4,128,512]{2,1,0:T(8,128)} %fusion, bf16[1,512,3,4,128]{1,4,3,2,0:T(8,128)(2,1)} %bitcast.31, f32[4,128,128]{2,1,0:T(8,128)} %collective-permute-done.4, f32[4,128,128]{2,1,0:T(8,128)} %copy-done.4, f32[4,128,128]{2,1,0:T(8,128)} %copy-done.3, ...), kind=kOutput, calls=%fused_computation.9 | convolution fusion | flops 403699712 | bytes 3940352 | tf_op jit(solution)/shard_map/bqhd,bhde->bqhe/dot_general | solution.py:63
  122.1 0.0 copy-done.5
  122.1 0.9 multiply_convert_fusion
  123.1 2.0 %copy.9 = bf16[512,512]{1,0:T(8,128)(2,1)} copy(bf16[512,512]{0,1:T(8,128)(2,1)} %bitcast.32) | data formatting | bytes 1048576 | tf_op jit(solution)/shard_map/convert_element_type | solution.py:72
  (4 shorter events, 0.1 us)
Async XLA Ops:
  6.5 33.7 %copy-start = (bf16[3072,512]{1,0:T(8,128)(2,1)S(1)}, bf16[3072,512]{1,0:T(8,128)(2,1)}, u32[]{:S(2)}) copy-start(bf16[3072,512]{1,0:T(8,128)(2,1)} %param.8) | copy-start | bytes 9437188
  6.5 33.7 %all-gather.2.cloned.1.call-start = ((), (), s32[]{:S(2)}) async-start(), calls=%async_computation | async-start | bytes 3538944 | tf_op jit(solution)/shard_map/all_gather | solution.py:36
  40.3 3.9 %copy-start.6 = (bf16[3072,512]{1,0:T(8,128)(2,1)S(1)}, bf16[3072,512]{1,0:T(8,128)(2,1)}, u32[]{:S(2)}) copy-start(bf16[3072,512]{1,0:T(8,128)(2,1)} %param.7) | copy-start | bytes 9437188
  40.3 3.9 %copy-start.8 = (bf16[512,3072]{1,0:T(8,128)(2,1)S(1)}, bf16[512,3072]{1,0:T(8,128)(2,1)}, u32[]{:S(2)}) copy-start(bf16[512,3072]{1,0:T(8,128)(2,1)} %all-gather.2.cloned.1.call-done) | copy-start | bytes 9437188
  44.2 1.9 %copy-start.7 = (bf16[3072,512]{1,0:T(8,128)(2,1)S(1)}, bf16[3072,512]{1,0:T(8,128)(2,1)}, u32[]{:S(2)}) copy-start(bf16[3072,512]{1,0:T(8,128)(2,1)} %param.6) | copy-start | bytes 9437188
  48.0 1.2 copy-start.1
  49.5 12.5 %collective-permute-start = (f32[4,128,128]{2,1,0:T(8,128)S(1)}, f32[4,128,128]{2,1,0:T(8,128)S(1)}, u32[]{:S(2)}, u32[]{:S(2)}) collective-permute-start(f32[4,128,128]{2,1,0:T(8,128)S(1)} %fusion.2), channel_id=1, source_target_pairs={{0,8},{8,16},{16,24},{24,32},{32,40},{40,48},{48,56},{56,64},{64,7... | collective-permute-start | bytes 786440 | tf_op jit(solution)/shard_map/ppermute | solution.py:16
  61.9 11.9 %collective-permute-start.1 = (f32[4,128,128]{2,1,0:T(8,128)S(1)}, f32[4,128,128]{2,1,0:T(8,128)S(1)}, u32[]{:S(2)}, u32[]{:S(2)}) collective-permute-start(f32[4,128,128]{2,1,0:T(8,128)S(1)} %add.44), channel_id=1, source_target_pairs={{0,16},{8,24},{16,32},{24,40},{32,48},{40,56},{48,64},{56,72},{64,... | collective-permute-start | bytes 786440 | tf_op jit(solution)/shard_map/ppermute | solution.py:16
  73.8 27.1 %copy-start.2 = (f32[4,128,128]{2,1,0:T(8,128)}, f32[4,128,128]{2,1,0:T(8,128)S(1)}, u32[]{:S(2)}) copy-start(f32[4,128,128]{2,1,0:T(8,128)S(1)} %collective-permute-done.1) | copy-start | bytes 786436
  73.9 8.6 %collective-permute-start.2 = (f32[4,128,128]{2,1,0:T(8,128)S(1)}, f32[4,128,128]{2,1,0:T(8,128)S(1)}, u32[]{:S(2)}, u32[]{:S(2)}) collective-permute-start(f32[4,128,128]{2,1,0:T(8,128)S(1)} %add.46), channel_id=1, source_target_pairs={{0,32},{8,40},{16,48},{24,56},{32,64},{40,72},{48,80},{56,88},{64,... | collective-permute-start | bytes 786440 | tf_op jit(solution)/shard_map/ppermute | solution.py:16
  82.5 18.4 %copy-start.3 = (f32[4,128,128]{2,1,0:T(8,128)}, f32[4,128,128]{2,1,0:T(8,128)S(1)}, u32[]{:S(2)}) copy-start(f32[4,128,128]{2,1,0:T(8,128)S(1)} %collective-permute-done.2) | copy-start | bytes 786436
  82.5 17.6 %collective-permute-start.3 = (f32[4,128,128]{2,1,0:T(8,128)S(1)}, f32[4,128,128]{2,1,0:T(8,128)S(1)}, u32[]{:S(2)}, u32[]{:S(2)}) collective-permute-start(f32[4,128,128]{2,1,0:T(8,128)S(1)} %add.48), channel_id=1, source_target_pairs={{0,64},{8,72},{16,80},{24,88},{32,96},{40,104},{48,112},{56,120},{... | collective-permute-start | bytes 786440 | tf_op jit(solution)/shard_map/ppermute | solution.py:16
  100.1 0.8 copy-start.4
  100.9 18.8 %collective-permute-start.4 = (f32[4,128,128]{2,1,0:T(8,128)}, f32[4,128,128]{2,1,0:T(8,128)}, u32[]{:S(2)}, u32[]{:S(2)}) collective-permute-start(f32[4,128,128]{2,1,0:T(8,128)} %add.50), channel_id=1, source_target_pairs={{0,128},{8,136},{16,144},{24,152},{32,160},{40,168},{48,176},{56,1... | collective-permute-start | bytes 786440 | tf_op jit(solution)/shard_map/ppermute | solution.py:16
  106.0 16.1 %copy-start.5 = (f32[512]{0:T(512)S(1)}, f32[512]{0:T(512)}, u32[]{:S(2)}) copy-start(f32[512]{0:T(512)} %param.9) | copy-start | bytes 6148
Sparse Core Ops, SparseCore 0:
  9.2 31.0 all-gather.1

commit v2 on v0

--- a/solution.py
+++ b/solution.py
@@ -14,6 +14,16 @@
     size = lax.axis_size(axis)
     pairs = [(i, i + by) for i in range(size) if 0 <= i + by < size]
     return lax.ppermute(value, axis, pairs)
+
+
+def exclusive_scan(value, axis):
+    size = lax.axis_size(axis)
+    pieces = value.reshape(size, -1, value.shape[-1])
+    gathered = lax.all_to_all(pieces, axis, 0, 0, tiled=True)
+    running = jnp.cumsum(gathered, axis=0)
+    before = jnp.concatenate([jnp.zeros_like(running[:1]), running[:-1]], axis=0)
+    returned = lax.all_to_all(before, axis, 0, 0, tiled=True)
+    return returned.reshape(value.shape)
 
 
 def body(tokens, w_query, w_key, w_value, norm_gain):
@@ -38,12 +48,7 @@
         "bshd,bshe->bhde", key_rows, value_rows, preferred_element_type=jnp.float32
     )
     local_state = jnp.sum(block_states, axis=0)
-    empty_state = jnp.zeros_like(local_state)
-
-    def advance(step_index, carried):
-        return from_behind(carried + local_state, "ctx", 1)
-
-    prefix_state = lax.fori_loop(0, lax.axis_size("ctx") - 1, advance, empty_state)
+    prefix_state = exclusive_scan(local_state, "ctx")
     running = jnp.cumsum(block_states, axis=0)
     earlier = jnp.concatenate([jnp.zeros_like(block_states), running[:-1]], axis=0)
     block_start = prefix_state[None] + earlier

time: 507 us -> 111 us (0.22)
  the two profiles are of different devices: /device:TPU:128 before, /device:TPU:1 now
where the time goes in v2:
time: 111 us; the launch traced here: 109 us
  waiting for transfers between devices  46.9 us (42%)
  blocking collectives  21 us (19%)
  matrix products  14.6 us (13%)
  between operations  13.5 us (12%)
  other arithmetic  4.87 us (4%)
  starting transfers between devices  4.5 us (4%)
  local copies, waits for them, and re-layouts  3.99 us (4%)
    all_gather x1, waiting for transfers between devices, body(): piece_rows = lax.all_gather(tokens, 'tp', axis=0, tiled=True)  36.4 us
    all_to_all x1, blocking collectives, exclusive_scan(): gathered = lax.all_to_all(pieces, axis, 0, 0, tiled=True)  21 us
    all_to_all x1, waiting for transfers between devices, exclusive_scan(): returned = lax.all_to_all(before, axis, 0, 0, tiled=True)  9.83 us
    all_to_all x1, starting transfers between devices, exclusive_scan(): returned = lax.all_to_all(before, axis, 0, 0, tiled=True)  4.5 us
    dot_general x1, matrix products, body(): jnp.einsum('bhqk,bkhe->bqhe', scores, value_rows, preferred_element_type=...  4.17 us
    dot_general x1, matrix products, body(): jnp.dot(piece_rows, w_value, preferred_element_type=jnp.float32)  3.87 us
    dot_general x1, matrix products, body(): jnp.einsum('bqhd,bhde->bqhe', query_rows.astype(jnp.float32), block_start...  2.65 us
  transfers between devices with their start and end apart: 2, of which 2 were waited for; matrix products, arithmetic and copies ran while one was open for 1% of the time, Pallas kernels for 0%

profile of v2, /device:TPU:1, one launch (start us, length us, event | category | flops | bytes accessed | tf_op | source)
XLA Modules:
  0.0 109.5 jit_solution(15340499090149745444)
XLA Ops:
  6.5 0.0 copy-start
  6.5 0.0 all-gather.2.cloned.1.call-start
  6.5 0.7 all-gather.2.cloned.1.call-update
  7.3 36.4 %all-gather.2.cloned.1.call-done = bf16[512,3072]{1,0:T(8,128)(2,1)} async-done(((bf16[64,3072]{1,0:T(8,128)(2,1)}), bf16[512,3072]{1,0:T(8,128)(2,1)}) %all-gather.2.cloned.1.call-update) | async-done | bytes 3145744 | tf_op jit(solution)/shard_map/all_gather | solution.py:32
  43.7 0.0 copy-done
  43.7 0.0 copy-start.3
  43.7 0.0 copy-start.5
  43.7 3.9 %convolution_convert_fusion = bf16[512,512]{0,1:T(8,128)(2,1)S(1)} fusion(bf16[512,3072]{1,0:T(8,128)(2,1)} %all-gather.2.cloned.1.call-done, bf16[3072,512]{1,0:T(8,128)(2,1)S(1)} %copy-done), kind=kOutput, calls=%fused_computation.5 | convolution fusion | flops 1610874880 | bytes 6815744 | tf_op jit(solution)/shard_map/dot_general | solution.py:37
  47.5 0.0 copy-done.3
  47.5 0.0 copy-done.5
  47.6 0.0 copy-start.4
  47.6 1.8 %convolution_convert_fusion.1 = bf16[512,512]{0,1:T(8,128)(2,1)S(1)} fusion(bf16[512,3072]{1,0:T(8,128)(2,1)S(1)} %copy-done.5, bf16[3072,512]{1,0:T(8,128)(2,1)S(1)} %copy-done.3), kind=kOutput, calls=%fused_computation.6 | convolution fusion | flops 1610874880 | bytes 6815744 | tf_op jit(solution)/shard_map/dot_general | solution.py:36
  49.4 0.0 copy-done.4
  49.5 1.8 %convolution_convert_fusion.2 = bf16[512,512]{0,1:T(8,128)(2,1)S(1)} fusion(bf16[512,3072]{1,0:T(8,128)(2,1)S(1)} %copy-done.5, bf16[3072,512]{1,0:T(8,128)(2,1)S(1)} %copy-done.4), kind=kOutput, calls=%fused_computation.7 | convolution fusion | flops 1610874880 | bytes 6815744 | tf_op jit(solution)/shard_map/dot_general | solution.py:33
  51.3 0.1 pad_maximum_fusion
  51.4 0.0 copy-start.1
  51.4 1.1 %copy-done.1 = bf16[512,1536]{0,1:T(8,128)(2,1)} copy-done((bf16[512,1536]{0,1:T(8,128)(2,1)}, bf16[512,1536]{0,1:T(8,128)(2,1)S(1)}, u32[]{:S(2)}) %copy-start.1) | copy-done | bytes 1572888
  52.6 0.3 fusion.3
  52.8 21.0 %all_to_all.10 = f32[32,16,128]{2,1,0:T(8,128)S(1)} all-to-all(f32[32,16,128]{2,1,0:T(8,128)S(1)} %bitcast.42), channel_id=1, replica_groups=mesh['ctx'=32,'tp'=8] {'ctx'}, dimensions={0} | all-to-all | bytes 524288 | tf_op jit(solution)/shard_map/all_to_all | solution.py:22
  73.9 1.8 %fusion.6 = f32[32,16,128]{2,1,0:T(8,128)S(1)} fusion(f32[32,16,128]{2,1,0:T(8,128)S(1)} %all_to_all.10), kind=kOutput, calls=%fused_computation.18 | output fusion | flops 2031616 | bytes 524288 | tf_op jit(solution)/shard_map/jit(cumsum)/reduce_window_sum | solution.py:23
  75.7 0.7 concatenate.7
  76.4 4.5 %all-to-all-start.1 = ((f32[32,16,128]{2,1,0:T(8,128)}), f32[32,16,128]{2,1,0:T(8,128)S(1)}, u32[]{:S(2)}, u32[]{:S(2)}) async-start(f32[32,16,128]{2,1,0:T(8,128)} %concatenate.7), calls=%async_computation.1 | async-start | bytes 524288 | tf_op jit(solution)/shard_map/all_to_all | solution.py:25
  80.9 0.8 iota_compare_fusion
  81.7 9.8 %all-to-all-done.1 = f32[32,16,128]{2,1,0:T(8,128)S(1)} async-done(((f32[32,16,128]{2,1,0:T(8,128)}), f32[32,16,128]{2,1,0:T(8,128)S(1)}, u32[]{:S(2)}, u32[]{:S(2)}) %all-to-all-start.1) | async-done | bytes 262176 | tf_op jit(solution)/shard_map/all_to_all | solution.py:25
  91.5 2.6 %fusion.4 = f32[4,128,512]{2,1,0:T(8,128)} fusion(f32[4,128,128]{2,1,0:T(8,128)S(1)} %bitcast.41, bf16[1,512,3,4,128]{1,4,3,2,0:T(8,128)(2,1)} %bitcast.38), kind=kOutput, calls=%fused_computation.15 | convolution fusion | flops 402653184 | bytes 1835008 | tf_op jit(solution)/shard_map/bqhd,bhde->bqhe/dot_general | solution.py:59
  94.2 0.0 copy-start.2
  94.2 4.2 %multiply_reduce_fusion = (f32[512,4]{0,1:T(4,128)S(1)}, f32[1,512,4,128]{1,3,2,0:T(8,128)}) fusion(f32[4,128,512]{2,1,0:T(8,128)} %fusion.4, pred[512,512]{1,0:T(8,128)(4,1)} %iota_compare_fusion, bf16[1,512,3,4,128]{1,4,3,2,0:T(8,128)(2,1)} %bitcast.39), kind=kOutput, calls=%fused_computation.9 | convolution fusion | flops 539752448 | bytes 3940352 | tf_op jit(solution)/shard_map/bhqk,bkhe->bqhe/dot_general | solution.py:58
  98.4 0.0 copy-done.2
  98.4 2.2 %multiply_convert_fusion = bf16[1,512,4,128]{1,3,2,0:T(8,128)(2,1)} fusion(f32[1,512,4,128]{1,3,2,0:T(8,128)} %get-tuple-element.6, f32[4,128]{1,0:T(4,128)S(1)} %bitcast.43, f32[512,4]{0,1:T(4,128)S(1)} %add_rsqrt_fusion), kind=kLoop, calls=%fused_computation.8 | loop fusion | flops 786432 | bytes 1583104 | tf_op jit(solution)/shard_map/convert_element_type | solution.py:68
  100.6 2.0 %copy.12 = bf16[512,512]{1,0:T(8,128)(2,1)} copy(bf16[512,512]{0,1:T(8,128)(2,1)} %bitcast.40) | data formatting | bytes 1048576 | tf_op jit(solution)/shard_map/convert_element_type | solution.py:68
  (2 shorter events, 0.0 us)
Async XLA Ops:
  6.5 37.1 %copy-start = (bf16[3072,512]{1,0:T(8,128)(2,1)S(1)}, bf16[3072,512]{1,0:T(8,128)(2,1)}, u32[]{:S(2)}) copy-start(bf16[3072,512]{1,0:T(8,128)(2,1)} %param.8) | copy-start | bytes 9437188
  6.5 37.1 %all-gather.2.cloned.1.call-start = ((), (), s32[]{:S(2)}) async-start(), calls=%async_computation.2 | async-start | bytes 3538944 | tf_op jit(solution)/shard_map/all_gather | solution.py:32
  43.7 3.9 %copy-start.3 = (bf16[3072,512]{1,0:T(8,128)(2,1)S(1)}, bf16[3072,512]{1,0:T(8,128)(2,1)}, u32[]{:S(2)}) copy-start(bf16[3072,512]{1,0:T(8,128)(2,1)} %param.7) | copy-start | bytes 9437188
  43.7 3.9 %copy-start.5 = (bf16[512,3072]{1,0:T(8,128)(2,1)S(1)}, bf16[512,3072]{1,0:T(8,128)(2,1)}, u32[]{:S(2)}) copy-start(bf16[512,3072]{1,0:T(8,128)(2,1)} %all-gather.2.cloned.1.call-done) | copy-start | bytes 9437188
  47.6 1.9 %copy-start.4 = (bf16[3072,512]{1,0:T(8,128)(2,1)S(1)}, bf16[3072,512]{1,0:T(8,128)(2,1)}, u32[]{:S(2)}) copy-start(bf16[3072,512]{1,0:T(8,128)(2,1)} %param.6) | copy-start | bytes 9437188
  51.4 1.2 %copy-start.1 = (bf16[512,1536]{0,1:T(8,128)(2,1)}, bf16[512,1536]{0,1:T(8,128)(2,1)S(1)}, u32[]{:S(2)}) copy-start(bf16[512,1536]{0,1:T(8,128)(2,1)S(1)} %pad_maximum_fusion) | copy-start | bytes 4718596
  76.4 15.1 %all-to-all-start.1 = ((f32[32,16,128]{2,1,0:T(8,128)}), f32[32,16,128]{2,1,0:T(8,128)S(1)}, u32[]{:S(2)}, u32[]{:S(2)}) async-start(f32[32,16,128]{2,1,0:T(8,128)} %concatenate.7), calls=%async_computation.1 | async-start | bytes 524288 | tf_op jit(solution)/shard_map/all_to_all | solution.py:25
  94.2 4.2 %copy-start.2 = (f32[512]{0:T(512)S(1)}, f32[512]{0:T(512)}, u32[]{:S(2)}) copy-start(f32[512]{0:T(512)} %param.9) | copy-start | bytes 6148
Sparse Core Ops, SparseCore 0:
  9.2 34.4 all-gather.1

commit v3 on v2

--- a/solution.py
+++ b/solution.py
@@ -1,7 +1,7 @@
 import jax
 import jax.numpy as jnp
 from jax import lax
-from jax.sharding import PartitionSpec as P
+from jax.sharding import Mesh, PartitionSpec as P
 
 HEAD_DIM = 128
 BLOCK = 512
@@ -29,7 +29,14 @@
 def body(tokens, w_query, w_key, w_value, norm_gain):
     local_width = w_query.shape[1]
     head_count = local_width // HEAD_DIM
-    piece_rows = lax.all_gather(tokens, "tp", axis=0, tiled=True)
+    near_rows = lax.all_gather(tokens, "y", axis=0, tiled=True)
+    both_rows = lax.all_gather(near_rows, "core", axis=0, tiled=False)
+    cores, chips = both_rows.shape[0], lax.axis_size("y")
+    piece_rows = (
+        both_rows.reshape(cores, chips, tokens.shape[0], tokens.shape[1])
+        .transpose(1, 0, 2, 3)
+        .reshape(cores * chips * tokens.shape[0], tokens.shape[1])
+    )
     query_part = jnp.dot(piece_rows, w_query, preferred_element_type=jnp.float32).astype(
         jnp.bfloat16
     )
@@ -68,8 +75,16 @@
     return normed.reshape(group_len, local_width).astype(jnp.bfloat16)
 
 
+def chip_split(mesh):
+    first = mesh.devices[0]
+    cores = len({getattr(device, "core_on_chip", 0) for device in first})
+    return mesh.devices.reshape(mesh.devices.shape[0], -1, cores)
+
+
 def solution(mesh):
-    placed = (P(("ctx", "tp"), None), P(None, "tp"), P(None, "tp"), P(None, "tp"), P("tp"))
+    fine = Mesh(chip_split(mesh), ("ctx", "y", "core"))
+    heads = ("y", "core")
+    placed = (P(("ctx",) + heads, None), P(None, heads), P(None, heads), P(None, heads), P(heads))
     return jax.shard_map(
-        body, mesh=mesh, in_specs=placed, out_specs=P("ctx", "tp"), check_vma=False
+        body, mesh=fine, in_specs=placed, out_specs=P("ctx", heads), check_vma=False
     )

time: 111 us -> 130 us (1.17)
  waiting for transfers between devices: 46.9 us -> 65 us
  local copies, waits for them, and re-layouts: 3.99 us -> 6.21 us
  matrix products: 14.6 us -> 12.6 us
    all_gather x1 -> x2, waiting for transfers between devices: 36.4 us -> 54.7 us  [the longest x1 34.5 us: body(): near_rows = lax.all_gather(tokens, 'y', axis=0, tiled=True)]
    transpose x0 -> x1, local copies, waits for them, and re-layouts: none -> 2.21 us  [body(): piece_rows = both_rows.reshape(cores, chips, tokens.shape[0], tokens.shap...]
    dot_general x1, matrix products: 3.87 us -> 1.86 us  [body(): jnp.dot(piece_rows, w_value, preferred_element_type=jnp.float32)]
  transfers between devices with their start and end apart: 2 -> 3, of which waited for: 2 -> 3; matrix products, arithmetic and copies ran while one was open for 1% -> 1% of each run, Pallas kernels for 0% -> 0%
where the time goes in v3:
time: 130 us; the launch traced here: 128 us
  waiting for transfers between devices  65 us (50%)
  blocking collectives  20.7 us (16%)
  between operations  13.5 us (10%)
  matrix products  12.6 us (10%)
  local copies, waits for them, and re-layouts  6.21 us (5%)
  other arithmetic  4.89 us (4%)
  starting transfers between devices  4.59 us (4%)
    all_gather x1, waiting for transfers between devices, body(): near_rows = lax.all_gather(tokens, 'y', axis=0, tiled=True)  34.5 us
    all_to_all x1, blocking collectives, exclusive_scan(): gathered = lax.all_to_all(pieces, axis, 0, 0, tiled=True)  20.7 us
    all_gather x1, waiting for transfers between devices, body(): both_rows = lax.all_gather(near_rows, 'core', axis=0, tiled=False)  20.1 us
    all_to_all x1, waiting for transfers between devices, exclusive_scan(): returned = lax.all_to_all(before, axis, 0, 0, tiled=True)  9.64 us
    all_to_all x1, starting transfers between devices, exclusive_scan(): returned = lax.all_to_all(before, axis, 0, 0, tiled=True)  4.55 us
    dot_general x1, matrix products, body(): jnp.einsum('bhqk,bkhe->bqhe', scores, value_rows, preferred_element_type=...  4.16 us
    dot_general x1, matrix products, body(): jnp.einsum('bqhd,bhde->bqhe', query_rows.astype(jnp.float32), block_start...  2.64 us
  transfers between devices with their start and end apart: 3, of which 3 were waited for; matrix products, arithmetic and copies ran while one was open for 1% of the time, Pallas kernels for 0%

profile of v3, /device:TPU:1, one launch (start us, length us, event | category | flops | bytes accessed | tf_op | source)
XLA Modules:
  0.0 127.5 jit_solution(9691579467286573109)
XLA Ops:
  6.5 0.0 copy-start
  6.5 0.0 all-gather.4.cloned.1.call-start
  6.5 0.7 all-gather.4.cloned.1.call-update
  7.3 0.0 all-gather.6.cloned.1.call-start
  7.3 34.5 %all-gather.4.cloned.1.call-done = bf16[256,3072]{1,0:T(8,128)(2,1)} async-done(((bf16[64,3072]{1,0:T(8,128)(2,1)}), bf16[256,3072]{1,0:T(8,128)(2,1)}) %all-gather.4.cloned.1.call-update) | async-done | bytes 1572880 | tf_op jit(solution)/shard_map/all_gather | solution.py:32
  41.8 0.0 all-gather.6.cloned.1.call-update
  41.9 20.1 %all-gather.6.cloned.1.call-done = bf16[512,3072]{1,0:T(8,128)(2,1)} async-done(((bf16[256,3072]{1,0:T(8,128)(2,1)}), bf16[512,3072]{1,0:T(8,128)(2,1)}) %all-gather.6.cloned.1.call-update) | async-done | bytes 3145744 | tf_op jit(solution)/shard_map/all_gather | solution.py:33
  62.0 2.2 %copy.13 = bf16[4,2,64,3072]{3,2,1,0:T(8,128)(2,1)S(1)} copy(bf16[4,2,64,3072]{3,2,0,1:T(8,128)(2,1)} %bitcast.45) | data formatting | bytes 6291456 | tf_op jit(solution)/shard_map/transpose | solution.py:37
  64.2 0.0 copy-done
  64.2 0.0 copy-start.3
  64.2 1.9 %convolution_convert_fusion = bf16[512,512]{0,1:T(8,128)(2,1)S(1)} fusion(bf16[512,3072]{1,0:T(8,128)(2,1)S(1)} %bitcast.46, bf16[3072,512]{1,0:T(8,128)(2,1)S(1)} %copy-done), kind=kOutput, calls=%fused_computation.5 | convolution fusion | flops 1610874880 | bytes 6815744 | tf_op jit(solution)/shard_map/dot_general | solution.py:44
  66.1 0.0 copy-done.3
  66.1 0.0 copy-start.4
  66.1 1.8 %convolution_convert_fusion.1 = bf16[512,512]{0,1:T(8,128)(2,1)S(1)} fusion(bf16[512,3072]{1,0:T(8,128)(2,1)S(1)} %bitcast.47, bf16[3072,512]{1,0:T(8,128)(2,1)S(1)} %copy-done.3), kind=kOutput, calls=%fused_computation.6 | convolution fusion | flops 1610874880 | bytes 6815744 | tf_op jit(solution)/shard_map/dot_general | solution.py:43
  68.0 0.0 copy-done.4
  68.0 1.8 %convolution_convert_fusion.2 = bf16[512,512]{0,1:T(8,128)(2,1)S(1)} fusion(bf16[512,3072]{1,0:T(8,128)(2,1)S(1)} %bitcast.48, bf16[3072,512]{1,0:T(8,128)(2,1)S(1)} %copy-done.4), kind=kOutput, calls=%fused_computation.7 | convolution fusion | flops 1610874880 | bytes 6815744 | tf_op jit(solution)/shard_map/dot_general | solution.py:40
  69.8 0.1 pad_maximum_fusion
  70.0 0.0 copy-start.1
  70.0 1.1 copy-done.1
  71.1 0.3 fusion.3
  71.4 20.7 %all_to_all.10 = f32[32,16,128]{2,1,0:T(8,128)S(1)} all-to-all(f32[32,16,128]{2,1,0:T(8,128)S(1)} %bitcast.54), channel_id=1, replica_groups=mesh['ctx'=32,'y'=4,'core'=2] {'ctx'}, dimensions={0} | all-to-all | bytes 524288 | tf_op jit(solution)/shard_map/all_to_all | solution.py:22
  92.1 1.8 %fusion.6 = f32[32,16,128]{2,1,0:T(8,128)S(1)} fusion(f32[32,16,128]{2,1,0:T(8,128)S(1)} %all_to_all.10), kind=kOutput, calls=%fused_computation.18 | output fusion | flops 2031616 | bytes 524288 | tf_op jit(solution)/shard_map/jit(cumsum)/reduce_window_sum | solution.py:23
  93.9 0.7 concatenate.7
  94.7 4.5 %all-to-all-start.1 = ((f32[32,16,128]{2,1,0:T(8,128)}), f32[32,16,128]{2,1,0:T(8,128)S(1)}, u32[]{:S(2)}, u32[]{:S(2)}) async-start(f32[32,16,128]{2,1,0:T(8,128)} %concatenate.7), calls=%async_computation.1 | async-start | bytes 524288 | tf_op jit(solution)/shard_map/all_to_all | solution.py:25
  99.2 0.8 iota_compare_fusion
  100.0 9.6 %all-to-all-done.1 = f32[32,16,128]{2,1,0:T(8,128)S(1)} async-done(((f32[32,16,128]{2,1,0:T(8,128)}), f32[32,16,128]{2,1,0:T(8,128)S(1)}, u32[]{:S(2)}, u32[]{:S(2)}) %all-to-all-start.1) | async-done | bytes 262176 | tf_op jit(solution)/shard_map/all_to_all | solution.py:25
  109.7 2.6 %fusion.4 = f32[4,128,512]{2,1,0:T(8,128)} fusion(f32[4,128,128]{2,1,0:T(8,128)S(1)} %bitcast.53, bf16[1,512,3,4,128]{1,4,3,2,0:T(8,128)(2,1)} %bitcast.50), kind=kOutput, calls=%fused_computation.15 | convolution fusion | flops 402653184 | bytes 1835008 | tf_op jit(solution)/shard_map/bqhd,bhde->bqhe/dot_general | solution.py:66
  112.3 0.0 copy-start.2
  112.3 4.2 %multiply_reduce_fusion = (f32[512,4]{0,1:T(4,128)S(1)}, f32[1,512,4,128]{1,3,2,0:T(8,128)}) fusion(f32[4,128,512]{2,1,0:T(8,128)} %fusion.4, pred[512,512]{1,0:T(8,128)(4,1)} %iota_compare_fusion, bf16[1,512,3,4,128]{1,4,3,2,0:T(8,128)(2,1)} %bitcast.51), kind=kOutput, calls=%fused_computation.9 | convolution fusion | flops 539752448 | bytes 3940352 | tf_op jit(solution)/shard_map/bhqk,bkhe->bqhe/dot_general | solution.py:65
  116.5 0.0 copy-done.2
  116.5 2.2 %multiply_convert_fusion = bf16[1,512,4,128]{1,3,2,0:T(8,128)(2,1)} fusion(f32[1,512,4,128]{1,3,2,0:T(8,128)} %get-tuple-element.6, f32[4,128]{1,0:T(4,128)S(1)} %bitcast.55, f32[512,4]{0,1:T(4,128)S(1)} %add_rsqrt_fusion), kind=kLoop, calls=%fused_computation.8 | loop fusion | flops 786432 | bytes 1583104 | tf_op jit(solution)/shard_map/convert_element_type | solution.py:75
  118.7 2.0 %copy.19 = bf16[512,512]{1,0:T(8,128)(2,1)} copy(bf16[512,512]{0,1:T(8,128)(2,1)} %bitcast.52) | data formatting | bytes 1048576 | tf_op jit(solution)/shard_map/convert_element_type | solution.py:75
  (2 shorter events, 0.0 us)
Async XLA Ops:
  6.5 57.7 %copy-start = (bf16[3072,512]{1,0:T(8,128)(2,1)S(1)}, bf16[3072,512]{1,0:T(8,128)(2,1)}, u32[]{:S(2)}) copy-start(bf16[3072,512]{1,0:T(8,128)(2,1)} %param.8) | copy-start | bytes 9437188
  6.5 35.3 %all-gather.4.cloned.1.call-start = ((), (), s32[]{:S(2)}) async-start(), calls=%async_computation.2 | async-start | bytes 1966080 | tf_op jit(solution)/shard_map/all_gather | solution.py:32
  7.3 54.7 %all-gather.6.cloned.1.call-start = ((), (), s32[]{:S(2)}) async-start(), calls=%async_computation.3 | async-start | bytes 4718592 | tf_op jit(solution)/shard_map/all_gather | solution.py:33
  64.2 1.9 %copy-start.3 = (bf16[3072,512]{1,0:T(8,128)(2,1)S(1)}, bf16[3072,512]{1,0:T(8,128)(2,1)}, u32[]{:S(2)}) copy-start(bf16[3072,512]{1,0:T(8,128)(2,1)} %param.7) | copy-start | bytes 9437188
  66.1 1.9 %copy-start.4 = (bf16[3072,512]{1,0:T(8,128)(2,1)S(1)}, bf16[3072,512]{1,0:T(8,128)(2,1)}, u32[]{:S(2)}) copy-start(bf16[3072,512]{1,0:T(8,128)(2,1)} %param.6) | copy-start | bytes 9437188
  70.0 1.1 copy-start.1
  94.7 15.0 %all-to-all-start.1 = ((f32[32,16,128]{2,1,0:T(8,128)}), f32[32,16,128]{2,1,0:T(8,128)S(1)}, u32[]{:S(2)}, u32[]{:S(2)}) async-start(f32[32,16,128]{2,1,0:T(8,128)} %concatenate.7), calls=%async_computation.1 | async-start | bytes 524288 | tf_op jit(solution)/shard_map/all_to_all | solution.py:25
  112.3 4.2 %copy-start.2 = (f32[512]{0:T(512)S(1)}, f32[512]{0:T(512)}, u32[]{:S(2)}) copy-start(f32[512]{0:T(512)} %param.9) | copy-start | bytes 6148
Sparse Core Ops, SparseCore 0:
  9.1 32.6 all-gather.3
  43.6 18.3 all-gather.5

commit v4 on v3

--- a/solution.py
+++ b/solution.py
@@ -26,17 +26,22 @@
     return returned.reshape(value.shape)
 
 
+def spread(value, axis):
+    size = lax.axis_size(axis)
+    copies = jnp.broadcast_to(value[None], (size,) + value.shape)
+    return lax.all_to_all(copies, axis, 0, 0, tiled=True)
+
+
+def gather_rows(tokens):
+    near = spread(tokens, "y")
+    both = spread(near, "core")
+    return both.transpose(1, 0, 2, 3).reshape(-1, tokens.shape[1])
+
+
 def body(tokens, w_query, w_key, w_value, norm_gain):
     local_width = w_query.shape[1]
     head_count = local_width // HEAD_DIM
-    near_rows = lax.all_gather(tokens, "y", axis=0, tiled=True)
-    both_rows = lax.all_gather(near_rows, "core", axis=0, tiled=False)
-    cores, chips = both_rows.shape[0], lax.axis_size("y")
-    piece_rows = (
-        both_rows.reshape(cores, chips, tokens.shape[0], tokens.shape[1])
-        .transpose(1, 0, 2, 3)
-        .reshape(cores * chips * tokens.shape[0], tokens.shape[1])
-    )
+    piece_rows = gather_rows(tokens)
     query_part = jnp.dot(piece_rows, w_query, preferred_element_type=jnp.float32).astype(
         jnp.bfloat16
     )

time: 130 us -> 94 us (0.72)
  waiting for transfers between devices: 65 us -> 9.85 us
  blocking collectives: 20.7 us -> 54.8 us
  between operations: 13.5 us -> 0.13 us
    all_gather x2 -> x0, waiting for transfers between devices: 54.7 us -> none  [the longest x1 34.5 us: body(): near_rows = lax.all_gather(tokens, 'y', axis=0, tiled=True)]
    all_to_all x0 -> x2, blocking collectives: none -> 32.4 us  [spread(): return lax.all_to_all(copies, axis, 0, 0, tiled=True)]
    transpose x1 -> x0, local copies, waits for them, and re-layouts: 2.21 us -> none  [body(): piece_rows = both_rows.reshape(cores, chips, tokens.shape[0], tokens.shap...]
    all_to_all x1, blocking collectives: 20.7 us -> 22.4 us  [exclusive_scan(): gathered = lax.all_to_all(pieces, axis, 0, 0, tiled=True)]
    broadcast_in_dim x0 -> x2, local copies, waits for them, and re-layouts: none -> 1.69 us  [spread(): copies = jnp.broadcast_to(value[None], (size,) + value.shape)]
  transfers between devices with their start and end apart: 3 -> 1, of which waited for: 3 -> 1; matrix products, arithmetic and copies ran while one was open for 1% -> 1% of each run, Pallas kernels for 0% -> 0%
where the time goes in v4:
time: 94 us; the launch traced here: 92.7 us
  blocking collectives  54.8 us (58%)
  matrix products  12.6 us (13%)
  waiting for transfers between devices  9.85 us (10%)
  local copies, waits for them, and re-layouts  5.91 us (6%)
  other arithmetic  4.88 us (5%)
  starting transfers between devices  4.59 us (5%)
    all_to_all x2, blocking collectives, spread(): return lax.all_to_all(copies, axis, 0, 0, tiled=True)  32.4 us
    all_to_all x1, blocking collectives, exclusive_scan(): gathered = lax.all_to_all(pieces, axis, 0, 0, tiled=True)  22.4 us
    all_to_all x1, waiting for transfers between devices, exclusive_scan(): returned = lax.all_to_all(before, axis, 0, 0, tiled=True)  9.85 us
    all_to_all x1, starting transfers between devices, exclusive_scan(): returned = lax.all_to_all(before, axis, 0, 0, tiled=True)  4.59 us
    dot_general x1, matrix products, body(): jnp.einsum('bhqk,bkhe->bqhe', scores, value_rows, preferred_element_type=...  4.16 us
    dot_general x1, matrix products, body(): jnp.einsum('bqhd,bhde->bqhe', query_rows.astype(jnp.float32), block_start...  2.63 us
    convert_element_type x1, other arithmetic, body(): return normed.reshape(group_len, local_width).astype(jnp.bfloat16)  2.17 us
    convert_element_type x1, local copies, waits for them, and re-layouts, body(): return normed.reshape(group_len, local_width).astype(jnp.bfloat16)  2.05 us
  transfers between devices with their start and end apart: 1, of which 1 were waited for; matrix products, arithmetic and copies ran while one was open for 1% of the time, Pallas kernels for 0%

profile of v4, /device:TPU:1, one launch (start us, length us, event | category | flops | bytes accessed | tf_op | source)
XLA Modules:
  0.0 92.7 jit_solution(12762818792315771368)
XLA Ops:
  0.0 0.0 copy-start
  0.0 1.3 %broadcast_in_dim.12 = bf16[4,64,3072]{2,1,0:T(8,128)(2,1)S(1)} broadcast(bf16[64,3072]{1,0:T(8,128)(2,1)} %param.5), dimensions={1,2} | broadcast | bytes 1966080 | tf_op jit(solution)/shard_map/broadcast_in_dim | solution.py:31
  1.3 24.7 %all_to_all.20 = bf16[4,64,3072]{2,1,0:T(8,128)(2,1)S(1)} all-to-all(bf16[4,64,3072]{2,1,0:T(8,128)(2,1)S(1)} %broadcast_in_dim.12), channel_id=1, replica_groups=mesh['ctx'=32,'y'=4,'core'=2] {'y'}, dimensions={0} | all-to-all | bytes 3145728 | tf_op jit(solution)/shard_map/all_to_all | solution.py:32
  26.0 0.4 broadcast_in_dim.13
  26.4 7.7 %all_to_all.21 = bf16[2,4,64,3072]{3,2,1,0:T(8,128)(2,1)S(1)} all-to-all(bf16[2,4,64,3072]{3,2,1,0:T(8,128)(2,1)S(1)} %broadcast_in_dim.13), channel_id=1, replica_groups=mesh['ctx'=32,'y'=4,'core'=2] {'core'}, dimensions={0} | all-to-all | bytes 6291456 | tf_op jit(solution)/shard_map/all_to_all | solution.py:32
  34.1 0.2 copy.13
  34.3 0.0 copy-done
  34.3 0.0 copy-start.3
  34.3 1.9 %convolution_convert_fusion = bf16[512,512]{0,1:T(8,128)(2,1)S(1)} fusion(bf16[512,3072]{1,0:T(8,128)(2,1)S(1)} %bitcast.44, bf16[3072,512]{1,0:T(8,128)(2,1)S(1)} %copy-done), kind=kOutput, calls=%fused_computation.5 | convolution fusion | flops 1610874880 | bytes 6815744 | tf_op jit(solution)/shard_map/dot_general | solution.py:49
  36.2 0.0 copy-done.3
  36.2 0.0 copy-start.4
  36.2 1.8 %convolution_convert_fusion.1 = bf16[512,512]{0,1:T(8,128)(2,1)S(1)} fusion(bf16[512,3072]{1,0:T(8,128)(2,1)S(1)} %bitcast.45, bf16[3072,512]{1,0:T(8,128)(2,1)S(1)} %copy-done.3), kind=kOutput, calls=%fused_computation.6 | convolution fusion | flops 1610874880 | bytes 6815744 | tf_op jit(solution)/shard_map/dot_general | solution.py:48
  38.0 0.0 copy-done.4
  38.1 1.8 %convolution_convert_fusion.2 = bf16[512,512]{0,1:T(8,128)(2,1)S(1)} fusion(bf16[512,3072]{1,0:T(8,128)(2,1)S(1)} %bitcast.46, bf16[3072,512]{1,0:T(8,128)(2,1)S(1)} %copy-done.4), kind=kOutput, calls=%fused_computation.7 | convolution fusion | flops 1610874880 | bytes 6815744 | tf_op jit(solution)/shard_map/dot_general | solution.py:45
  39.9 0.1 pad_maximum_fusion
  40.0 0.0 copy-start.1
  40.0 1.2 %copy-done.1 = bf16[512,1536]{0,1:T(8,128)(2,1)} copy-done((bf16[512,1536]{0,1:T(8,128)(2,1)}, bf16[512,1536]{0,1:T(8,128)(2,1)S(1)}, u32[]{:S(2)}) %copy-start.1) | copy-done | bytes 1572888
  41.2 0.3 fusion.3
  41.5 22.4 %all_to_all.22 = f32[32,16,128]{2,1,0:T(8,128)S(1)} all-to-all(f32[32,16,128]{2,1,0:T(8,128)S(1)} %bitcast.52), channel_id=1, replica_groups=mesh['ctx'=32,'y'=4,'core'=2] {'ctx'}, dimensions={0} | all-to-all | bytes 524288 | tf_op jit(solution)/shard_map/all_to_all | solution.py:22
  63.9 1.8 %fusion.6 = f32[32,16,128]{2,1,0:T(8,128)S(1)} fusion(f32[32,16,128]{2,1,0:T(8,128)S(1)} %all_to_all.22), kind=kOutput, calls=%fused_computation.18 | output fusion | flops 2031616 | bytes 524288 | tf_op jit(solution)/shard_map/jit(cumsum)/reduce_window_sum | solution.py:23
  65.8 0.7 concatenate.7
  66.5 4.6 %all-to-all-start.3 = ((f32[32,16,128]{2,1,0:T(8,128)}), f32[32,16,128]{2,1,0:T(8,128)S(1)}, u32[]{:S(2)}, u32[]{:S(2)}) async-start(f32[32,16,128]{2,1,0:T(8,128)} %concatenate.7), calls=%async_computation.3 | async-start | bytes 524288 | tf_op jit(solution)/shard_map/all_to_all | solution.py:25
  71.1 0.8 iota_compare_fusion
  71.9 9.8 %all-to-all-done.3 = f32[32,16,128]{2,1,0:T(8,128)S(1)} async-done(((f32[32,16,128]{2,1,0:T(8,128)}), f32[32,16,128]{2,1,0:T(8,128)S(1)}, u32[]{:S(2)}, u32[]{:S(2)}) %all-to-all-start.3) | async-done | bytes 262176 | tf_op jit(solution)/shard_map/all_to_all | solution.py:25
  81.7 2.6 %fusion.4 = f32[4,128,512]{2,1,0:T(8,128)} fusion(f32[4,128,128]{2,1,0:T(8,128)S(1)} %bitcast.51, bf16[1,512,3,4,128]{1,4,3,2,0:T(8,128)(2,1)} %bitcast.48), kind=kOutput, calls=%fused_computation.15 | convolution fusion | flops 402653184 | bytes 1835008 | tf_op jit(solution)/shard_map/bqhd,bhde->bqhe/dot_general | solution.py:71
  84.3 0.0 copy-start.2
  84.3 4.2 %multiply_reduce_fusion = (f32[512,4]{0,1:T(4,128)S(1)}, f32[1,512,4,128]{1,3,2,0:T(8,128)}) fusion(f32[4,128,512]{2,1,0:T(8,128)} %fusion.4, pred[512,512]{1,0:T(8,128)(4,1)} %iota_compare_fusion, bf16[1,512,3,4,128]{1,4,3,2,0:T(8,128)(2,1)} %bitcast.49), kind=kOutput, calls=%fused_computation.9 | convolution fusion | flops 539752448 | bytes 3940352 | tf_op jit(solution)/shard_map/bhqk,bkhe->bqhe/dot_general | solution.py:70
  88.5 0.0 copy-done.2
  88.5 2.2 %multiply_convert_fusion = bf16[1,512,4,128]{1,3,2,0:T(8,128)(2,1)} fusion(f32[1,512,4,128]{1,3,2,0:T(8,128)} %get-tuple-element.6, f32[4,128]{1,0:T(4,128)S(1)} %bitcast.53, f32[512,4]{0,1:T(4,128)S(1)} %add_rsqrt_fusion), kind=kLoop, calls=%fused_computation.8 | loop fusion | flops 786432 | bytes 1583104 | tf_op jit(solution)/shard_map/convert_element_type | solution.py:80
  90.7 2.0 %copy.19 = bf16[512,512]{1,0:T(8,128)(2,1)} copy(bf16[512,512]{0,1:T(8,128)(2,1)} %bitcast.50) | data formatting | bytes 1048576 | tf_op jit(solution)/shard_map/convert_element_type | solution.py:80
  (2 shorter events, 0.0 us)
Async XLA Ops:
  0.0 34.3 %copy-start = (bf16[3072,512]{1,0:T(8,128)(2,1)S(1)}, bf16[3072,512]{1,0:T(8,128)(2,1)}, u32[]{:S(2)}) copy-start(bf16[3072,512]{1,0:T(8,128)(2,1)} %param.8) | copy-start | bytes 9437188
  34.3 1.9 %copy-start.3 = (bf16[3072,512]{1,0:T(8,128)(2,1)S(1)}, bf16[3072,512]{1,0:T(8,128)(2,1)}, u32[]{:S(2)}) copy-start(bf16[3072,512]{1,0:T(8,128)(2,1)} %param.7) | copy-start | bytes 9437188
  36.2 1.9 %copy-start.4 = (bf16[3072,512]{1,0:T(8,128)(2,1)S(1)}, bf16[3072,512]{1,0:T(8,128)(2,1)}, u32[]{:S(2)}) copy-start(bf16[3072,512]{1,0:T(8,128)(2,1)} %param.6) | copy-start | bytes 9437188
  40.0 1.2 %copy-start.1 = (bf16[512,1536]{0,1:T(8,128)(2,1)}, bf16[512,1536]{0,1:T(8,128)(2,1)S(1)}, u32[]{:S(2)}) copy-start(bf16[512,1536]{0,1:T(8,128)(2,1)S(1)} %pad_maximum_fusion) | copy-start | bytes 4718596
  66.5 15.2 %all-to-all-start.3 = ((f32[32,16,128]{2,1,0:T(8,128)}), f32[32,16,128]{2,1,0:T(8,128)S(1)}, u32[]{:S(2)}, u32[]{:S(2)}) async-start(f32[32,16,128]{2,1,0:T(8,128)} %concatenate.7), calls=%async_computation.3 | async-start | bytes 524288 | tf_op jit(solution)/shard_map/all_to_all | solution.py:25
  84.3 4.2 %copy-start.2 = (f32[512]{0:T(512)S(1)}, f32[512]{0:T(512)}, u32[]{:S(2)}) copy-start(f32[512]{0:T(512)} %param.9) | copy-start | bytes 6148

commit v5 on v4

--- a/solution.py
+++ b/solution.py
@@ -20,8 +20,13 @@
     size = lax.axis_size(axis)
     pieces = value.reshape(size, -1, value.shape[-1])
     gathered = lax.all_to_all(pieces, axis, 0, 0, tiled=True)
-    running = jnp.cumsum(gathered, axis=0)
-    before = jnp.concatenate([jnp.zeros_like(running[:1]), running[:-1]], axis=0)
+    earlier = jnp.arange(size)[:, None] > jnp.arange(size)[None, :]
+    before = jnp.einsum(
+        "jk,kre->jre",
+        earlier.astype(gathered.dtype),
+        gathered,
+        precision=lax.Precision.HIGHEST,
+    )
     returned = lax.all_to_all(before, axis, 0, 0, tiled=True)
     return returned.reshape(value.shape)
 
@@ -68,12 +73,12 @@
     causal = jnp.arange(BLOCK)[:, None] >= jnp.arange(BLOCK)[None, :]
     scores = jnp.where(causal[None, None], scores, jnp.float32(0.0)).astype(jnp.bfloat16)
     inner = jnp.einsum("bhqk,bkhe->bqhe", scores, value_rows, preferred_element_type=jnp.float32)
+    inner = lax.optimization_barrier(inner)
+    start_high = block_start.astype(jnp.bfloat16)
+    start_low = (block_start - start_high.astype(jnp.float32)).astype(jnp.bfloat16)
     carried_part = jnp.einsum(
-        "bqhd,bhde->bqhe",
-        query_rows.astype(jnp.float32),
-        block_start,
-        precision=lax.Precision.HIGHEST,
-    )
+        "bqhd,bhde->bqhe", query_rows, start_high, preferred_element_type=jnp.float32
+    ) + jnp.einsum("bqhd,bhde->bqhe", query_rows, start_low, preferred_element_type=jnp.float32)
     mixed = inner + carried_part
     mean_square = jnp.mean(mixed * mixed, axis=-1, keepdims=True)
     normed = mixed * lax.rsqrt(mean_square + EPSILON) * norm_gain.reshape(head_count, HEAD_DIM)

time: 94 us -> 89.5 us (0.952)
  waiting for transfers between devices: 9.85 us -> 6.06 us
  other arithmetic: 4.88 us -> 1.84 us
  local copies, waits for them, and re-layouts: 5.91 us -> 7.8 us
    all_to_all x1, waiting for transfers between devices: 9.85 us -> 6.06 us  [exclusive_scan(): returned = lax.all_to_all(before, axis, 0, 0, tiled=True)]
    another operation x1 -> x0, other arithmetic: 1.81 us -> none  [exclusive_scan(): running = jnp.cumsum(gathered, axis=0)]
    convert_element_type x1, other arithmetic: 2.17 us -> 0.95 us  [body(): return normed.reshape(group_len, local_width).astype(jnp.bfloat16)]
    another operation x0 -> x1, local copies, waits for them, and re-layouts: none -> 1.09 us  [body(): block_start = prefix_state[None] + earlier]
    dot_general x1 -> x3, matrix products: 2.63 us -> 3.37 us  [the longest x1 1.71 us: body(): jnp.einsum('bqhd,bhde->bqhe', query_rows, start_low, preferred_element_ty...]
    unnamed x10 -> x12, local copies, waits for them, and re-layouts: 1.24 us -> 1.92 us
  transfers between devices with their start and end apart: 1 -> 1, of which waited for: 1 -> 1; matrix products, arithmetic and copies ran while one was open for 1% -> 5% of each run, Pallas kernels for 0% -> 0%
where the time goes in v5:
time: 89.5 us; the launch traced here: 88.2 us
  blocking collectives  54.8 us (61%)
  matrix products  13 us (15%)
  local copies, waits for them, and re-layouts  7.8 us (9%)
  waiting for transfers between devices  6.06 us (7%)
  starting transfers between devices  4.6 us (5%)
  other arithmetic  1.84 us (2%)
    all_to_all x2, blocking collectives, spread(): return lax.all_to_all(copies, axis, 0, 0, tiled=True)  32.4 us
    all_to_all x1, blocking collectives, exclusive_scan(): gathered = lax.all_to_all(pieces, axis, 0, 0, tiled=True)  22.4 us
    all_to_all x1, waiting for transfers between devices, exclusive_scan(): returned = lax.all_to_all(before, axis, 0, 0, tiled=True)  6.06 us
    all_to_all x1, starting transfers between devices, exclusive_scan(): returned = lax.all_to_all(before, axis, 0, 0, tiled=True)  4.6 us
    dot_general x1, matrix products, body(): jnp.einsum('bhqk,bkhe->bqhe', scores, value_rows, preferred_element_type=...  3.79 us
    convert_element_type x1, local copies, waits for them, and re-layouts, body(): return normed.reshape(group_len, local_width).astype(jnp.bfloat16)  2.05 us
    unnamed x12, local copies, waits for them, and re-layouts  1.92 us
    dot_general x1, matrix products, body(): jnp.dot(piece_rows, w_value, preferred_element_type=jnp.float32)  1.86 us
  transfers between devices with their start and end apart: 1, of which 1 were waited for; matrix products, arithmetic and copies ran while one was open for 5% of the time, Pallas kernels for 0%

profile of v5, /device:TPU:1, one launch (start us, length us, event | category | flops | bytes accessed | tf_op | source)
XLA Modules:
  0.0 88.2 jit_solution(9255065050022134919)
XLA Ops:
  0.0 0.0 copy-start
  0.0 1.3 %broadcast_in_dim.12 = bf16[4,64,3072]{2,1,0:T(8,128)(2,1)S(1)} broadcast(bf16[64,3072]{1,0:T(8,128)(2,1)} %param.5), dimensions={1,2} | broadcast | bytes 1966080 | tf_op jit(solution)/shard_map/broadcast_in_dim | solution.py:36
  1.3 24.7 %all_to_all.20 = bf16[4,64,3072]{2,1,0:T(8,128)(2,1)S(1)} all-to-all(bf16[4,64,3072]{2,1,0:T(8,128)(2,1)S(1)} %broadcast_in_dim.12), channel_id=1, replica_groups=mesh['ctx'=32,'y'=4,'core'=2] {'y'}, dimensions={0} | all-to-all | bytes 3145728 | tf_op jit(solution)/shard_map/all_to_all | solution.py:37
  26.0 0.4 broadcast_in_dim.13
  26.4 7.7 %all_to_all.21 = bf16[2,4,64,3072]{3,2,1,0:T(8,128)(2,1)S(1)} all-to-all(bf16[2,4,64,3072]{3,2,1,0:T(8,128)(2,1)S(1)} %broadcast_in_dim.13), channel_id=1, replica_groups=mesh['ctx'=32,'y'=4,'core'=2] {'core'}, dimensions={0} | all-to-all | bytes 6291456 | tf_op jit(solution)/shard_map/all_to_all | solution.py:37
  34.1 0.2 copy.19
  34.3 0.0 copy-done
  34.3 0.0 copy-start.4
  34.3 1.9 %convolution_convert_fusion = bf16[512,512]{0,1:T(8,128)(2,1)S(1)} fusion(bf16[512,3072]{1,0:T(8,128)(2,1)S(1)} %bitcast.53, bf16[3072,512]{1,0:T(8,128)(2,1)S(1)} %copy-done), kind=kOutput, calls=%fused_computation.7 | convolution fusion | flops 1610874880 | bytes 6815744 | tf_op jit(solution)/shard_map/dot_general | solution.py:54
  36.2 0.0 copy-done.4
  36.2 0.0 copy-start.5
  36.2 1.8 %convolution_convert_fusion.1 = bf16[512,512]{0,1:T(8,128)(2,1)S(1)} fusion(bf16[512,3072]{1,0:T(8,128)(2,1)S(1)} %bitcast.54, bf16[3072,512]{1,0:T(8,128)(2,1)S(1)} %copy-done.4), kind=kOutput, calls=%fused_computation.8 | convolution fusion | flops 1610874880 | bytes 6815744 | tf_op jit(solution)/shard_map/dot_general | solution.py:53
  38.0 0.0 copy-done.5
  38.1 1.8 %convolution_convert_fusion.2 = bf16[512,512]{0,1:T(8,128)(2,1)S(1)} fusion(bf16[512,3072]{1,0:T(8,128)(2,1)S(1)} %bitcast.55, bf16[3072,512]{1,0:T(8,128)(2,1)S(1)} %copy-done.5), kind=kOutput, calls=%fused_computation.9 | convolution fusion | flops 1610874880 | bytes 6815744 | tf_op jit(solution)/shard_map/dot_general | solution.py:50
  39.9 0.1 pad_maximum_fusion
  40.0 0.0 copy-start.1
  40.0 1.1 %copy-done.1 = bf16[512,1536]{0,1:T(8,128)(2,1)} copy-done((bf16[512,1536]{0,1:T(8,128)(2,1)}, bf16[512,1536]{0,1:T(8,128)(2,1)S(1)}, u32[]{:S(2)}) %copy-start.1) | copy-done | bytes 1572888
  41.2 0.3 fusion.4
  41.5 22.4 %all_to_all.22 = f32[32,16,128]{2,1,0:T(8,128)S(1)} all-to-all(f32[32,16,128]{2,1,0:T(8,128)S(1)} %bitcast.58), channel_id=1, replica_groups=mesh['ctx'=32,'y'=4,'core'=2] {'ctx'}, dimensions={0} | all-to-all | bytes 524288 | tf_op jit(solution)/shard_map/all_to_all | solution.py:22
  63.9 0.3 fusion.6
  64.2 0.9 copy.25
  65.1 4.6 %all-to-all-start.3 = ((f32[32,16,128]{2,1,0:T(8,128)}), f32[32,16,128]{2,1,0:T(8,128)S(1)}, u32[]{:S(2)}, u32[]{:S(2)}) async-start(f32[32,16,128]{2,1,0:T(8,128)} %copy.25), calls=%async_computation.3 | async-start | bytes 524288 | tf_op jit(solution)/shard_map/all_to_all | solution.py:30
  69.7 0.8 iota_compare_fusion
  70.5 3.8 %fusion.1 = f32[1,512,4,128]{1,3,2,0:T(8,128)} fusion(pred[512,512]{1,0:T(8,128)(4,1)} %iota_compare_fusion, bf16[1,512,3,4,128]{1,4,3,2,0:T(8,128)(2,1)} %bitcast.50), kind=kOutput, calls=%fused_computation.3 | convolution fusion | flops 538968064 | bytes 2883584 | tf_op jit(solution)/shard_map/bhqk,bkhe->bqhe/dot_general | solution.py:75
  74.3 6.1 %all-to-all-done.3 = f32[32,16,128]{2,1,0:T(8,128)S(1)} async-done(((f32[32,16,128]{2,1,0:T(8,128)}), f32[32,16,128]{2,1,0:T(8,128)S(1)}, u32[]{:S(2)}, u32[]{:S(2)}) %all-to-all-start.3) | async-done | bytes 262176 | tf_op jit(solution)/shard_map/all_to_all | solution.py:30
  80.3 0.0 copy-start.2
  80.3 0.7 copy-done.2
  81.0 0.0 copy-start.3
  81.0 1.1 %copy.26 = f32[4,128,128]{1,2,0:T(8,128)S(1)} copy(f32[4,128,128]{2,1,0:T(8,128)} %bitcast.57) | data formatting | bytes 524288 | tf_op jit(solution)/shard_map/broadcast_in_dim;reshape | solution.py:71
  82.1 1.3 %fusion.5 = f32[4,128,512]{2,1,0:T(8,128)S(1)} fusion(bf16[1,512,3,4,128]{1,4,3,2,0:T(8,128)(2,1)} %bitcast.51, f32[4,128,128]{1,2,0:T(8,128)S(1)} %copy.26), kind=kOutput, calls=%fused_computation.17 | convolution fusion | flops 67174400 | bytes 1835008 | tf_op jit(solution)/shard_map/bqhd,bhde->bqhe/dot_general | solution.py:79
  83.5 1.7 %multiply_reduce_fusion = (f32[512,4]{0,1:T(4,128)S(1)}, f32[1,512,4,128]{1,3,2,0:T(8,128)S(1)}) fusion(f32[1,512,4,128]{1,3,2,0:T(8,128)} %fusion.1, f32[4,128,512]{2,1,0:T(8,128)S(1)} %fusion.5, bf16[1,512,3,4,128]{1,4,3,2,0:T(8,128)(2,1)} %bitcast.52, f32[4,128,128]{1,2,0:T(8,128)S(1)} %copy.26), kind=kOutput, calls=%fused_computation.11 | convolution fusion | flops 68417536 | bytes 3940352 | tf_op jit(solution)/shard_map/bqhd,bhde->bqhe/dot_general | solution.py:81
  85.2 0.0 copy-done.3
  85.2 0.9 %multiply_convert_fusion = bf16[1,512,4,128]{1,3,2,0:T(8,128)(2,1)} fusion(f32[1,512,4,128]{1,3,2,0:T(8,128)S(1)} %get-tuple-element.6, f32[4,128]{1,0:T(4,128)S(1)} %bitcast.59, f32[512,4]{0,1:T(4,128)S(1)} %add_rsqrt_fusion), kind=kLoop, calls=%fused_computation.10 | loop fusion | flops 786432 | bytes 1583104 | tf_op jit(solution)/shard_map/convert_element_type | solution.py:85
  86.2 2.0 %copy.28 = bf16[512,512]{1,0:T(8,128)(2,1)} copy(bf16[512,512]{0,1:T(8,128)(2,1)} %bitcast.56) | data formatting | bytes 1048576 | tf_op jit(solution)/shard_map/convert_element_type | solution.py:85
  (1 shorter events, 0.0 us)
Async XLA Ops:
  0.0 34.3 %copy-start = (bf16[3072,512]{1,0:T(8,128)(2,1)S(1)}, bf16[3072,512]{1,0:T(8,128)(2,1)}, u32[]{:S(2)}) copy-start(bf16[3072,512]{1,0:T(8,128)(2,1)} %param.8) | copy-start | bytes 9437188
  34.3 1.9 %copy-start.4 = (bf16[3072,512]{1,0:T(8,128)(2,1)S(1)}, bf16[3072,512]{1,0:T(8,128)(2,1)}, u32[]{:S(2)}) copy-start(bf16[3072,512]{1,0:T(8,128)(2,1)} %param.7) | copy-start | bytes 9437188
  36.2 1.9 %copy-start.5 = (bf16[3072,512]{1,0:T(8,128)(2,1)S(1)}, bf16[3072,512]{1,0:T(8,128)(2,1)}, u32[]{:S(2)}) copy-start(bf16[3072,512]{1,0:T(8,128)(2,1)} %param.6) | copy-start | bytes 9437188
  40.0 1.2 %copy-start.1 = (bf16[512,1536]{0,1:T(8,128)(2,1)}, bf16[512,1536]{0,1:T(8,128)(2,1)S(1)}, u32[]{:S(2)}) copy-start(bf16[512,1536]{0,1:T(8,128)(2,1)S(1)} %pad_maximum_fusion) | copy-start | bytes 4718596
  65.1 15.2 %all-to-all-start.3 = ((f32[32,16,128]{2,1,0:T(8,128)}), f32[32,16,128]{2,1,0:T(8,128)S(1)}, u32[]{:S(2)}, u32[]{:S(2)}) async-start(f32[32,16,128]{2,1,0:T(8,128)} %copy.25), calls=%async_computation.3 | async-start | bytes 524288 | tf_op jit(solution)/shard_map/all_to_all | solution.py:30
  80.3 0.7 copy-start.2
  81.0 4.2 %copy-start.3 = (f32[512]{0:T(512)S(1)}, f32[512]{0:T(512)}, u32[]{:S(2)}) copy-start(f32[512]{0:T(512)} %param.9) | copy-start | bytes 6148

commit v6 on v5

--- a/solution.py
+++ b/solution.py
@@ -21,12 +21,11 @@
     pieces = value.reshape(size, -1, value.shape[-1])
     gathered = lax.all_to_all(pieces, axis, 0, 0, tiled=True)
     earlier = jnp.arange(size)[:, None] > jnp.arange(size)[None, :]
-    before = jnp.einsum(
-        "jk,kre->jre",
+    before = jnp.dot(
         earlier.astype(gathered.dtype),
-        gathered,
+        gathered.reshape(size, -1),
         precision=lax.Precision.HIGHEST,
-    )
+    ).reshape(pieces.shape)
     returned = lax.all_to_all(before, axis, 0, 0, tiled=True)
     return returned.reshape(value.shape)
 
@@ -74,7 +73,7 @@
     scores = jnp.where(causal[None, None], scores, jnp.float32(0.0)).astype(jnp.bfloat16)
     inner = jnp.einsum("bhqk,bkhe->bqhe", scores, value_rows, preferred_element_type=jnp.float32)
     inner = lax.optimization_barrier(inner)
-    start_high = block_start.astype(jnp.bfloat16)
+    start_high = lax.optimization_barrier(block_start.astype(jnp.bfloat16))
     start_low = (block_start - start_high.astype(jnp.float32)).astype(jnp.bfloat16)
     carried_part = jnp.einsum(
         "bqhd,bhde->bqhe", query_rows, start_high, preferred_element_type=jnp.float32

time: 89.5 us -> 87.8 us (0.981)
  local copies, waits for them, and re-layouts: 7.8 us -> 6.02 us
    another operation x1 -> x0, local copies, waits for them, and re-layouts: 1.09 us -> none  [body(): block_start = prefix_state[None] + earlier]
    unnamed x12 -> x10, local copies, waits for them, and re-layouts: 1.92 us -> 1.22 us
where the time goes in v6:
time: 87.8 us; the launch traced here: 86.6 us
  blocking collectives  54.8 us (62%)
  matrix products  13.1 us (15%)
  waiting for transfers between devices  6.07 us (7%)
  local copies, waits for them, and re-layouts  6.02 us (7%)
  starting transfers between devices  4.59 us (5%)
  other arithmetic  1.86 us (2%)
    all_to_all x2, blocking collectives, spread(): return lax.all_to_all(copies, axis, 0, 0, tiled=True)  32.4 us
    all_to_all x1, blocking collectives, exclusive_scan(): gathered = lax.all_to_all(pieces, axis, 0, 0, tiled=True)  22.4 us
    all_to_all x1, waiting for transfers between devices, exclusive_scan(): returned = lax.all_to_all(before, axis, 0, 0, tiled=True)  6.07 us
    all_to_all x1, starting transfers between devices, exclusive_scan(): returned = lax.all_to_all(before, axis, 0, 0, tiled=True)  4.59 us
    dot_general x1, matrix products, body(): jnp.einsum('bhqk,bkhe->bqhe', scores, value_rows, preferred_element_type=...  3.78 us
    convert_element_type x1, local copies, waits for them, and re-layouts, body(): return normed.reshape(group_len, local_width).astype(jnp.bfloat16)  2.05 us
    dot_general x1, matrix products, body(): jnp.dot(piece_rows, w_value, preferred_element_type=jnp.float32)  1.86 us
    dot_general x1, matrix products, body(): jnp.dot(piece_rows, w_key, preferred_element_type=jnp.float32)  1.83 us
  transfers between devices with their start and end apart: 1, of which 1 were waited for; matrix products, arithmetic and copies ran while one was open for 5% of the time, Pallas kernels for 0%

profile of v6, /device:TPU:1, one launch (start us, length us, event | category | flops | bytes accessed | tf_op | source)
XLA Modules:
  0.0 86.6 jit_solution(10604242759914316568)
XLA Ops:
  0.0 0.0 copy-start
  0.0 1.3 %broadcast_in_dim.12 = bf16[4,64,3072]{2,1,0:T(8,128)(2,1)S(1)} broadcast(bf16[64,3072]{1,0:T(8,128)(2,1)} %param.5), dimensions={1,2} | broadcast | bytes 1966080 | tf_op jit(solution)/shard_map/broadcast_in_dim | solution.py:35
  1.3 24.7 %all_to_all.20 = bf16[4,64,3072]{2,1,0:T(8,128)(2,1)S(1)} all-to-all(bf16[4,64,3072]{2,1,0:T(8,128)(2,1)S(1)} %broadcast_in_dim.12), channel_id=1, replica_groups=mesh['ctx'=32,'y'=4,'core'=2] {'y'}, dimensions={0} | all-to-all | bytes 3145728 | tf_op jit(solution)/shard_map/all_to_all | solution.py:36
  26.0 0.4 broadcast_in_dim.13
  26.4 7.7 %all_to_all.21 = bf16[2,4,64,3072]{3,2,1,0:T(8,128)(2,1)S(1)} all-to-all(bf16[2,4,64,3072]{3,2,1,0:T(8,128)(2,1)S(1)} %broadcast_in_dim.13), channel_id=1, replica_groups=mesh['ctx'=32,'y'=4,'core'=2] {'core'}, dimensions={0} | all-to-all | bytes 6291456 | tf_op jit(solution)/shard_map/all_to_all | solution.py:36
  34.1 0.2 copy.18
  34.3 0.0 copy-done
  34.3 0.0 copy-start.3
  34.3 1.9 %convolution_convert_fusion = bf16[512,512]{0,1:T(8,128)(2,1)S(1)} fusion(bf16[512,3072]{1,0:T(8,128)(2,1)S(1)} %bitcast.74, bf16[3072,512]{1,0:T(8,128)(2,1)S(1)} %copy-done), kind=kOutput, calls=%fused_computation.7 | convolution fusion | flops 1610874880 | bytes 6815744 | tf_op jit(solution)/shard_map/dot_general | solution.py:53
  36.2 0.0 copy-done.3
  36.2 0.0 copy-start.4
  36.2 1.8 %convolution_convert_fusion.1 = bf16[512,512]{0,1:T(8,128)(2,1)S(1)} fusion(bf16[512,3072]{1,0:T(8,128)(2,1)S(1)} %bitcast.75, bf16[3072,512]{1,0:T(8,128)(2,1)S(1)} %copy-done.3), kind=kOutput, calls=%fused_computation.8 | convolution fusion | flops 1610874880 | bytes 6815744 | tf_op jit(solution)/shard_map/dot_general | solution.py:52
  38.0 0.0 copy-done.4
  38.1 1.8 %convolution_convert_fusion.2 = bf16[512,512]{0,1:T(8,128)(2,1)S(1)} fusion(bf16[512,3072]{1,0:T(8,128)(2,1)S(1)} %bitcast.76, bf16[3072,512]{1,0:T(8,128)(2,1)S(1)} %copy-done.4), kind=kOutput, calls=%fused_computation.9 | convolution fusion | flops 1610874880 | bytes 6815744 | tf_op jit(solution)/shard_map/dot_general | solution.py:49
  39.9 0.1 pad_maximum_fusion
  40.0 0.0 copy-start.1
  40.0 1.1 %copy-done.1 = bf16[512,1536]{0,1:T(8,128)(2,1)} copy-done((bf16[512,1536]{0,1:T(8,128)(2,1)}, bf16[512,1536]{0,1:T(8,128)(2,1)S(1)}, u32[]{:S(2)}) %copy-start.1) | copy-done | bytes 1572888
  41.2 0.3 fusion.4
  41.5 22.4 %all_to_all.22 = f32[32,16,128]{2,1,0:T(8,128)S(1)} all-to-all(f32[32,16,128]{2,1,0:T(8,128)S(1)} %bitcast.81), channel_id=1, replica_groups=mesh['ctx'=32,'y'=4,'core'=2] {'ctx'}, dimensions={0} | all-to-all | bytes 524288 | tf_op jit(solution)/shard_map/all_to_all | solution.py:22
  63.9 0.4 fusion.6
  64.2 0.9 copy.24
  65.1 4.6 %all-to-all-start.3 = ((f32[32,16,128]{2,1,0:T(8,128)}), f32[32,16,128]{2,1,0:T(8,128)S(1)}, u32[]{:S(2)}, u32[]{:S(2)}) async-start(f32[32,16,128]{2,1,0:T(8,128)} %copy.24), calls=%async_computation.3 | async-start | bytes 524288 | tf_op jit(solution)/shard_map/all_to_all | solution.py:29
  69.7 0.8 iota_compare_fusion
  70.5 3.8 %fusion.1 = f32[1,512,4,128]{1,3,2,0:T(8,128)} fusion(pred[512,512]{1,0:T(8,128)(4,1)} %iota_compare_fusion, bf16[1,512,3,4,128]{1,4,3,2,0:T(8,128)(2,1)} %bitcast.71), kind=kOutput, calls=%fused_computation.3 | convolution fusion | flops 538968064 | bytes 2883584 | tf_op jit(solution)/shard_map/bhqk,bkhe->bqhe/dot_general | solution.py:74
  74.3 0.0 copy-start.2
  74.3 6.1 %all-to-all-done.3 = f32[32,16,128]{2,1,0:T(8,128)S(1)} async-done(((f32[32,16,128]{2,1,0:T(8,128)}), f32[32,16,128]{2,1,0:T(8,128)S(1)}, u32[]{:S(2)}, u32[]{:S(2)}) %all-to-all-start.3) | async-done | bytes 262176 | tf_op jit(solution)/shard_map/all_to_all | solution.py:29
  80.4 1.4 %fusion.5 = f32[4,128,512]{2,1,0:T(8,128)S(1)} fusion(bf16[1,512,3,4,128]{1,4,3,2,0:T(8,128)(2,1)} %bitcast.72, bf16[1,4,128,128]{3,2,1,0:T(8,128)(2,1)S(1)} %convert_element_type.41), kind=kOutput, calls=%fused_computation.17 | convolution fusion | flops 67108864 | bytes 1703936 | tf_op jit(solution)/shard_map/bqhd,bhde->bqhe/dot_general | solution.py:78
  81.8 1.8 %multiply_reduce_fusion = (f32[512,4]{0,1:T(4,128)S(1)}, f32[1,512,4,128]{1,3,2,0:T(8,128)S(1)}) fusion(f32[1,512,4,128]{1,3,2,0:T(8,128)} %fusion.1, f32[4,128,512]{2,1,0:T(8,128)S(1)} %fusion.5, bf16[1,512,3,4,128]{1,4,3,2,0:T(8,128)(2,1)} %bitcast.73, f32[1,4,128,128]{3,2,1,0:T(8,128)S(1)} %bitcast.78, bf16[1,4,128,128]{3,2,1,0:T(8,128)(2,1)S(1)} %convert_element_type.41), kind=kOutput, calls=%fused_computation.11 | convolution fusion | flops 68352000 | bytes 4071424 | tf_op jit(solution)/shard_map/bqhd,bhde->bqhe/dot_general | solution.py:80
  83.6 0.0 copy-done.2
  83.6 0.9 %multiply_convert_fusion = bf16[1,512,4,128]{1,3,2,0:T(8,128)(2,1)} fusion(f32[1,512,4,128]{1,3,2,0:T(8,128)S(1)} %get-tuple-element.6, f32[4,128]{1,0:T(4,128)S(1)} %bitcast.82, f32[512,4]{0,1:T(4,128)S(1)} %add_rsqrt_fusion), kind=kLoop, calls=%fused_computation.10 | loop fusion | flops 786432 | bytes 1583104 | tf_op jit(solution)/shard_map/convert_element_type | solution.py:84
  84.5 2.0 %copy.27 = bf16[512,512]{1,0:T(8,128)(2,1)} copy(bf16[512,512]{0,1:T(8,128)(2,1)} %bitcast.79) | data formatting | bytes 1048576 | tf_op jit(solution)/shard_map/convert_element_type | solution.py:84
  (2 shorter events, 0.0 us)
Async XLA Ops:
  0.0 34.3 %copy-start = (bf16[3072,512]{1,0:T(8,128)(2,1)S(1)}, bf16[3072,512]{1,0:T(8,128)(2,1)}, u32[]{:S(2)}) copy-start(bf16[3072,512]{1,0:T(8,128)(2,1)} %param.8) | copy-start | bytes 9437188
  34.3 1.9 %copy-start.3 = (bf16[3072,512]{1,0:T(8,128)(2,1)S(1)}, bf16[3072,512]{1,0:T(8,128)(2,1)}, u32[]{:S(2)}) copy-start(bf16[3072,512]{1,0:T(8,128)(2,1)} %param.7) | copy-start | bytes 9437188
  36.2 1.9 %copy-start.4 = (bf16[3072,512]{1,0:T(8,128)(2,1)S(1)}, bf16[3072,512]{1,0:T(8,128)(2,1)}, u32[]{:S(2)}) copy-start(bf16[3072,512]{1,0:T(8,128)(2,1)} %param.6) | copy-start | bytes 9437188
  40.0 1.2 %copy-start.1 = (bf16[512,1536]{0,1:T(8,128)(2,1)}, bf16[512,1536]{0,1:T(8,128)(2,1)S(1)}, u32[]{:S(2)}) copy-start(bf16[512,1536]{0,1:T(8,128)(2,1)S(1)} %pad_maximum_fusion) | copy-start | bytes 4718596
  65.1 15.2 %all-to-all-start.3 = ((f32[32,16,128]{2,1,0:T(8,128)}), f32[32,16,128]{2,1,0:T(8,128)S(1)}, u32[]{:S(2)}, u32[]{:S(2)}) async-start(f32[32,16,128]{2,1,0:T(8,128)} %copy.24), calls=%async_computation.3 | async-start | bytes 524288 | tf_op jit(solution)/shard_map/all_to_all | solution.py:29
  74.3 9.3 %copy-start.2 = (f32[512]{0:T(512)S(1)}, f32[512]{0:T(512)}, u32[]{:S(2)}) copy-start(f32[512]{0:T(512)} %param.9) | copy-start | bytes 6148

commit v7 on v6

--- a/solution.py
+++ b/solution.py
@@ -18,15 +18,15 @@
 
 def exclusive_scan(value, axis):
     size = lax.axis_size(axis)
-    pieces = value.reshape(size, -1, value.shape[-1])
+    pieces = value.reshape(size, -1, value.shape[-1]).astype(jnp.bfloat16)
     gathered = lax.all_to_all(pieces, axis, 0, 0, tiled=True)
     earlier = jnp.arange(size)[:, None] > jnp.arange(size)[None, :]
     before = jnp.dot(
         earlier.astype(gathered.dtype),
         gathered.reshape(size, -1),
-        precision=lax.Precision.HIGHEST,
-    ).reshape(pieces.shape)
-    returned = lax.all_to_all(before, axis, 0, 0, tiled=True)
+        preferred_element_type=jnp.float32,
+    ).astype(jnp.bfloat16)
+    returned = lax.all_to_all(before.reshape(pieces.shape), axis, 0, 0, tiled=True)
     return returned.reshape(value.shape)
 
 
@@ -67,17 +67,15 @@
     prefix_state = exclusive_scan(local_state, "ctx")
     running = jnp.cumsum(block_states, axis=0)
     earlier = jnp.concatenate([jnp.zeros_like(block_states), running[:-1]], axis=0)
-    block_start = prefix_state[None] + earlier
+    block_start = (prefix_state.astype(jnp.float32)[None] + earlier).astype(jnp.bfloat16)
     scores = jnp.einsum("bqhd,bkhd->bhqk", query_rows, key_rows, preferred_element_type=jnp.float32)
     causal = jnp.arange(BLOCK)[:, None] >= jnp.arange(BLOCK)[None, :]
     scores = jnp.where(causal[None, None], scores, jnp.float32(0.0)).astype(jnp.bfloat16)
     inner = jnp.einsum("bhqk,bkhe->bqhe", scores, value_rows, preferred_element_type=jnp.float32)
     inner = lax.optimization_barrier(inner)
-    start_high = lax.optimization_barrier(block_start.astype(jnp.bfloat16))
-    start_low = (block_start - start_high.astype(jnp.float32)).astype(jnp.bfloat16)
     carried_part = jnp.einsum(
-        "bqhd,bhde->bqhe", query_rows, start_high, preferred_element_type=jnp.float32
-    ) + jnp.einsum("bqhd,bhde->bqhe", query_rows, start_low, preferred_element_type=jnp.float32)
+        "bqhd,bhde->bqhe", query_rows, block_start, preferred_element_type=jnp.float32
+    )
     mixed = inner + carried_part
     mean_square = jnp.mean(mixed * mixed, axis=-1, keepdims=True)
     normed = mixed * lax.rsqrt(mean_square + EPSILON) * norm_gain.reshape(head_count, HEAD_DIM)

time: 87.8 us -> 82.6 us (0.941)
  blocking collectives: 54.8 us -> 32.4 us
  starting transfers between devices: 4.59 us -> 14.9 us
  waiting for transfers between devices: 6.07 us -> 14.9 us
  matrix products: 13.1 us -> 12.1 us
    all_to_all x1 -> x0, blocking collectives: 22.4 us -> none  [exclusive_scan(): gathered = lax.all_to_all(pieces, axis, 0, 0, tiled=True)]
    all_to_all x1 -> x2, starting transfers between devices: 4.59 us -> 14.9 us  [the longest x1 11 us: exclusive_scan(): gathered = lax.all_to_all(pieces, axis, 0, 0, tiled=True)]
    all_to_all x1 -> x2, waiting for transfers between devices: 6.07 us -> 14.9 us  [the longest x1 9.26 us: exclusive_scan(): gathered = lax.all_to_all(pieces, axis, 0, 0, tiled=True)]
    dot_general x3 -> x2, matrix products: 3.52 us -> 1.91 us  [the longest x1 1.75 us: body(): jnp.einsum('bqhd,bhde->bqhe', query_rows, block_start, preferred_element_...]
    unnamed x10 -> x11, local copies, waits for them, and re-layouts: 1.22 us -> 1.89 us
  transfers between devices with their start and end apart: 1 -> 2, of which waited for: 1 -> 2; matrix products, arithmetic and copies ran while one was open for 5% -> 5% of each run, Pallas kernels for 0% -> 0%
where the time goes in v7:
time: 82.6 us; the launch traced here: 81.4 us
  blocking collectives  32.4 us (39%)
  starting transfers between devices  14.9 us (18%)
  waiting for transfers between devices  14.9 us (18%)
  matrix products  12.1 us (15%)
  local copies, waits for them, and re-layouts  5.82 us (7%)
  other arithmetic  1.14 us (1%)
    all_to_all x2, blocking collectives, spread(): return lax.all_to_all(copies, axis, 0, 0, tiled=True)  32.4 us
    all_to_all x1, starting transfers between devices, exclusive_scan(): gathered = lax.all_to_all(pieces, axis, 0, 0, tiled=True)  11 us
    all_to_all x1, waiting for transfers between devices, exclusive_scan(): gathered = lax.all_to_all(pieces, axis, 0, 0, tiled=True)  9.26 us
    all_to_all x1, waiting for transfers between devices, exclusive_scan(): lax.all_to_all(before.reshape(pieces.shape), axis, 0, 0, tiled=True)  5.61 us
    all_to_all x1, starting transfers between devices, exclusive_scan(): lax.all_to_all(before.reshape(pieces.shape), axis, 0, 0, tiled=True)  3.88 us
    dot_general x1, matrix products, body(): jnp.einsum('bhqk,bkhe->bqhe', scores, value_rows, preferred_element_type=...  3.73 us
    convert_element_type x1, local copies, waits for them, and re-layouts, body(): return normed.reshape(group_len, local_width).astype(jnp.bfloat16)  2.05 us
    unnamed x11, local copies, waits for them, and re-layouts  1.89 us
  transfers between devices with their start and end apart: 2, of which 2 were waited for; matrix products, arithmetic and copies ran while one was open for 5% of the time, Pallas kernels for 0%

profile of v7, /device:TPU:1, one launch (start us, length us, event | category | flops | bytes accessed | tf_op | source)
XLA Modules:
  0.0 81.4 jit_solution(17143215756382555337)
XLA Ops:
  0.0 0.0 copy-start
  0.0 1.3 %broadcast_in_dim.12 = bf16[4,64,3072]{2,1,0:T(8,128)(2,1)S(1)} broadcast(bf16[64,3072]{1,0:T(8,128)(2,1)} %param.5), dimensions={1,2} | broadcast | bytes 1966080 | tf_op jit(solution)/shard_map/broadcast_in_dim | solution.py:35
  1.3 24.7 %all_to_all.20 = bf16[4,64,3072]{2,1,0:T(8,128)(2,1)S(1)} all-to-all(bf16[4,64,3072]{2,1,0:T(8,128)(2,1)S(1)} %broadcast_in_dim.12), channel_id=1, replica_groups=mesh['ctx'=32,'y'=4,'core'=2] {'y'}, dimensions={0} | all-to-all | bytes 3145728 | tf_op jit(solution)/shard_map/all_to_all | solution.py:36
  26.0 0.4 broadcast_in_dim.13
  26.4 7.7 %all_to_all.21 = bf16[2,4,64,3072]{3,2,1,0:T(8,128)(2,1)S(1)} all-to-all(bf16[2,4,64,3072]{3,2,1,0:T(8,128)(2,1)S(1)} %broadcast_in_dim.13), channel_id=1, replica_groups=mesh['ctx'=32,'y'=4,'core'=2] {'core'}, dimensions={0} | all-to-all | bytes 6291456 | tf_op jit(solution)/shard_map/all_to_all | solution.py:36
  34.1 0.2 copy.13
  34.3 0.0 copy-done
  34.3 0.0 copy-start.3
  34.3 1.9 %convolution_convert_fusion.1 = bf16[512,512]{0,1:T(8,128)(2,1)S(1)} fusion(bf16[512,3072]{1,0:T(8,128)(2,1)S(1)} %bitcast.52, bf16[3072,512]{1,0:T(8,128)(2,1)S(1)} %copy-done), kind=kOutput, calls=%fused_computation.7 | convolution fusion | flops 1610874880 | bytes 6815744 | tf_op jit(solution)/shard_map/dot_general | solution.py:53
  36.2 0.0 copy-done.3
  36.2 0.0 copy-start.4
  36.2 1.8 %convolution_convert_fusion.2 = bf16[512,512]{0,1:T(8,128)(2,1)S(1)} fusion(bf16[512,3072]{1,0:T(8,128)(2,1)S(1)} %bitcast.53, bf16[3072,512]{1,0:T(8,128)(2,1)S(1)} %copy-done.3), kind=kOutput, calls=%fused_computation.8 | convolution fusion | flops 1610874880 | bytes 6815744 | tf_op jit(solution)/shard_map/dot_general | solution.py:52
  38.0 0.0 copy-done.4
  38.1 1.8 %convolution_convert_fusion.3 = bf16[512,512]{0,1:T(8,128)(2,1)S(1)} fusion(bf16[512,3072]{1,0:T(8,128)(2,1)S(1)} %bitcast.54, bf16[3072,512]{1,0:T(8,128)(2,1)S(1)} %copy-done.4), kind=kOutput, calls=%fused_computation.9 | convolution fusion | flops 1610874880 | bytes 6815744 | tf_op jit(solution)/shard_map/dot_general | solution.py:49
  39.9 0.1 pad_maximum_fusion
  40.0 0.0 copy-start.1
  40.0 1.1 %copy-done.1 = bf16[512,1536]{0,1:T(8,128)(2,1)} copy-done((bf16[512,1536]{0,1:T(8,128)(2,1)}, bf16[512,1536]{0,1:T(8,128)(2,1)S(1)}, u32[]{:S(2)}) %copy-start.1) | copy-done | bytes 1572888
  41.2 1.0 %convolution_convert_fusion.4 = bf16[4,128,128]{2,1,0:T(8,128)(2,1)} fusion(bf16[1,512,3,4,128]{1,4,3,2,0:T(8,128)(2,1)S(1)} %bitcast.55), kind=kOutput, calls=%fused_computation.10 | convolution fusion | flops 67174400 | bytes 1179648 | tf_op jit(solution)/shard_map/bshd,bshe->bhde/dot_general | solution.py:63
  42.1 11.0 %all-to-all-start.2 = ((bf16[32,16,128]{2,1,0:T(8,128)(2,1)}), bf16[32,16,128]{2,1,0:T(8,128)(2,1)S(1)}, u32[]{:S(2)}, u32[]{:S(2)}) async-start(bf16[32,16,128]{2,1,0:T(8,128)(2,1)} %bitcast.9), calls=%async_computation.2 | async-start | bytes 262144 | tf_op jit(solution)/shard_map/all_to_all | solution.py:22
  53.2 0.1 iota_compare_fusion
  53.2 9.3 %all-to-all-done.2 = bf16[32,16,128]{2,1,0:T(8,128)(2,1)S(1)} async-done(((bf16[32,16,128]{2,1,0:T(8,128)(2,1)}), bf16[32,16,128]{2,1,0:T(8,128)(2,1)S(1)}, u32[]{:S(2)}, u32[]{:S(2)}) %all-to-all-start.2) | async-done | bytes 131104 | tf_op jit(solution)/shard_map/all_to_all | solution.py:22
  62.5 0.2 fusion.3
  62.7 0.7 copy.26
  63.4 3.9 %all-to-all-start.3 = ((bf16[32,16,128]{2,1,0:T(8,128)(2,1)}), bf16[32,16,128]{2,1,0:T(8,128)(2,1)S(1)}, u32[]{:S(2)}, u32[]{:S(2)}) async-start(bf16[32,16,128]{2,1,0:T(8,128)(2,1)} %bitcast.24), calls=%async_computation.3 | async-start | bytes 262144 | tf_op jit(solution)/shard_map/all_to_all | solution.py:29
  67.2 0.0 copy-start.2
  67.3 3.7 %fusion.1 = f32[1,512,4,128]{1,3,2,0:T(8,128)} fusion(pred[512,512]{1,0:T(8,128)(4,1)S(1)} %iota_compare_fusion, bf16[1,512,3,4,128]{1,4,3,2,0:T(8,128)(2,1)} %bitcast.56), kind=kOutput, calls=%fused_computation.4 | convolution fusion | flops 538968064 | bytes 2883584 | tf_op jit(solution)/shard_map/bhqk,bkhe->bqhe/dot_general | solution.py:74
  71.0 5.6 %all-to-all-done.3 = bf16[32,16,128]{2,1,0:T(8,128)(2,1)S(1)} async-done(((bf16[32,16,128]{2,1,0:T(8,128)(2,1)}), bf16[32,16,128]{2,1,0:T(8,128)(2,1)S(1)}, u32[]{:S(2)}, u32[]{:S(2)}) %all-to-all-start.3) | async-done | bytes 131104 | tf_op jit(solution)/shard_map/all_to_all | solution.py:29
  76.6 1.7 %multiply_reduce_fusion = (f32[512,4]{0,1:T(4,128)S(1)}, f32[1,512,4,128]{1,3,2,0:T(8,128)S(1)}) fusion(f32[1,512,4,128]{1,3,2,0:T(8,128)} %fusion.1, bf16[4,128,128]{2,1,0:T(8,128)(2,1)S(1)} %bitcast.60, bf16[1,512,3,4,128]{1,4,3,2,0:T(8,128)(2,1)} %bitcast.57), kind=kOutput, calls=%fused_computation.13 | convolution fusion | flops 67893248 | bytes 2760704 | tf_op jit(solution)/shard_map/bqhd,bhde->bqhe/dot_general | solution.py:76
  78.4 0.0 copy-done.2
  78.4 0.9 %multiply_convert_fusion = bf16[1,512,4,128]{1,3,2,0:T(8,128)(2,1)} fusion(f32[1,512,4,128]{1,3,2,0:T(8,128)S(1)} %get-tuple-element.6, f32[4,128]{1,0:T(4,128)S(1)} %bitcast.61, f32[512,4]{0,1:T(4,128)S(1)} %add_rsqrt_fusion), kind=kLoop, calls=%fused_computation.12 | loop fusion | flops 786432 | bytes 1583104 | tf_op jit(solution)/shard_map/convert_element_type | solution.py:82
  79.3 2.0 %copy.19 = bf16[512,512]{1,0:T(8,128)(2,1)} copy(bf16[512,512]{0,1:T(8,128)(2,1)} %bitcast.58) | data formatting | bytes 1048576 | tf_op jit(solution)/shard_map/convert_element_type | solution.py:82
  (1 shorter events, 0.0 us)
Async XLA Ops:
  0.0 34.3 %copy-start = (bf16[3072,512]{1,0:T(8,128)(2,1)S(1)}, bf16[3072,512]{1,0:T(8,128)(2,1)}, u32[]{:S(2)}) copy-start(bf16[3072,512]{1,0:T(8,128)(2,1)} %param.8) | copy-start | bytes 9437188
  34.3 1.9 %copy-start.3 = (bf16[3072,512]{1,0:T(8,128)(2,1)S(1)}, bf16[3072,512]{1,0:T(8,128)(2,1)}, u32[]{:S(2)}) copy-start(bf16[3072,512]{1,0:T(8,128)(2,1)} %param.7) | copy-start | bytes 9437188
  36.2 1.9 %copy-start.4 = (bf16[3072,512]{1,0:T(8,128)(2,1)S(1)}, bf16[3072,512]{1,0:T(8,128)(2,1)}, u32[]{:S(2)}) copy-start(bf16[3072,512]{1,0:T(8,128)(2,1)} %param.6) | copy-start | bytes 9437188
  40.0 1.1 %copy-start.1 = (bf16[512,1536]{0,1:T(8,128)(2,1)}, bf16[512,1536]{0,1:T(8,128)(2,1)S(1)}, u32[]{:S(2)}) copy-start(bf16[512,1536]{0,1:T(8,128)(2,1)S(1)} %pad_maximum_fusion) | copy-start | bytes 4718596
  42.1 20.4 %all-to-all-start.2 = ((bf16[32,16,128]{2,1,0:T(8,128)(2,1)}), bf16[32,16,128]{2,1,0:T(8,128)(2,1)S(1)}, u32[]{:S(2)}, u32[]{:S(2)}) async-start(bf16[32,16,128]{2,1,0:T(8,128)(2,1)} %bitcast.9), calls=%async_computation.2 | async-start | bytes 262144 | tf_op jit(solution)/shard_map/all_to_all | solution.py:22
  63.4 13.2 %all-to-all-start.3 = ((bf16[32,16,128]{2,1,0:T(8,128)(2,1)}), bf16[32,16,128]{2,1,0:T(8,128)(2,1)S(1)}, u32[]{:S(2)}, u32[]{:S(2)}) async-start(bf16[32,16,128]{2,1,0:T(8,128)(2,1)} %bitcast.24), calls=%async_computation.3 | async-start | bytes 262144 | tf_op jit(solution)/shard_map/all_to_all | solution.py:29
  67.2 11.1 %copy-start.2 = (f32[512]{0:T(512)S(1)}, f32[512]{0:T(512)}, u32[]{:S(2)}) copy-start(f32[512]{0:T(512)} %param.9) | copy-start | bytes 6148

commit v8 on v7

--- a/solution.py
+++ b/solution.py
@@ -46,24 +46,22 @@
     local_width = w_query.shape[1]
     head_count = local_width // HEAD_DIM
     piece_rows = gather_rows(tokens)
-    query_part = jnp.dot(piece_rows, w_query, preferred_element_type=jnp.float32).astype(
-        jnp.bfloat16
-    )
-    key_part = jnp.dot(piece_rows, w_key, preferred_element_type=jnp.float32).astype(jnp.bfloat16)
-    value_part = jnp.dot(piece_rows, w_value, preferred_element_type=jnp.float32).astype(
-        jnp.bfloat16
-    )
-    projected = jnp.concatenate([query_part, key_part, value_part], axis=1)
-    group_len = projected.shape[0]
+    group_len = piece_rows.shape[0]
     block_count = group_len // BLOCK
-    shaped = projected.reshape(block_count, BLOCK, 3, head_count, HEAD_DIM)
-    query_rows = shaped[:, :, 0]
-    key_rows = shaped[:, :, 1]
-    value_rows = shaped[:, :, 2]
+
+    def project(weight):
+        part = jnp.dot(piece_rows_now, weight, preferred_element_type=jnp.float32)
+        return part.astype(jnp.bfloat16).reshape(block_count, BLOCK, head_count, HEAD_DIM)
+
+    piece_rows_now = piece_rows
+    key_rows = project(w_key)
+    value_rows = project(w_value)
     block_states = jnp.einsum(
         "bshd,bshe->bhde", key_rows, value_rows, preferred_element_type=jnp.float32
     )
     local_state = jnp.sum(block_states, axis=0)
+    piece_rows_now, local_state = lax.optimization_barrier((piece_rows, local_state))
+    query_rows = project(w_query)
     prefix_state = exclusive_scan(local_state, "ctx")
     running = jnp.cumsum(block_states, axis=0)
     earlier = jnp.concatenate([jnp.zeros_like(block_states), running[:-1]], axis=0)

time: 82.6 us -> 84.4 us (1.022)
  blocking collectives: 32.4 us -> 9.16 us
  waiting for transfers between devices: 14.9 us -> 28 us
  starting transfers between devices: 14.9 us -> 21.4 us
  matrix products: 12.1 us -> 15.8 us
  local copies, waits for them, and re-layouts: 5.82 us -> 8.36 us
    all_to_all x2 -> x1, blocking collectives: 32.4 us -> 9.16 us  [spread(): return lax.all_to_all(copies, axis, 0, 0, tiled=True)]
    all_to_all x0 -> x1, waiting for transfers between devices: none -> 18.5 us  [spread(): return lax.all_to_all(copies, axis, 0, 0, tiled=True)]
    all_to_all x1, waiting for transfers between devices: 9.26 us -> 3.86 us  [exclusive_scan(): gathered = lax.all_to_all(pieces, axis, 0, 0, tiled=True)]
    all_to_all x0 -> x1, starting transfers between devices: none -> 5 us  [spread(): return lax.all_to_all(copies, axis, 0, 0, tiled=True)]
    dot_general x3, matrix products: 5.52 us -> 9.18 us  [project(): part = jnp.dot(piece_rows_now, weight, preferred_element_type=jnp.float32)]
    broadcast_in_dim x2, local copies, waits for them, and re-layouts: 1.69 us -> 4.27 us  [spread(): copies = jnp.broadcast_to(value[None], (size,) + value.shape)]
    all_to_all x1, starting transfers between devices: 3.88 us -> 5.36 us  [exclusive_scan(): lax.all_to_all(before.reshape(pieces.shape), axis, 0, 0, tiled=True)]
    unnamed x11 -> x13, local copies, waits for them, and re-layouts: 1.89 us -> 1.84 us
  transfers between devices with their start and end apart: 2 -> 3, of which waited for: 2 -> 3; matrix products, arithmetic and copies ran while one was open for 5% -> 11% of each run, Pallas kernels for 0% -> 0%
where the time goes in v8:
time: 84.4 us; the launch traced here: 83.9 us
  waiting for transfers between devices  28 us (33%)
  starting transfers between devices  21.4 us (25%)
  matrix products  15.8 us (19%)
  blocking collectives  9.16 us (11%)
  local copies, waits for them, and re-layouts  8.36 us (10%)
  other arithmetic  1.04 us (1%)
    all_to_all x1, waiting for transfers between devices, spread(): return lax.all_to_all(copies, axis, 0, 0, tiled=True)  18.5 us
    all_to_all x1, starting transfers between devices, exclusive_scan(): gathered = lax.all_to_all(pieces, axis, 0, 0, tiled=True)  11.1 us
    dot_general x3, matrix products, project(): part = jnp.dot(piece_rows_now, weight, preferred_element_type=jnp.float32)  9.18 us
    all_to_all x1, blocking collectives, spread(): return lax.all_to_all(copies, axis, 0, 0, tiled=True)  9.16 us
    all_to_all x1, waiting for transfers between devices, exclusive_scan(): lax.all_to_all(before.reshape(pieces.shape), axis, 0, 0, tiled=True)  5.61 us
    all_to_all x1, starting transfers between devices, exclusive_scan(): lax.all_to_all(before.reshape(pieces.shape), axis, 0, 0, tiled=True)  5.36 us
    all_to_all x1, starting transfers between devices, spread(): return lax.all_to_all(copies, axis, 0, 0, tiled=True)  5 us
    broadcast_in_dim x2, local copies, waits for them, and re-layouts, spread(): copies = jnp.broadcast_to(value[None], (size,) + value.shape)  4.27 us
  transfers between devices with their start and end apart: 3, of which 3 were waited for; matrix products, arithmetic and copies ran while one was open for 11% of the time, Pallas kernels for 0%

profile of v8, /device:TPU:1, one launch (start us, length us, event | category | flops | bytes accessed | tf_op | source)
XLA Modules:
  0.0 83.9 jit_solution(11634793591808810816)
XLA Ops:
  0.0 0.0 copy-start
  0.0 2.5 %broadcast_in_dim.12 = bf16[4,64,3072]{2,1,0:T(8,128)(2,1)} broadcast(bf16[64,3072]{1,0:T(8,128)(2,1)} %param.5), dimensions={1,2} | broadcast | bytes 1966080 | tf_op jit(solution)/shard_map/broadcast_in_dim | solution.py:35
  2.5 5.0 %all-to-all-start = ((bf16[4,64,3072]{2,1,0:T(8,128)(2,1)}), bf16[4,64,3072]{2,1,0:T(8,128)(2,1)}, u32[]{:S(2)}, u32[]{:S(2)}) async-start(bf16[4,64,3072]{2,1,0:T(8,128)(2,1)} %broadcast_in_dim.12), calls=%async_computation | async-start | bytes 3145728 | tf_op jit(solution)/shard_map/all_to_all | solution.py:36
  7.5 0.1 iota_compare_fusion
  7.6 18.5 %all-to-all-done = bf16[4,64,3072]{2,1,0:T(8,128)(2,1)} async-done(((bf16[4,64,3072]{2,1,0:T(8,128)(2,1)}), bf16[4,64,3072]{2,1,0:T(8,128)(2,1)}, u32[]{:S(2)}, u32[]{:S(2)}) %all-to-all-start) | async-done | bytes 1572896 | tf_op jit(solution)/shard_map/all_to_all | solution.py:36
  26.1 1.8 %broadcast_in_dim.13 = bf16[2,4,64,3072]{3,2,1,0:T(8,128)(2,1)S(1)} broadcast(bf16[4,64,3072]{2,1,0:T(8,128)(2,1)} %all-to-all-done), dimensions={1,2,3} | broadcast | bytes 4718592 | tf_op jit(solution)/shard_map/broadcast_in_dim | solution.py:35
  27.9 9.2 %all_to_all.20 = bf16[2,4,64,3072]{3,2,1,0:T(8,128)(2,1)S(1)} all-to-all(bf16[2,4,64,3072]{3,2,1,0:T(8,128)(2,1)S(1)} %broadcast_in_dim.13), channel_id=1, replica_groups=mesh['ctx'=32,'y'=4,'core'=2] {'core'}, dimensions={0} | all-to-all | bytes 6291456 | tf_op jit(solution)/shard_map/all_to_all | solution.py:36
  37.0 0.2 copy.13
  37.2 0.0 copy-start.1
  37.2 0.0 copy-done
  37.3 0.0 copy-start.5
  37.3 1.9 %convolution_convert_fusion.3 = bf16[512,512]{0,1:T(8,128)(2,1)S(1)} fusion(bf16[512,3072]{1,0:T(8,128)(2,1)S(1)} %bitcast.40, bf16[3072,512]{1,0:T(8,128)(2,1)S(1)} %copy-done), kind=kOutput, calls=%fused_computation.8 | convolution fusion | flops 1610874880 | bytes 6815744 | tf_op jit(solution)/shard_map/dot_general | solution.py:53
  39.1 0.0 copy-done.1
  39.1 1.1 %copy-done.5 = bf16[3072,512]{1,0:T(8,128)(2,1)S(1)} copy-done((bf16[3072,512]{1,0:T(8,128)(2,1)S(1)}, bf16[3072,512]{1,0:T(8,128)(2,1)}, u32[]{:S(2)}) %copy-start.5) | copy-done | bytes 3145752
  40.3 0.0 copy-start.2
  40.3 1.8 %convolution_convert_fusion.2 = bf16[512,512]{0,1:T(8,128)(2,1)S(1)} fusion(bf16[512,3072]{1,0:T(8,128)(2,1)S(1)} %bitcast.41, bf16[3072,512]{1,0:T(8,128)(2,1)S(1)} %copy-done.5), kind=kOutput, calls=%fused_computation.7 | convolution fusion | flops 1610874880 | bytes 6815744 | tf_op jit(solution)/shard_map/dot_general | solution.py:53
  42.1 0.0 copy-start.3
  42.1 0.0 copy-done.2
  42.1 0.9 %fusion.7 = bf16[4,128,128]{2,1,0:T(8,128)(2,1)} fusion(bf16[512,4,128]{0,2,1:T(8,128)(2,1)S(1)} %bitcast.46, bf16[512,4,128]{0,2,1:T(8,128)(2,1)S(1)} %bitcast.44), kind=kOutput, calls=%fused_computation.18 | convolution fusion | flops 67108864 | bytes 1179648 | tf_op jit(solution)/shard_map/bshd,bshe->bhde/dot_general | solution.py:59
  43.1 0.0 copy-done.3
  43.1 11.1 %all-to-all-start.2 = ((bf16[32,16,128]{2,1,0:T(8,128)(2,1)}), bf16[32,16,128]{2,1,0:T(8,128)(2,1)S(1)}, u32[]{:S(2)}, u32[]{:S(2)}) async-start(bf16[32,16,128]{2,1,0:T(8,128)(2,1)} %bitcast.8), calls=%async_computation.2 | async-start | bytes 262144 | tf_op jit(solution)/shard_map/all_to_all | solution.py:22
  54.2 5.5 %convolution_convert_fusion.1 = bf16[512,512]{0,1:T(8,128)(2,1)} fusion(bf16[512,3072]{1,0:T(8,128)(2,1)} %bitcast.42, bf16[3072,512]{1,0:T(8,128)(2,1)} %param.6), kind=kOutput, calls=%fused_computation.6 | convolution fusion | flops 1610874880 | bytes 6815744 | tf_op jit(solution)/shard_map/dot_general | solution.py:53
  59.7 3.9 %all-to-all-done.2 = bf16[32,16,128]{2,1,0:T(8,128)(2,1)S(1)} async-done(((bf16[32,16,128]{2,1,0:T(8,128)(2,1)}), bf16[32,16,128]{2,1,0:T(8,128)(2,1)S(1)}, u32[]{:S(2)}, u32[]{:S(2)}) %all-to-all-start.2) | async-done | bytes 131104 | tf_op jit(solution)/shard_map/all_to_all | solution.py:22
  63.5 0.2 fusion.3
  63.7 0.7 copy.26
  64.4 5.4 %all-to-all-start.3 = ((bf16[32,16,128]{2,1,0:T(8,128)(2,1)}), bf16[32,16,128]{2,1,0:T(8,128)(2,1)S(1)}, u32[]{:S(2)}, u32[]{:S(2)}) async-start(bf16[32,16,128]{2,1,0:T(8,128)(2,1)} %bitcast.19), calls=%async_computation.3 | async-start | bytes 262144 | tf_op jit(solution)/shard_map/all_to_all | solution.py:29
  69.7 0.0 copy-start.4
  69.7 3.7 %fusion.1 = f32[1,512,4,128]{1,3,2,0:T(8,128)} fusion(bf16[512,4,128]{0,2,1:T(8,128)(2,1)} %bitcast.45, bf16[512,4,128]{0,2,1:T(8,128)(2,1)} %bitcast.49, bf16[512,4,128]{0,2,1:T(8,128)(2,1)} %bitcast.47, pred[512,512]{1,0:T(8,128)(4,1)S(1)} %iota_compare_fusion), kind=kOutput, calls=%fused_computation.3 | convolution fusion | flops 538968064 | bytes 2883584 | tf_op jit(solution)/shard_map/bhqk,bkhe->bqhe/dot_general | solution.py:72
  73.5 5.6 %all-to-all-done.3 = bf16[32,16,128]{2,1,0:T(8,128)(2,1)S(1)} async-done(((bf16[32,16,128]{2,1,0:T(8,128)(2,1)}), bf16[32,16,128]{2,1,0:T(8,128)(2,1)S(1)}, u32[]{:S(2)}, u32[]{:S(2)}) %all-to-all-start.3) | async-done | bytes 131104 | tf_op jit(solution)/shard_map/all_to_all | solution.py:29
  79.1 1.7 %multiply_reduce_fusion = (f32[512,4]{0,1:T(4,128)S(1)}, f32[1,512,4,128]{1,3,2,0:T(8,128)S(1)}) fusion(f32[1,512,4,128]{1,3,2,0:T(8,128)} %fusion.1, bf16[4,128,128]{2,1,0:T(8,128)(2,1)S(1)} %bitcast.51, bf16[512,4,128]{0,2,1:T(8,128)(2,1)} %bitcast.50), kind=kOutput, calls=%fused_computation.11 | convolution fusion | flops 67893248 | bytes 2760704 | tf_op jit(solution)/shard_map/bqhd,bhde->bqhe/dot_general | solution.py:74
  80.8 0.0 copy-done.4
  80.9 1.0 %multiply_convert_fusion = bf16[1,512,4,128]{1,3,2,0:T(8,128)(2,1)} fusion(f32[1,512,4,128]{1,3,2,0:T(8,128)S(1)} %get-tuple-element.10, f32[4,128]{1,0:T(4,128)S(1)} %bitcast.52, f32[512,4]{0,1:T(4,128)S(1)} %add_rsqrt_fusion), kind=kLoop, calls=%fused_computation.10 | loop fusion | flops 786432 | bytes 1583104 | tf_op jit(solution)/shard_map/convert_element_type | solution.py:80
  81.8 2.0 %copy.19 = bf16[512,512]{1,0:T(8,128)(2,1)} copy(bf16[512,512]{0,1:T(8,128)(2,1)} %bitcast.43) | data formatting | bytes 1048576 | tf_op jit(solution)/shard_map/convert_element_type | solution.py:80
  (1 shorter events, 0.0 us)
Async XLA Ops:
  0.0 37.2 %copy-start = (bf16[3072,512]{1,0:T(8,128)(2,1)S(1)}, bf16[3072,512]{1,0:T(8,128)(2,1)}, u32[]{:S(2)}) copy-start(bf16[3072,512]{1,0:T(8,128)(2,1)} %param.8) | copy-start | bytes 9437188
  2.5 23.6 %all-to-all-start = ((bf16[4,64,3072]{2,1,0:T(8,128)(2,1)}), bf16[4,64,3072]{2,1,0:T(8,128)(2,1)}, u32[]{:S(2)}, u32[]{:S(2)}) async-start(bf16[4,64,3072]{2,1,0:T(8,128)(2,1)} %broadcast_in_dim.12), calls=%async_computation | async-start | bytes 3145728 | tf_op jit(solution)/shard_map/all_to_all | solution.py:36
  37.2 1.9 %copy-start.1 = (bf16[2,4,64,3072]{3,2,0,1:T(8,128)(2,1)}, bf16[2,4,64,3072]{3,2,0,1:T(8,128)(2,1)S(1)}, u32[]{:S(2)}) copy-start(bf16[2,4,64,3072]{3,2,0,1:T(8,128)(2,1)S(1)} %copy.13) | copy-start | bytes 9437188
  37.3 3.0 %copy-start.5 = (bf16[3072,512]{1,0:T(8,128)(2,1)S(1)}, bf16[3072,512]{1,0:T(8,128)(2,1)}, u32[]{:S(2)}) copy-start(bf16[3072,512]{1,0:T(8,128)(2,1)} %param.7) | copy-start | bytes 9437188
  40.3 1.9 %copy-start.2 = (bf16[512,512]{0,1:T(8,128)(2,1)}, bf16[512,512]{0,1:T(8,128)(2,1)S(1)}, u32[]{:S(2)}) copy-start(bf16[512,512]{0,1:T(8,128)(2,1)S(1)} %convolution_convert_fusion.3) | copy-start | bytes 1572868
  42.1 1.0 %copy-start.3 = (bf16[512,512]{0,1:T(8,128)(2,1)}, bf16[512,512]{0,1:T(8,128)(2,1)S(1)}, u32[]{:S(2)}) copy-start(bf16[512,512]{0,1:T(8,128)(2,1)S(1)} %convolution_convert_fusion.2) | copy-start | bytes 1572868
  43.1 20.4 %all-to-all-start.2 = ((bf16[32,16,128]{2,1,0:T(8,128)(2,1)}), bf16[32,16,128]{2,1,0:T(8,128)(2,1)S(1)}, u32[]{:S(2)}, u32[]{:S(2)}) async-start(bf16[32,16,128]{2,1,0:T(8,128)(2,1)} %bitcast.8), calls=%async_computation.2 | async-start | bytes 262144 | tf_op jit(solution)/shard_map/all_to_all | solution.py:22
  64.4 14.7 %all-to-all-start.3 = ((bf16[32,16,128]{2,1,0:T(8,128)(2,1)}), bf16[32,16,128]{2,1,0:T(8,128)(2,1)S(1)}, u32[]{:S(2)}, u32[]{:S(2)}) async-start(bf16[32,16,128]{2,1,0:T(8,128)(2,1)} %bitcast.19), calls=%async_computation.3 | async-start | bytes 262144 | tf_op jit(solution)/shard_map/all_to_all | solution.py:29
  69.7 11.1 %copy-start.4 = (f32[512]{0:T(512)S(1)}, f32[512]{0:T(512)}, u32[]{:S(2)}) copy-start(f32[512]{0:T(512)} %param.9) | copy-start | bytes 6148

commit v9 on v7

--- a/solution.py
+++ b/solution.py
@@ -30,16 +30,19 @@
     return returned.reshape(value.shape)
 
 
-def spread(value, axis):
-    size = lax.axis_size(axis)
-    copies = jnp.broadcast_to(value[None], (size,) + value.shape)
-    return lax.all_to_all(copies, axis, 0, 0, tiled=True)
-
-
 def gather_rows(tokens):
-    near = spread(tokens, "y")
-    both = spread(near, "core")
-    return both.transpose(1, 0, 2, 3).reshape(-1, tokens.shape[1])
+    chips = lax.axis_size("y")
+    chip = lax.axis_index("y")
+    ahead = [tokens] + [
+        lax.ppermute(tokens, "y", [(i, (i - by) % chips) for i in range(chips)])
+        for by in range(1, chips)
+    ]
+    twice = jnp.stack(ahead + ahead)
+    near = lax.dynamic_slice_in_dim(twice, (chips - chip) % chips, chips, axis=0)
+    other = lax.ppermute(near, "core", [(0, 1), (1, 0)])
+    trio = jnp.stack([near, other, near], axis=1)
+    both = lax.dynamic_slice_in_dim(trio, lax.axis_index("core"), 2, axis=1)
+    return both.reshape(-1, tokens.shape[1])
 
 
 def body(tokens, w_query, w_key, w_value, norm_gain):

time: 82.6 us -> 87.6 us (1.061)
  blocking collectives: 32.4 us -> 0 us
  waiting for transfers between devices: 14.9 us -> 33.8 us
  local copies, waits for them, and re-layouts: 5.82 us -> 15.6 us
  starting transfers between devices: 14.9 us -> 20 us
  other arithmetic: 1.14 us -> 4.24 us
    all_to_all x2 -> x0, blocking collectives: 32.4 us -> none  [spread(): return lax.all_to_all(copies, axis, 0, 0, tiled=True)]
    ppermute x0 -> x4, waiting for transfers between devices: none -> 19 us  [the longest x3 17.1 us: gather_rows(): lax.ppermute(tokens, 'y', [(i, (i - by) % chips) for i in range(chips)])]
    unnamed x11 -> x22, local copies, waits for them, and re-layouts: 1.89 us -> 9.73 us
    ppermute x0 -> x4, starting transfers between devices: none -> 5.09 us  [the longest x3 4.59 us: gather_rows(): lax.ppermute(tokens, 'y', [(i, (i - by) % chips) for i in range(chips)])]
    another operation x0 -> x1, other arithmetic: none -> 3.09 us  [gather_rows(): trio = jnp.stack([near, other, near], axis=1)]
    another operation x0 -> x2, local copies, waits for them, and re-layouts: none -> 2.53 us  [the longest x1 1.51 us: gather_rows(): trio = jnp.stack([near, other, near], axis=1)]
    broadcast_in_dim x2 -> x0, local copies, waits for them, and re-layouts: 1.69 us -> none  [spread(): copies = jnp.broadcast_to(value[None], (size,) + value.shape)]
    dynamic_slice x0 -> x1, local copies, waits for them, and re-layouts: none -> 1.26 us  [gather_rows(): lax.dynamic_slice_in_dim(twice, (chips - chip) % chips, chips, axis=0)]
  transfers between devices with their start and end apart: 2 -> 6, of which waited for: 2 -> 5; matrix products, arithmetic and copies ran while one was open for 5% -> 10% of each run, Pallas kernels for 0% -> 0%
where the time goes in v9:
time: 87.6 us; the launch traced here: 85.9 us
  waiting for transfers between devices  33.8 us (39%)
  starting transfers between devices  20 us (23%)
  local copies, waits for them, and re-layouts  15.6 us (18%)
  matrix products  12.1 us (14%)
  other arithmetic  4.24 us (5%)
    ppermute x3, waiting for transfers between devices, gather_rows(): lax.ppermute(tokens, 'y', [(i, (i - by) % chips) for i in range(chips)])  17.1 us
    all_to_all x1, starting transfers between devices, exclusive_scan(): gathered = lax.all_to_all(pieces, axis, 0, 0, tiled=True)  11 us
    unnamed x22, local copies, waits for them, and re-layouts  9.73 us
    all_to_all x1, waiting for transfers between devices, exclusive_scan(): gathered = lax.all_to_all(pieces, axis, 0, 0, tiled=True)  9.26 us
    all_to_all x1, waiting for transfers between devices, exclusive_scan(): lax.all_to_all(before.reshape(pieces.shape), axis, 0, 0, tiled=True)  5.59 us
    ppermute x3, starting transfers between devices, gather_rows(): lax.ppermute(tokens, 'y', [(i, (i - by) % chips) for i in range(chips)])  4.59 us
    all_to_all x1, starting transfers between devices, exclusive_scan(): lax.all_to_all(before.reshape(pieces.shape), axis, 0, 0, tiled=True)  3.86 us
    dot_general x1, matrix products, body(): jnp.einsum('bhqk,bkhe->bqhe', scores, value_rows, preferred_element_type=...  3.73 us
  transfers between devices with their start and end apart: 6, of which 5 were waited for; matrix products, arithmetic and copies ran while one was open for 10% of the time, Pallas kernels for 0%

profile of v9, /device:TPU:1, one launch (start us, length us, event | category | flops | bytes accessed | tf_op | source)
XLA Modules:
  0.0 85.9 jit_solution(414125446134604543)
XLA Ops:
  0.0 0.0 copy-start
  0.0 0.0 copy-start.3
  0.0 3.6 %collective-permute-start = (bf16[64,3072]{1,0:T(8,128)(2,1)}, bf16[64,3072]{1,0:T(8,128)(2,1)}, u32[]{:S(2)}, u32[]{:S(2)}) collective-permute-start(bf16[64,3072]{1,0:T(8,128)(2,1)} %param.5), channel_id=1, source_target_pairs={{0,6},{2,0},{4,2},{6,4},{1,7},{3,1},{5,3},{7,5},{8,14},{10,8},{12,... | collective-permute-start | bytes 1179656 | tf_op jit(solution)/shard_map/ppermute | solution.py:37
  3.6 0.3 collective-permute-start.1
  3.9 0.7 collective-permute-start.2
  4.6 1.1 %bitcast_dynamic-update-slice_fusion.6 = bf16[8,64,3072]{2,1,0:T(8,128)(2,1)S(1)} fusion(bf16[64,3072]{1,0:T(8,128)(2,1)} %param.5), kind=kLoop, calls=%fused_computation.29 | loop fusion | bytes 786432
  5.7 14.3 %collective-permute-done = bf16[64,3072]{1,0:T(8,128)(2,1)} collective-permute-done((bf16[64,3072]{1,0:T(8,128)(2,1)}, bf16[64,3072]{1,0:T(8,128)(2,1)}, u32[]{:S(2)}, u32[]{:S(2)}) %collective-permute-start) | collective-permute-done | bytes 393248 | tf_op jit(solution)/shard_map/ppermute | solution.py:37
  20.0 1.0 %bitcast_dynamic-update-slice_fusion.4 = bf16[8,64,3072]{2,1,0:T(8,128)(2,1)S(1)} fusion(bf16[8,64,3072]{2,1,0:T(8,128)(2,1)S(1)} %bitcast_dynamic-update-slice_fusion.6, bf16[64,3072]{1,0:T(8,128)(2,1)} %collective-permute-done), kind=kLoop, calls=%fused_computation.27 | loop fusion | bytes 786432
  21.0 0.0 collective-permute-done.1
  21.0 1.0 %bitcast_dynamic-update-slice_fusion.2 = bf16[8,64,3072]{2,1,0:T(8,128)(2,1)S(1)} fusion(bf16[8,64,3072]{2,1,0:T(8,128)(2,1)S(1)} %bitcast_dynamic-update-slice_fusion.4, bf16[64,3072]{1,0:T(8,128)(2,1)} %collective-permute-done.1), kind=kLoop, calls=%fused_computation.25 | loop fusion | bytes 786432
  22.0 2.8 %collective-permute-done.2 = bf16[64,3072]{1,0:T(8,128)(2,1)} collective-permute-done((bf16[64,3072]{1,0:T(8,128)(2,1)}, bf16[64,3072]{1,0:T(8,128)(2,1)}, u32[]{:S(2)}, u32[]{:S(2)}) %collective-permute-start.2) | collective-permute-done | bytes 393248 | tf_op jit(solution)/shard_map/ppermute | solution.py:37
  24.8 1.0 %bitcast_dynamic-update-slice_fusion = bf16[8,64,3072]{2,1,0:T(8,128)(2,1)S(1)} fusion(bf16[8,64,3072]{2,1,0:T(8,128)(2,1)S(1)} %bitcast_dynamic-update-slice_fusion.2, bf16[64,3072]{1,0:T(8,128)(2,1)} %collective-permute-done.2), kind=kLoop, calls=%fused_computation.23 | loop fusion | bytes 786432
  25.9 0.0 copy-done.3
  25.9 1.0 %bitcast_dynamic-update-slice_fusion.5 = bf16[8,64,3072]{2,1,0:T(8,128)(2,1)S(1)} fusion(bf16[8,64,3072]{2,1,0:T(8,128)(2,1)S(1)} %bitcast_dynamic-update-slice_fusion.7, bf16[64,3072]{1,0:T(8,128)(2,1)} %collective-permute-done), kind=kLoop, calls=%fused_computation.28 | loop fusion | bytes 786432
  26.9 1.0 %bitcast_dynamic-update-slice_fusion.3 = bf16[8,64,3072]{2,1,0:T(8,128)(2,1)S(1)} fusion(bf16[8,64,3072]{2,1,0:T(8,128)(2,1)S(1)} %bitcast_dynamic-update-slice_fusion.5, bf16[64,3072]{1,0:T(8,128)(2,1)} %collective-permute-done.1), kind=kLoop, calls=%fused_computation.26 | loop fusion | bytes 786432
  28.0 1.0 %bitcast_dynamic-update-slice_fusion.1 = bf16[8,64,3072]{2,1,0:T(8,128)(2,1)S(1)} fusion(bf16[8,64,3072]{2,1,0:T(8,128)(2,1)S(1)} %bitcast_dynamic-update-slice_fusion.3, bf16[64,3072]{1,0:T(8,128)(2,1)} %collective-permute-done.2), kind=kLoop, calls=%fused_computation.24 | loop fusion | bytes 786432 | tf_op jit(solution)/shard_map/stack | solution.py:40
  29.0 0.0 copy-start.1
  29.0 1.6 %copy-done.1 = bf16[8,64,3072]{2,1,0:T(8,128)(2,1)} copy-done((bf16[8,64,3072]{2,1,0:T(8,128)(2,1)}, bf16[8,64,3072]{2,1,0:T(8,128)(2,1)S(1)}, u32[]{:S(2)}) %copy-start.1) | copy-done | bytes 3145752
  30.6 1.3 %constant_dynamic-slice_fusion = bf16[4,64,3072]{2,1,0:T(8,128)(2,1)} fusion(bf16[8,64,3072]{2,1,0:T(8,128)(2,1)S(1)} %bitcast_dynamic-update-slice_fusion.1, s32[]{:T(128)S(6)} %select_n.19), kind=kLoop, calls=%fused_computation.35 | loop fusion | bytes 3145732 | tf_op jit(solution)/shard_map/dynamic_slice | solution.py:41
  31.9 0.5 collective-permute-start.3
  32.4 1.5 %fusion.16 = bf16[4,1,64,3072]{3,2,1,0:T(8,128)(2,1)S(1)} fusion(bf16[8,64,3072]{2,1,0:T(8,128)(2,1)} %copy-done.1, s32[]{:T(128)S(6)} %select_n.19), kind=kLoop, calls=%fused_computation.37 | loop fusion | bytes 3145732 | tf_op jit(solution)/shard_map/stack | solution.py:43
  33.9 1.9 %collective-permute-done.3 = bf16[4,64,3072]{2,1,0:T(8,128)(2,1)} collective-permute-done((bf16[4,64,3072]{2,1,0:T(8,128)(2,1)}, bf16[4,64,3072]{2,1,0:T(8,128)(2,1)}, u32[]{:S(2)}, u32[]{:S(2)}) %collective-permute-start.3) | collective-permute-done | bytes 1572896 | tf_op jit(solution)/shard_map/ppermute | solution.py:42
  35.8 3.1 %fusion.1 = bf16[4,2,64,3072]{3,2,1,0:T(8,128)(2,1)S(1)} fusion(s32[]{:T(128)S(6)} %select_n.20, bf16[4,1,64,3072]{3,2,1,0:T(8,128)(2,1)S(1)} %fusion.16, bf16[4,1,64,3072]{3,2,1,0:T(8,128)(2,1)} %bitcast.5), kind=kLoop, calls=%fused_computation.5 | loop fusion | flops 3145728 | bytes 6291460 | tf_op jit(solution)/shard_map/stack | solution.py:43
  38.9 0.0 copy-done
  38.9 0.0 copy-start.5
  38.9 1.9 %convolution_convert_fusion.1 = bf16[512,512]{0,1:T(8,128)(2,1)S(1)} fusion(bf16[512,3072]{1,0:T(8,128)(2,1)S(1)} %bitcast.61, bf16[3072,512]{1,0:T(8,128)(2,1)S(1)} %copy-done), kind=kOutput, calls=%fused_computation.12 | convolution fusion | flops 1610874880 | bytes 6815744 | tf_op jit(solution)/shard_map/dot_general | solution.py:56
  40.7 0.0 copy-done.5
  40.8 0.0 copy-start.6
  40.8 1.8 %convolution_convert_fusion.2 = bf16[512,512]{0,1:T(8,128)(2,1)S(1)} fusion(bf16[512,3072]{1,0:T(8,128)(2,1)S(1)} %bitcast.62, bf16[3072,512]{1,0:T(8,128)(2,1)S(1)} %copy-done.5), kind=kOutput, calls=%fused_computation.13 | convolution fusion | flops 1610874880 | bytes 6815744 | tf_op jit(solution)/shard_map/dot_general | solution.py:55
  42.6 0.0 copy-done.6
  42.6 1.8 %convolution_convert_fusion.3 = bf16[512,512]{0,1:T(8,128)(2,1)S(1)} fusion(bf16[512,3072]{1,0:T(8,128)(2,1)S(1)} %bitcast.63, bf16[3072,512]{1,0:T(8,128)(2,1)S(1)} %copy-done.6), kind=kOutput, calls=%fused_computation.14 | convolution fusion | flops 1610874880 | bytes 6815744 | tf_op jit(solution)/shard_map/dot_general | solution.py:52
  44.5 0.1 pad_maximum_fusion
  44.6 0.0 copy-start.2
  44.6 1.2 %copy-done.2 = bf16[512,1536]{0,1:T(8,128)(2,1)} copy-done((bf16[512,1536]{0,1:T(8,128)(2,1)}, bf16[512,1536]{0,1:T(8,128)(2,1)S(1)}, u32[]{:S(2)}) %copy-start.2) | copy-done | bytes 1572888
  45.8 1.0 %convolution_convert_fusion.4 = bf16[4,128,128]{2,1,0:T(8,128)(2,1)} fusion(bf16[1,512,3,4,128]{1,4,3,2,0:T(8,128)(2,1)S(1)} %bitcast.64), kind=kOutput, calls=%fused_computation.15 | convolution fusion | flops 67174400 | bytes 1179648 | tf_op jit(solution)/shard_map/bshd,bshe->bhde/dot_general | solution.py:66
  46.7 11.0 %all-to-all-start = ((bf16[32,16,128]{2,1,0:T(8,128)(2,1)}), bf16[32,16,128]{2,1,0:T(8,128)(2,1)S(1)}, u32[]{:S(2)}, u32[]{:S(2)}) async-start(bf16[32,16,128]{2,1,0:T(8,128)(2,1)} %bitcast.13), calls=%async_computation | async-start | bytes 262144 | tf_op jit(solution)/shard_map/all_to_all | solution.py:22
  57.8 0.1 iota_compare_fusion
  57.8 9.3 %all-to-all-done = bf16[32,16,128]{2,1,0:T(8,128)(2,1)S(1)} async-done(((bf16[32,16,128]{2,1,0:T(8,128)(2,1)}), bf16[32,16,128]{2,1,0:T(8,128)(2,1)S(1)}, u32[]{:S(2)}, u32[]{:S(2)}) %all-to-all-start) | async-done | bytes 131104 | tf_op jit(solution)/shard_map/all_to_all | solution.py:22
  67.1 0.2 fusion.5
  67.3 0.7 copy.17
  68.0 3.9 %all-to-all-start.1 = ((bf16[32,16,128]{2,1,0:T(8,128)(2,1)}), bf16[32,16,128]{2,1,0:T(8,128)(2,1)S(1)}, u32[]{:S(2)}, u32[]{:S(2)}) async-start(bf16[32,16,128]{2,1,0:T(8,128)(2,1)} %bitcast.24), calls=%async_computation.1 | async-start | bytes 262144 | tf_op jit(solution)/shard_map/all_to_all | solution.py:29
  71.8 0.0 copy-start.4
  71.8 3.7 %fusion.3 = f32[1,512,4,128]{1,3,2,0:T(8,128)} fusion(pred[512,512]{1,0:T(8,128)(4,1)S(1)} %iota_compare_fusion, bf16[1,512,3,4,128]{1,4,3,2,0:T(8,128)(2,1)} %bitcast.65), kind=kOutput, calls=%fused_computation.9 | convolution fusion | flops 538968064 | bytes 2883584 | tf_op jit(solution)/shard_map/bhqk,bkhe->bqhe/dot_general | solution.py:77
  75.6 5.6 %all-to-all-done.1 = bf16[32,16,128]{2,1,0:T(8,128)(2,1)S(1)} async-done(((bf16[32,16,128]{2,1,0:T(8,128)(2,1)}), bf16[32,16,128]{2,1,0:T(8,128)(2,1)S(1)}, u32[]{:S(2)}, u32[]{:S(2)}) %all-to-all-start.1) | async-done | bytes 131104 | tf_op jit(solution)/shard_map/all_to_all | solution.py:29
  81.2 1.7 %multiply_reduce_fusion = (f32[512,4]{0,1:T(4,128)S(1)}, f32[1,512,4,128]{1,3,2,0:T(8,128)S(1)}) fusion(f32[1,512,4,128]{1,3,2,0:T(8,128)} %fusion.3, bf16[4,128,128]{2,1,0:T(8,128)(2,1)S(1)} %bitcast.69, bf16[1,512,3,4,128]{1,4,3,2,0:T(8,128)(2,1)} %bitcast.66), kind=kOutput, calls=%fused_computation.18 | convolution fusion | flops 67893248 | bytes 2760704 | tf_op jit(solution)/shard_map/bqhd,bhde->bqhe/dot_general | solution.py:79
  82.9 0.0 copy-done.4
  82.9 1.0 %multiply_convert_fusion = bf16[1,512,4,128]{1,3,2,0:T(8,128)(2,1)} fusion(f32[1,512,4,128]{1,3,2,0:T(8,128)S(1)} %get-tuple-element.6, f32[4,128]{1,0:T(4,128)S(1)} %bitcast.70, f32[512,4]{0,1:T(4,128)S(1)} %add_rsqrt_fusion), kind=kLoop, calls=%fused_computation.17 | loop fusion | flops 786432 | bytes 1583104 | tf_op jit(solution)/shard_map/convert_element_type | solution.py:85
  83.9 2.0 %copy.12 = bf16[512,512]{1,0:T(8,128)(2,1)} copy(bf16[512,512]{0,1:T(8,128)(2,1)} %bitcast.67) | data formatting | bytes 1048576 | tf_op jit(solution)/shard_map/convert_element_type | solution.py:85
  (2 shorter events, 0.0 us)
Async XLA Ops:
  0.0 38.9 %copy-start = (bf16[3072,512]{1,0:T(8,128)(2,1)S(1)}, bf16[3072,512]{1,0:T(8,128)(2,1)}, u32[]{:S(2)}) copy-start(bf16[3072,512]{1,0:T(8,128)(2,1)} %param.8) | copy-start | bytes 9437188
  0.0 25.9 %copy-start.3 = (bf16[64,3072]{1,0:T(8,128)(2,1)S(1)}, bf16[64,3072]{1,0:T(8,128)(2,1)}, u32[]{:S(2)}) copy-start(bf16[64,3072]{1,0:T(8,128)(2,1)} %param.5) | copy-start | bytes 1179652
  0.0 20.0 %collective-permute-start = (bf16[64,3072]{1,0:T(8,128)(2,1)}, bf16[64,3072]{1,0:T(8,128)(2,1)}, u32[]{:S(2)}, u32[]{:S(2)}) collective-permute-start(bf16[64,3072]{1,0:T(8,128)(2,1)} %param.5), channel_id=1, source_target_pairs={{0,6},{2,0},{4,2},{6,4},{1,7},{3,1},{5,3},{7,5},{8,14},{10,8},{12,... | collective-permute-start | bytes 1179656 | tf_op jit(solution)/shard_map/ppermute | solution.py:37
  3.6 17.4 %collective-permute-start.1 = (bf16[64,3072]{1,0:T(8,128)(2,1)}, bf16[64,3072]{1,0:T(8,128)(2,1)}, u32[]{:S(2)}, u32[]{:S(2)}) collective-permute-start(bf16[64,3072]{1,0:T(8,128)(2,1)} %param.5), channel_id=1, source_target_pairs={{0,4},{2,6},{4,0},{6,2},{1,5},{3,7},{5,1},{7,3},{8,12},{10,14},{12... | collective-permute-start | bytes 1179656 | tf_op jit(solution)/shard_map/ppermute | solution.py:37
  3.9 20.9 %collective-permute-start.2 = (bf16[64,3072]{1,0:T(8,128)(2,1)}, bf16[64,3072]{1,0:T(8,128)(2,1)}, u32[]{:S(2)}, u32[]{:S(2)}) collective-permute-start(bf16[64,3072]{1,0:T(8,128)(2,1)} %param.5), channel_id=1, source_target_pairs={{0,2},{2,4},{4,6},{6,0},{1,3},{3,5},{5,7},{7,1},{8,10},{10,12},{12... | collective-permute-start | bytes 1179656 | tf_op jit(solution)/shard_map/ppermute | solution.py:37
  29.0 1.6 %copy-start.1 = (bf16[8,64,3072]{2,1,0:T(8,128)(2,1)}, bf16[8,64,3072]{2,1,0:T(8,128)(2,1)S(1)}, u32[]{:S(2)}) copy-start(bf16[8,64,3072]{2,1,0:T(8,128)(2,1)S(1)} %bitcast_dynamic-update-slice_fusion.1) | copy-start | bytes 9437188
  31.9 3.9 %collective-permute-start.3 = (bf16[4,64,3072]{2,1,0:T(8,128)(2,1)}, bf16[4,64,3072]{2,1,0:T(8,128)(2,1)}, u32[]{:S(2)}, u32[]{:S(2)}) collective-permute-start(bf16[4,64,3072]{2,1,0:T(8,128)(2,1)} %constant_dynamic-slice_fusion), channel_id=1, source_target_pairs={{0,1},{1,0},{2,3},{3,2},{4,5},{5,4},{6,7},{7,6},{8,9},{9,8},{10,11... | collective-permute-start | bytes 4718600 | tf_op jit(solution)/shard_map/ppermute | solution.py:42
  38.9 1.9 %copy-start.5 = (bf16[3072,512]{1,0:T(8,128)(2,1)S(1)}, bf16[3072,512]{1,0:T(8,128)(2,1)}, u32[]{:S(2)}) copy-start(bf16[3072,512]{1,0:T(8,128)(2,1)} %param.7) | copy-start | bytes 9437188
  40.8 1.9 %copy-start.6 = (bf16[3072,512]{1,0:T(8,128)(2,1)S(1)}, bf16[3072,512]{1,0:T(8,128)(2,1)}, u32[]{:S(2)}) copy-start(bf16[3072,512]{1,0:T(8,128)(2,1)} %param.6) | copy-start | bytes 9437188
  44.6 1.2 %copy-start.2 = (bf16[512,1536]{0,1:T(8,128)(2,1)}, bf16[512,1536]{0,1:T(8,128)(2,1)S(1)}, u32[]{:S(2)}) copy-start(bf16[512,1536]{0,1:T(8,128)(2,1)S(1)} %pad_maximum_fusion) | copy-start | bytes 4718596
  46.7 20.4 %all-to-all-start = ((bf16[32,16,128]{2,1,0:T(8,128)(2,1)}), bf16[32,16,128]{2,1,0:T(8,128)(2,1)S(1)}, u32[]{:S(2)}, u32[]{:S(2)}) async-start(bf16[32,16,128]{2,1,0:T(8,128)(2,1)} %bitcast.13), calls=%async_computation | async-start | bytes 262144 | tf_op jit(solution)/shard_map/all_to_all | solution.py:22
  68.0 13.2 %all-to-all-start.1 = ((bf16[32,16,128]{2,1,0:T(8,128)(2,1)}), bf16[32,16,128]{2,1,0:T(8,128)(2,1)S(1)}, u32[]{:S(2)}, u32[]{:S(2)}) async-start(bf16[32,16,128]{2,1,0:T(8,128)(2,1)} %bitcast.24), calls=%async_computation.1 | async-start | bytes 262144 | tf_op jit(solution)/shard_map/all_to_all | solution.py:29
  71.8 11.1 %copy-start.4 = (f32[512]{0:T(512)S(1)}, f32[512]{0:T(512)}, u32[]{:S(2)}) copy-start(f32[512]{0:T(512)} %param.9) | copy-start | bytes 6148

commit v10 on v9

--- a/solution.py
+++ b/solution.py
@@ -33,16 +33,21 @@
 def gather_rows(tokens):
     chips = lax.axis_size("y")
     chip = lax.axis_index("y")
-    ahead = [tokens] + [
-        lax.ppermute(tokens, "y", [(i, (i - by) % chips) for i in range(chips)])
-        for by in range(1, chips)
-    ]
-    twice = jnp.stack(ahead + ahead)
-    near = lax.dynamic_slice_in_dim(twice, (chips - chip) % chips, chips, axis=0)
+    near = jnp.stack(
+        [tokens]
+        + [
+            lax.ppermute(tokens, "y", [(i, (i - by) % chips) for i in range(chips)])
+            for by in range(1, chips)
+        ]
+    )
     other = lax.ppermute(near, "core", [(0, 1), (1, 0)])
-    trio = jnp.stack([near, other, near], axis=1)
-    both = lax.dynamic_slice_in_dim(trio, lax.axis_index("core"), 2, axis=1)
-    return both.reshape(-1, tokens.shape[1])
+    cores = 2
+    both = jnp.concatenate([near, other], axis=0)
+    slot = jnp.arange(chips * cores)
+    ahead = (slot // cores - chip) % chips
+    across = (slot % cores - lax.axis_index("core")) % cores
+    ordered = jnp.take(both, across * chips + ahead, axis=0, mode="clip")
+    return ordered.reshape(-1, tokens.shape[1])
 
 
 def body(tokens, w_query, w_key, w_value, norm_gain):

time: 87.6 us -> 87 us (level); the launches traced: 85.9 us -> 86.5 us
  matrix products: 12.1 us -> 14.1 us
  other arithmetic: 4.24 us -> 2.61 us
    gather x0 -> x1, local copies, waits for them, and re-layouts: none -> 4.31 us  [gather_rows(): ordered = jnp.take(both, across * chips + ahead, axis=0, mode='clip')]
    another operation x2 -> x0, local copies, waits for them, and re-layouts: 2.53 us -> none  [the longest x1 1.51 us: gather_rows(): trio = jnp.stack([near, other, near], axis=1)]
    dot_general x1, matrix products: 1.86 us -> 3.87 us  [body(): jnp.dot(piece_rows, w_value, preferred_element_type=jnp.float32)]
    ppermute x1, waiting for transfers between devices: 1.87 us -> 0.01 us  [gather_rows(): other = lax.ppermute(near, 'core', [(0, 1), (1, 0)])]
    unnamed x22 -> x17, local copies, waits for them, and re-layouts: 9.73 us -> 8.02 us
    another operation x1, other arithmetic: 3.09 us -> 1.43 us  [gather_rows(): jnp.stack([tokens] + [lax.ppermute(tokens, 'y', [(i, (i - by) % chips) fo...]
    ppermute x3, waiting for transfers between devices: 17.1 us -> 18.4 us  [gather_rows(): lax.ppermute(tokens, 'y', [(i, (i - by) % chips) for i in range(chips)])]
    dynamic_slice x1 -> x0, local copies, waits for them, and re-layouts: 1.26 us -> none  [gather_rows(): lax.dynamic_slice_in_dim(twice, (chips - chip) % chips, chips, axis=0)]
  transfers between devices with their start and end apart: 6 -> 6, of which waited for: 5 -> 4; matrix products, arithmetic and copies ran while one was open for 10% -> 12% of each run, Pallas kernels for 0% -> 0%
where the time goes in v10:
time: 87 us; the launch traced here: 86.5 us
  waiting for transfers between devices  33.9 us (39%)
  starting transfers between devices  20.1 us (23%)
  local copies, waits for them, and re-layouts  15.6 us (18%)
  matrix products  14.1 us (16%)
  other arithmetic  2.61 us (3%)
    ppermute x3, waiting for transfers between devices, gather_rows(): lax.ppermute(tokens, 'y', [(i, (i - by) % chips) for i in range(chips)])  18.4 us
    all_to_all x1, starting transfers between devices, exclusive_scan(): gathered = lax.all_to_all(pieces, axis, 0, 0, tiled=True)  11 us
    all_to_all x1, waiting for transfers between devices, exclusive_scan(): gathered = lax.all_to_all(pieces, axis, 0, 0, tiled=True)  9.83 us
    unnamed x17, local copies, waits for them, and re-layouts  8.02 us
    all_to_all x1, waiting for transfers between devices, exclusive_scan(): lax.all_to_all(before.reshape(pieces.shape), axis, 0, 0, tiled=True)  5.66 us
    ppermute x3, starting transfers between devices, gather_rows(): lax.ppermute(tokens, 'y', [(i, (i - by) % chips) for i in range(chips)])  4.59 us
    gather x1, local copies, waits for them, and re-layouts, gather_rows(): ordered = jnp.take(both, across * chips + ahead, axis=0, mode='clip')  4.31 us
    dot_general x1, matrix products, body(): jnp.dot(piece_rows, w_value, preferred_element_type=jnp.float32)  3.87 us
  transfers between devices with their start and end apart: 6, of which 4 were waited for; matrix products, arithmetic and copies ran while one was open for 12% of the time, Pallas kernels for 0%

profile of v10, /device:TPU:1, one launch (start us, length us, event | category | flops | bytes accessed | tf_op | source)
XLA Modules:
  0.0 86.5 jit_solution(4189965794460088071)
XLA Ops:
  0.0 0.0 copy-start
  0.0 3.6 %collective-permute-start = (bf16[64,3072]{1,0:T(8,128)(2,1)}, bf16[64,3072]{1,0:T(8,128)(2,1)S(1)}, u32[]{:S(2)}, u32[]{:S(2)}) collective-permute-start(bf16[64,3072]{1,0:T(8,128)(2,1)} %param.5), channel_id=1, source_target_pairs={{0,6},{2,0},{4,2},{6,4},{1,7},{3,1},{5,3},{7,5},{8,14},{10,8},{12,... | collective-permute-start | bytes 1179656 | tf_op jit(solution)/shard_map/ppermute | solution.py:39
  3.6 0.3 collective-permute-start.1
  3.9 0.7 collective-permute-start.2
  4.6 1.8 %constant_dynamic-update-slice_fusion.4 = bf16[8,64,3072]{2,1,0:T(8,128)(2,1)} fusion(bf16[64,3072]{1,0:T(8,128)(2,1)} %param.5), kind=kLoop, calls=%fused_computation.27 | loop fusion | bytes 786432
  6.4 13.5 %collective-permute-done = bf16[64,3072]{1,0:T(8,128)(2,1)S(1)} collective-permute-done((bf16[64,3072]{1,0:T(8,128)(2,1)}, bf16[64,3072]{1,0:T(8,128)(2,1)S(1)}, u32[]{:S(2)}, u32[]{:S(2)}) %collective-permute-start) | collective-permute-done | bytes 393248 | tf_op jit(solution)/shard_map/ppermute | solution.py:39
  20.0 0.0 collective-permute-done.1
  20.0 4.9 %collective-permute-done.2 = bf16[64,3072]{1,0:T(8,128)(2,1)} collective-permute-done((bf16[64,3072]{1,0:T(8,128)(2,1)}, bf16[64,3072]{1,0:T(8,128)(2,1)}, u32[]{:S(2)}, u32[]{:S(2)}) %collective-permute-start.2) | collective-permute-done | bytes 393248 | tf_op jit(solution)/shard_map/ppermute | solution.py:39
  24.8 1.4 %pad_maximum_fusion = bf16[4,64,3072]{2,1,0:T(8,128)(2,1)S(1)} fusion(bf16[1,64,3072]{2,1,0:T(8,128)(2,1)} %bitcast.3, bf16[1,64,3072]{2,1,0:T(8,128)(2,1)} %bitcast.2, bf16[1,64,3072]{2,1,0:T(8,128)(2,1)S(1)} %bitcast.64, bf16[1,64,3072]{2,1,0:T(8,128)(2,1)} %bitcast.63), kind=kLoop, calls=%fused_computation.4 | loop fusion | flops 2359296 | bytes 3145728 | tf_op jit(solution)/shard_map/stack | solution.py:36
  26.3 0.6 collective-permute-start.3
  26.9 0.8 constant_dynamic-update-slice_fusion.3
  27.6 1.8 %constant_dynamic-update-slice_fusion.2 = bf16[8,64,3072]{2,1,0:T(8,128)(2,1)} fusion(bf16[8,64,3072]{2,1,0:T(8,128)(2,1)} %constant_dynamic-update-slice_fusion.3, bf16[64,3072]{1,0:T(8,128)(2,1)} %collective-permute-done.1), kind=kLoop, calls=%fused_computation.25 | loop fusion | bytes 786432
  29.4 1.8 %constant_dynamic-update-slice_fusion.1 = bf16[8,64,3072]{2,1,0:T(8,128)(2,1)} fusion(bf16[8,64,3072]{2,1,0:T(8,128)(2,1)} %constant_dynamic-update-slice_fusion.2, bf16[64,3072]{1,0:T(8,128)(2,1)} %collective-permute-done.2), kind=kLoop, calls=%fused_computation.24 | loop fusion | bytes 786432
  31.2 0.0 collective-permute-done.3
  31.2 1.3 %constant_dynamic-update-slice_fusion = bf16[8,64,3072]{2,1,0:T(8,128)(2,1)} fusion(bf16[8,64,3072]{2,1,0:T(8,128)(2,1)} %constant_dynamic-update-slice_fusion.1, bf16[4,64,3072]{2,1,0:T(8,128)(2,1)S(1)} %collective-permute-done.3), kind=kLoop, calls=%fused_computation.23 | loop fusion | bytes 3145728 | tf_op jit(solution)/shard_map/concatenate | solution.py:45
  32.4 4.3 %gather_fusion = bf16[8,64,3072]{2,1,0:T(8,128)(2,1)} fusion(bf16[8,64,3072]{2,1,0:T(8,128)(2,1)} %constant_dynamic-update-slice_fusion, s32[1024]{0:T(1024)S(1)} %pad_clamp_fusion), kind=kCustom, calls=%fused_computation | custom fusion | bytes 6291488 | tf_op jit(solution)/shard_map/jit(_take)/gather | solution.py:49
  36.7 0.0 copy-done
  36.7 0.0 copy-start.1
  36.7 0.0 copy-start.4
  36.8 3.9 %convolution_convert_fusion.1 = bf16[512,512]{0,1:T(8,128)(2,1)S(1)} fusion(bf16[512,3072]{1,0:T(8,128)(2,1)} %bitcast.56, bf16[3072,512]{1,0:T(8,128)(2,1)S(1)} %copy-done), kind=kOutput, calls=%fused_computation.9 | convolution fusion | flops 1610874880 | bytes 6815744 | tf_op jit(solution)/shard_map/dot_general | solution.py:61
  40.6 0.0 copy-done.1
  40.6 0.0 copy-done.4
  40.6 0.0 copy-start.5
  40.7 1.8 %convolution_convert_fusion.2 = bf16[512,512]{0,1:T(8,128)(2,1)S(1)} fusion(bf16[512,3072]{1,0:T(8,128)(2,1)S(1)} %bitcast.57, bf16[3072,512]{1,0:T(8,128)(2,1)S(1)} %copy-done.4), kind=kOutput, calls=%fused_computation.10 | convolution fusion | flops 1610874880 | bytes 6815744 | tf_op jit(solution)/shard_map/dot_general | solution.py:60
  42.5 0.0 copy-done.5
  42.5 1.8 %convolution_convert_fusion.3 = bf16[512,512]{0,1:T(8,128)(2,1)S(1)} fusion(bf16[512,3072]{1,0:T(8,128)(2,1)S(1)} %bitcast.58, bf16[3072,512]{1,0:T(8,128)(2,1)S(1)} %copy-done.5), kind=kOutput, calls=%fused_computation.11 | convolution fusion | flops 1610874880 | bytes 6815744 | tf_op jit(solution)/shard_map/dot_general | solution.py:57
  44.4 0.1 pad_maximum_fusion.1
  44.5 0.0 copy-start.2
  44.5 1.2 %copy-done.2 = bf16[512,1536]{0,1:T(8,128)(2,1)} copy-done((bf16[512,1536]{0,1:T(8,128)(2,1)}, bf16[512,1536]{0,1:T(8,128)(2,1)S(1)}, u32[]{:S(2)}) %copy-start.2) | copy-done | bytes 1572888
  45.7 1.0 %convolution_convert_fusion.4 = bf16[4,128,128]{2,1,0:T(8,128)(2,1)} fusion(bf16[1,512,3,4,128]{1,4,3,2,0:T(8,128)(2,1)S(1)} %bitcast.59), kind=kOutput, calls=%fused_computation.12 | convolution fusion | flops 67174400 | bytes 1179648 | tf_op jit(solution)/shard_map/bshd,bshe->bhde/dot_general | solution.py:71
  46.6 11.0 %all-to-all-start = ((bf16[32,16,128]{2,1,0:T(8,128)(2,1)}), bf16[32,16,128]{2,1,0:T(8,128)(2,1)S(1)}, u32[]{:S(2)}, u32[]{:S(2)}) async-start(bf16[32,16,128]{2,1,0:T(8,128)(2,1)} %bitcast.12), calls=%async_computation | async-start | bytes 262144 | tf_op jit(solution)/shard_map/all_to_all | solution.py:22
  57.7 0.1 iota_compare_fusion
  57.7 9.8 %all-to-all-done = bf16[32,16,128]{2,1,0:T(8,128)(2,1)S(1)} async-done(((bf16[32,16,128]{2,1,0:T(8,128)(2,1)}), bf16[32,16,128]{2,1,0:T(8,128)(2,1)S(1)}, u32[]{:S(2)}, u32[]{:S(2)}) %all-to-all-start) | async-done | bytes 131104 | tf_op jit(solution)/shard_map/all_to_all | solution.py:22
  67.6 0.2 fusion.3
  67.7 0.7 copy.17
  68.4 3.9 %all-to-all-start.1 = ((bf16[32,16,128]{2,1,0:T(8,128)(2,1)}), bf16[32,16,128]{2,1,0:T(8,128)(2,1)S(1)}, u32[]{:S(2)}, u32[]{:S(2)}) async-start(bf16[32,16,128]{2,1,0:T(8,128)(2,1)} %bitcast.23), calls=%async_computation.1 | async-start | bytes 262144 | tf_op jit(solution)/shard_map/all_to_all | solution.py:29
  72.3 0.0 copy-start.3
  72.3 3.7 %fusion.1 = f32[1,512,4,128]{1,3,2,0:T(8,128)} fusion(pred[512,512]{1,0:T(8,128)(4,1)S(1)} %iota_compare_fusion, bf16[1,512,3,4,128]{1,4,3,2,0:T(8,128)(2,1)} %bitcast.60), kind=kOutput, calls=%fused_computation.6 | convolution fusion | flops 538968064 | bytes 2883584 | tf_op jit(solution)/shard_map/bhqk,bkhe->bqhe/dot_general | solution.py:82
  76.0 5.7 %all-to-all-done.1 = bf16[32,16,128]{2,1,0:T(8,128)(2,1)S(1)} async-done(((bf16[32,16,128]{2,1,0:T(8,128)(2,1)}), bf16[32,16,128]{2,1,0:T(8,128)(2,1)S(1)}, u32[]{:S(2)}, u32[]{:S(2)}) %all-to-all-start.1) | async-done | bytes 131104 | tf_op jit(solution)/shard_map/all_to_all | solution.py:29
  81.7 1.7 %multiply_reduce_fusion = (f32[512,4]{0,1:T(4,128)S(1)}, f32[1,512,4,128]{1,3,2,0:T(8,128)S(1)}) fusion(f32[1,512,4,128]{1,3,2,0:T(8,128)} %fusion.1, bf16[4,128,128]{2,1,0:T(8,128)(2,1)S(1)} %bitcast.66, bf16[1,512,3,4,128]{1,4,3,2,0:T(8,128)(2,1)} %bitcast.61), kind=kOutput, calls=%fused_computation.15 | convolution fusion | flops 67893248 | bytes 2760704 | tf_op jit(solution)/shard_map/bqhd,bhde->bqhe/dot_general | solution.py:84
  83.5 0.0 copy-done.3
  83.5 1.0 %multiply_convert_fusion = bf16[1,512,4,128]{1,3,2,0:T(8,128)(2,1)} fusion(f32[1,512,4,128]{1,3,2,0:T(8,128)S(1)} %get-tuple-element.6, f32[4,128]{1,0:T(4,128)S(1)} %bitcast.67, f32[512,4]{0,1:T(4,128)S(1)} %add_rsqrt_fusion), kind=kLoop, calls=%fused_computation.14 | loop fusion | flops 786432 | bytes 1583104 | tf_op jit(solution)/shard_map/convert_element_type | solution.py:90
  84.4 2.0 %copy.12 = bf16[512,512]{1,0:T(8,128)(2,1)} copy(bf16[512,512]{0,1:T(8,128)(2,1)} %bitcast.62) | data formatting | bytes 1048576 | tf_op jit(solution)/shard_map/convert_element_type | solution.py:90
  (3 shorter events, 0.0 us)
Async XLA Ops:
  0.0 36.7 %copy-start = (bf16[3072,512]{1,0:T(8,128)(2,1)S(1)}, bf16[3072,512]{1,0:T(8,128)(2,1)}, u32[]{:S(2)}) copy-start(bf16[3072,512]{1,0:T(8,128)(2,1)} %param.8) | copy-start | bytes 9437188
  0.0 20.0 %collective-permute-start = (bf16[64,3072]{1,0:T(8,128)(2,1)}, bf16[64,3072]{1,0:T(8,128)(2,1)S(1)}, u32[]{:S(2)}, u32[]{:S(2)}) collective-permute-start(bf16[64,3072]{1,0:T(8,128)(2,1)} %param.5), channel_id=1, source_target_pairs={{0,6},{2,0},{4,2},{6,4},{1,7},{3,1},{5,3},{7,5},{8,14},{10,8},{12,... | collective-permute-start | bytes 1179656 | tf_op jit(solution)/shard_map/ppermute | solution.py:39
  3.6 16.4 %collective-permute-start.1 = (bf16[64,3072]{1,0:T(8,128)(2,1)}, bf16[64,3072]{1,0:T(8,128)(2,1)}, u32[]{:S(2)}, u32[]{:S(2)}) collective-permute-start(bf16[64,3072]{1,0:T(8,128)(2,1)} %param.5), channel_id=1, source_target_pairs={{0,4},{2,6},{4,0},{6,2},{1,5},{3,7},{5,1},{7,3},{8,12},{10,14},{12... | collective-permute-start | bytes 1179656 | tf_op jit(solution)/shard_map/ppermute | solution.py:39
  3.9 20.9 %collective-permute-start.2 = (bf16[64,3072]{1,0:T(8,128)(2,1)}, bf16[64,3072]{1,0:T(8,128)(2,1)}, u32[]{:S(2)}, u32[]{:S(2)}) collective-permute-start(bf16[64,3072]{1,0:T(8,128)(2,1)} %param.5), channel_id=1, source_target_pairs={{0,2},{2,4},{4,6},{6,0},{1,3},{3,5},{5,7},{7,1},{8,10},{10,12},{12... | collective-permute-start | bytes 1179656 | tf_op jit(solution)/shard_map/ppermute | solution.py:39
  26.3 4.9 %collective-permute-start.3 = (bf16[4,64,3072]{2,1,0:T(8,128)(2,1)S(1)}, bf16[4,64,3072]{2,1,0:T(8,128)(2,1)S(1)}, u32[]{:S(2)}, u32[]{:S(2)}) collective-permute-start(bf16[4,64,3072]{2,1,0:T(8,128)(2,1)S(1)} %pad_maximum_fusion), channel_id=1, source_target_pairs={{0,1},{1,0},{2,3},{3,2},{4,5},{5,4},{6,7},{7,6},{8,9},{9,8},{10,11... | collective-permute-start | bytes 4718600 | tf_op jit(solution)/shard_map/ppermute | solution.py:43
  36.7 3.9 %copy-start.1 = (bf16[8,64,3072]{2,1,0:T(8,128)(2,1)S(1)}, bf16[8,64,3072]{2,1,0:T(8,128)(2,1)}, u32[]{:S(2)}) copy-start(bf16[8,64,3072]{2,1,0:T(8,128)(2,1)} %gather_fusion) | copy-start | bytes 9437188
  36.7 3.9 %copy-start.4 = (bf16[3072,512]{1,0:T(8,128)(2,1)S(1)}, bf16[3072,512]{1,0:T(8,128)(2,1)}, u32[]{:S(2)}) copy-start(bf16[3072,512]{1,0:T(8,128)(2,1)} %param.7) | copy-start | bytes 9437188
  40.6 1.9 %copy-start.5 = (bf16[3072,512]{1,0:T(8,128)(2,1)S(1)}, bf16[3072,512]{1,0:T(8,128)(2,1)}, u32[]{:S(2)}) copy-start(bf16[3072,512]{1,0:T(8,128)(2,1)} %param.6) | copy-start | bytes 9437188
  44.5 1.2 %copy-start.2 = (bf16[512,1536]{0,1:T(8,128)(2,1)}, bf16[512,1536]{0,1:T(8,128)(2,1)S(1)}, u32[]{:S(2)}) copy-start(bf16[512,1536]{0,1:T(8,128)(2,1)S(1)} %pad_maximum_fusion.1) | copy-start | bytes 4718596
  46.6 21.0 %all-to-all-start = ((bf16[32,16,128]{2,1,0:T(8,128)(2,1)}), bf16[32,16,128]{2,1,0:T(8,128)(2,1)S(1)}, u32[]{:S(2)}, u32[]{:S(2)}) async-start(bf16[32,16,128]{2,1,0:T(8,128)(2,1)} %bitcast.12), calls=%async_computation | async-start | bytes 262144 | tf_op jit(solution)/shard_map/all_to_all | solution.py:22
  68.4 13.3 %all-to-all-start.1 = ((bf16[32,16,128]{2,1,0:T(8,128)(2,1)}), bf16[32,16,128]{2,1,0:T(8,128)(2,1)S(1)}, u32[]{:S(2)}, u32[]{:S(2)}) async-start(bf16[32,16,128]{2,1,0:T(8,128)(2,1)} %bitcast.23), calls=%async_computation.1 | async-start | bytes 262144 | tf_op jit(solution)/shard_map/all_to_all | solution.py:29
  72.3 11.2 %copy-start.3 = (f32[512]{0:T(512)S(1)}, f32[512]{0:T(512)}, u32[]{:S(2)}) copy-start(f32[512]{0:T(512)} %param.9) | copy-start | bytes 6148

commit v11 on v7

--- a/solution.py
+++ b/solution.py
@@ -36,23 +36,28 @@
     return lax.all_to_all(copies, axis, 0, 0, tiled=True)
 
 
-def gather_rows(tokens):
-    near = spread(tokens, "y")
-    both = spread(near, "core")
-    return both.transpose(1, 0, 2, 3).reshape(-1, tokens.shape[1])
-
-
 def body(tokens, w_query, w_key, w_value, norm_gain):
     local_width = w_query.shape[1]
     head_count = local_width // HEAD_DIM
-    piece_rows = gather_rows(tokens)
-    query_part = jnp.dot(piece_rows, w_query, preferred_element_type=jnp.float32).astype(
-        jnp.bfloat16
-    )
-    key_part = jnp.dot(piece_rows, w_key, preferred_element_type=jnp.float32).astype(jnp.bfloat16)
-    value_part = jnp.dot(piece_rows, w_value, preferred_element_type=jnp.float32).astype(
-        jnp.bfloat16
-    )
+    near = spread(tokens, "y")
+    other = lax.ppermute(near, "core", [(0, 1), (1, 0)])
+    first = lax.axis_index("core") == 0
+
+    def project(weight):
+        def half(rows):
+            flat = rows.reshape(-1, rows.shape[-1])
+            part = jnp.dot(flat, weight, preferred_element_type=jnp.float32).astype(jnp.bfloat16)
+            return part.reshape(rows.shape[0], rows.shape[1], weight.shape[1])
+
+        mine, theirs = half(near), half(other)
+        paired = jnp.where(
+            first, jnp.stack([mine, theirs], axis=1), jnp.stack([theirs, mine], axis=1)
+        )
+        return paired.reshape(-1, weight.shape[1])
+
+    query_part = project(w_query)
+    key_part = project(w_key)
+    value_part = project(w_value)
     projected = jnp.concatenate([query_part, key_part, value_part], axis=1)
     group_len = projected.shape[0]
     block_count = group_len // BLOCK

time: 82.6 us -> 89.3 us (1.081)
  matrix products: 12.1 us -> 22.5 us
  blocking collectives: 32.4 us -> 24 us
  starting transfers between devices: 14.9 us -> 17.5 us
  other arithmetic: 1.14 us -> 2.45 us
    dot_general x3 -> x6, matrix products: 5.52 us -> 14.7 us  [half(): jnp.dot(flat, weight, preferred_element_type=jnp.float32)]
    all_to_all x2 -> x1, blocking collectives: 32.4 us -> 24 us  [spread(): return lax.all_to_all(copies, axis, 0, 0, tiled=True)]
    ppermute x0 -> x1, starting transfers between devices: none -> 2.62 us  [body(): other = lax.ppermute(near, 'core', [(0, 1), (1, 0)])]
    concatenate x0 -> x1, local copies, waits for them, and re-layouts: none -> 2.61 us  [body(): projected = jnp.concatenate([query_part, key_part, value_part], axis=1)]
    dot_general x1, matrix products: 0.95 us -> 2.15 us  [body(): jnp.einsum('bshd,bshe->bhde', key_rows, value_rows, preferred_element_typ...]
    unnamed x11 -> x9, local copies, waits for them, and re-layouts: 1.89 us -> 0.69 us
    concatenate x1, other arithmetic: 0.1 us -> 1.25 us  [body(): projected = jnp.concatenate([query_part, key_part, value_part], axis=1)]
  transfers between devices with their start and end apart: 2 -> 3, of which waited for: 2 -> 2; matrix products, arithmetic and copies ran while one was open for 5% -> 13% of each run, Pallas kernels for 0% -> 0%
where the time goes in v11:
time: 89.3 us; the launch traced here: 88.8 us
  blocking collectives  24 us (27%)
  matrix products  22.5 us (25%)
  starting transfers between devices  17.5 us (20%)
  waiting for transfers between devices  15.5 us (17%)
  local copies, waits for them, and re-layouts  6.66 us (7%)
  other arithmetic  2.45 us (3%)
    all_to_all x1, blocking collectives, spread(): return lax.all_to_all(copies, axis, 0, 0, tiled=True)  24 us
    dot_general x6, matrix products, half(): jnp.dot(flat, weight, preferred_element_type=jnp.float32)  14.7 us
    all_to_all x1, starting transfers between devices, exclusive_scan(): gathered = lax.all_to_all(pieces, axis, 0, 0, tiled=True)  11 us
    all_to_all x1, waiting for transfers between devices, exclusive_scan(): gathered = lax.all_to_all(pieces, axis, 0, 0, tiled=True)  9.83 us
    all_to_all x1, waiting for transfers between devices, exclusive_scan(): lax.all_to_all(before.reshape(pieces.shape), axis, 0, 0, tiled=True)  5.69 us
    all_to_all x1, starting transfers between devices, exclusive_scan(): lax.all_to_all(before.reshape(pieces.shape), axis, 0, 0, tiled=True)  3.86 us
    dot_general x1, matrix products, body(): jnp.einsum('bhqk,bkhe->bqhe', scores, value_rows, preferred_element_type=...  3.71 us
    ppermute x1, starting transfers between devices, body(): other = lax.ppermute(near, 'core', [(0, 1), (1, 0)])  2.62 us
  transfers between devices with their start and end apart: 3, of which 2 were waited for; matrix products, arithmetic and copies ran while one was open for 13% of the time, Pallas kernels for 0%

profile of v11, /device:TPU:1, one launch (start us, length us, event | category | flops | bytes accessed | tf_op | source)
XLA Modules:
  0.0 88.8 jit_solution(4698722225408152685)
XLA Ops:
  0.0 0.0 copy-start
  0.0 1.3 %broadcast_in_dim.10 = bf16[4,64,3072]{2,1,0:T(8,128)(2,1)S(1)} broadcast(bf16[64,3072]{1,0:T(8,128)(2,1)} %param.5), dimensions={1,2} | broadcast | bytes 1966080 | tf_op jit(solution)/shard_map/broadcast_in_dim | solution.py:35
  1.3 24.0 %all_to_all.15 = bf16[4,64,3072]{2,1,0:T(8,128)(2,1)} all-to-all(bf16[4,64,3072]{2,1,0:T(8,128)(2,1)S(1)} %broadcast_in_dim.10), channel_id=1, replica_groups=mesh['ctx'=32,'y'=4,'core'=2] {'y'}, dimensions={0} | all-to-all | bytes 3145728 | tf_op jit(solution)/shard_map/all_to_all | solution.py:36
  25.3 2.6 %collective-permute-start = (bf16[4,64,3072]{2,1,0:T(8,128)(2,1)}, bf16[4,64,3072]{2,1,0:T(8,128)(2,1)}, u32[]{:S(2)}, u32[]{:S(2)}) collective-permute-start(bf16[4,64,3072]{2,1,0:T(8,128)(2,1)} %all_to_all.15), channel_id=1, source_target_pairs={{0,1},{1,0},{2,3},{3,2},{4,5},{5,4},{6,7},{7,6},{8,9},{9,8},{10,11... | collective-permute-start | bytes 4718600 | tf_op jit(solution)/shard_map/ppermute | solution.py:43
  27.9 0.0 copy-done
  27.9 0.0 copy-start.2
  27.9 2.5 %convolution_convert_fusion.2 = bf16[256,512]{1,0:T(8,128)(2,1)S(1)} fusion(bf16[256,3072]{1,0:T(8,128)(2,1)} %bitcast, bf16[3072,512]{1,0:T(8,128)(2,1)S(1)} %copy-done), kind=kOutput, calls=%fused_computation.8 | convolution fusion | flops 805437440 | bytes 4980736 | tf_op jit(solution)/shard_map/dot_general | solution.py:49
  30.4 0.0 copy-done.2
  30.5 0.0 copy-start.3
  30.5 2.6 %convolution_convert_fusion.4 = bf16[256,512]{1,0:T(8,128)(2,1)S(1)} fusion(bf16[256,3072]{1,0:T(8,128)(2,1)} %bitcast, bf16[3072,512]{1,0:T(8,128)(2,1)S(1)} %copy-done.2), kind=kOutput, calls=%fused_computation.10 | convolution fusion | flops 805437440 | bytes 4980736 | tf_op jit(solution)/shard_map/dot_general | solution.py:49
  33.0 0.0 copy-done.3
  33.1 2.4 %convolution_convert_fusion.6 = bf16[256,512]{1,0:T(8,128)(2,1)S(1)} fusion(bf16[256,3072]{1,0:T(8,128)(2,1)} %bitcast, bf16[3072,512]{1,0:T(8,128)(2,1)S(1)} %copy-done.3), kind=kOutput, calls=%fused_computation.12 | convolution fusion | flops 805437440 | bytes 4980736 | tf_op jit(solution)/shard_map/dot_general | solution.py:49
  35.5 0.0 collective-permute-done
  35.5 2.4 %convolution_convert_fusion.1 = bf16[256,512]{1,0:T(8,128)(2,1)S(1)} fusion(bf16[256,3072]{1,0:T(8,128)(2,1)} %bitcast.3, bf16[3072,512]{1,0:T(8,128)(2,1)S(1)} %copy-done), kind=kOutput, calls=%fused_computation.7 | convolution fusion | flops 805437440 | bytes 4980736 | tf_op jit(solution)/shard_map/dot_general | solution.py:49
  37.9 2.4 %convolution_convert_fusion.3 = bf16[256,512]{1,0:T(8,128)(2,1)S(1)} fusion(bf16[256,3072]{1,0:T(8,128)(2,1)} %bitcast.3, bf16[3072,512]{1,0:T(8,128)(2,1)S(1)} %copy-done.2), kind=kOutput, calls=%fused_computation.9 | convolution fusion | flops 805437440 | bytes 4980736 | tf_op jit(solution)/shard_map/dot_general | solution.py:49
  40.3 2.4 %convolution_convert_fusion.5 = bf16[256,512]{1,0:T(8,128)(2,1)S(1)} fusion(bf16[256,3072]{1,0:T(8,128)(2,1)} %bitcast.3, bf16[3072,512]{1,0:T(8,128)(2,1)S(1)} %copy-done.3), kind=kOutput, calls=%fused_computation.11 | convolution fusion | flops 805437440 | bytes 4980736 | tf_op jit(solution)/shard_map/dot_general | solution.py:49
  42.7 0.1 maximum_select_fusion.2
  42.8 0.1 maximum_select_fusion
  42.9 1.3 %pad_maximum_fusion = bf16[512,1536]{1,0:T(8,128)(2,1)} fusion(bf16[512,512]{1,0:T(8,128)(2,1)S(1)} %bitcast.86, bf16[512,512]{1,0:T(8,128)(2,1)S(1)} %bitcast.84, bf16[512,512]{1,0:T(8,128)(2,1)S(1)} %bitcast.83), kind=kLoop, calls=%fused_computation.3 | loop fusion | flops 4718592 | bytes 3145728 | tf_op jit(solution)/shard_map/concatenate | solution.py:61
  44.2 2.6 %copy.21 = bf16[512,1536]{0,1:T(8,128)(2,1)} copy(bf16[512,1536]{1,0:T(8,128)(2,1)} %pad_maximum_fusion) | data formatting | bytes 3145728 | tf_op jit(solution)/shard_map/concatenate | solution.py:61
  46.8 2.2 %convolution_convert_fusion.7 = bf16[4,128,128]{2,1,0:T(8,128)(2,1)} fusion(bf16[1,512,3,4,128]{1,4,3,2,0:T(8,128)(2,1)} %bitcast.80), kind=kOutput, calls=%fused_computation.13 | convolution fusion | flops 67174400 | bytes 1179648 | tf_op jit(solution)/shard_map/bshd,bshe->bhde/dot_general | solution.py:68
  48.9 11.0 %all-to-all-start.1 = ((bf16[32,16,128]{2,1,0:T(8,128)(2,1)}), bf16[32,16,128]{2,1,0:T(8,128)(2,1)S(1)}, u32[]{:S(2)}, u32[]{:S(2)}) async-start(bf16[32,16,128]{2,1,0:T(8,128)(2,1)} %bitcast.29), calls=%async_computation.1 | async-start | bytes 262144 | tf_op jit(solution)/shard_map/all_to_all | solution.py:22
  60.0 0.1 iota_compare_fusion
  60.0 9.8 %all-to-all-done.1 = bf16[32,16,128]{2,1,0:T(8,128)(2,1)S(1)} async-done(((bf16[32,16,128]{2,1,0:T(8,128)(2,1)}), bf16[32,16,128]{2,1,0:T(8,128)(2,1)S(1)}, u32[]{:S(2)}, u32[]{:S(2)}) %all-to-all-start.1) | async-done | bytes 131104 | tf_op jit(solution)/shard_map/all_to_all | solution.py:22
  69.9 0.2 fusion.3
  70.0 0.7 copy.30
  70.7 3.9 %all-to-all-start.2 = ((bf16[32,16,128]{2,1,0:T(8,128)(2,1)}), bf16[32,16,128]{2,1,0:T(8,128)(2,1)S(1)}, u32[]{:S(2)}, u32[]{:S(2)}) async-start(bf16[32,16,128]{2,1,0:T(8,128)(2,1)} %bitcast.46), calls=%async_computation.2 | async-start | bytes 262144 | tf_op jit(solution)/shard_map/all_to_all | solution.py:29
  74.6 3.7 %fusion.1 = f32[1,512,4,128]{1,3,2,0:T(8,128)} fusion(pred[512,512]{1,0:T(8,128)(4,1)S(1)} %iota_compare_fusion, bf16[1,512,3,4,128]{1,4,3,2,0:T(8,128)(2,1)} %bitcast.81), kind=kOutput, calls=%fused_computation.4 | convolution fusion | flops 538968064 | bytes 2883584 | tf_op jit(solution)/shard_map/bhqk,bkhe->bqhe/dot_general | solution.py:79
  78.3 0.0 copy-start.1
  78.3 5.7 %all-to-all-done.2 = bf16[32,16,128]{2,1,0:T(8,128)(2,1)S(1)} async-done(((bf16[32,16,128]{2,1,0:T(8,128)(2,1)}), bf16[32,16,128]{2,1,0:T(8,128)(2,1)S(1)}, u32[]{:S(2)}, u32[]{:S(2)}) %all-to-all-start.2) | async-done | bytes 131104 | tf_op jit(solution)/shard_map/all_to_all | solution.py:29
  84.0 1.7 %multiply_reduce_fusion = (f32[512,4]{0,1:T(4,128)S(1)}, f32[1,512,4,128]{1,3,2,0:T(8,128)S(1)}) fusion(f32[1,512,4,128]{1,3,2,0:T(8,128)} %fusion.1, bf16[4,128,128]{2,1,0:T(8,128)(2,1)S(1)} %bitcast.88, bf16[1,512,3,4,128]{1,4,3,2,0:T(8,128)(2,1)} %bitcast.82), kind=kOutput, calls=%fused_computation.16 | convolution fusion | flops 67893248 | bytes 2760704 | tf_op jit(solution)/shard_map/bqhd,bhde->bqhe/dot_general | solution.py:81
  85.8 0.0 copy-done.1
  85.8 1.0 %multiply_convert_fusion = bf16[1,512,4,128]{1,3,2,0:T(8,128)(2,1)} fusion(f32[1,512,4,128]{1,3,2,0:T(8,128)S(1)} %get-tuple-element.6, f32[4,128]{1,0:T(4,128)S(1)} %bitcast.95, f32[512,4]{0,1:T(4,128)S(1)} %add_rsqrt_fusion), kind=kLoop, calls=%fused_computation.15 | loop fusion | flops 786432 | bytes 1583104 | tf_op jit(solution)/shard_map/convert_element_type | solution.py:87
  86.7 2.0 %copy.25 = bf16[512,512]{1,0:T(8,128)(2,1)} copy(bf16[512,512]{0,1:T(8,128)(2,1)} %bitcast.85) | data formatting | bytes 1048576 | tf_op jit(solution)/shard_map/convert_element_type | solution.py:87
  (1 shorter events, 0.0 us)
Async XLA Ops:
  0.0 27.9 %copy-start = (bf16[3072,512]{1,0:T(8,128)(2,1)S(1)}, bf16[3072,512]{1,0:T(8,128)(2,1)}, u32[]{:S(2)}) copy-start(bf16[3072,512]{1,0:T(8,128)(2,1)} %param.8) | copy-start | bytes 9437188
  25.3 10.2 %collective-permute-start = (bf16[4,64,3072]{2,1,0:T(8,128)(2,1)}, bf16[4,64,3072]{2,1,0:T(8,128)(2,1)}, u32[]{:S(2)}, u32[]{:S(2)}) collective-permute-start(bf16[4,64,3072]{2,1,0:T(8,128)(2,1)} %all_to_all.15), channel_id=1, source_target_pairs={{0,1},{1,0},{2,3},{3,2},{4,5},{5,4},{6,7},{7,6},{8,9},{9,8},{10,11... | collective-permute-start | bytes 4718600 | tf_op jit(solution)/shard_map/ppermute | solution.py:43
  27.9 2.5 %copy-start.2 = (bf16[3072,512]{1,0:T(8,128)(2,1)S(1)}, bf16[3072,512]{1,0:T(8,128)(2,1)}, u32[]{:S(2)}) copy-start(bf16[3072,512]{1,0:T(8,128)(2,1)} %param.7) | copy-start | bytes 9437188
  30.5 2.6 %copy-start.3 = (bf16[3072,512]{1,0:T(8,128)(2,1)S(1)}, bf16[3072,512]{1,0:T(8,128)(2,1)}, u32[]{:S(2)}) copy-start(bf16[3072,512]{1,0:T(8,128)(2,1)} %param.6) | copy-start | bytes 9437188
  48.9 21.0 %all-to-all-start.1 = ((bf16[32,16,128]{2,1,0:T(8,128)(2,1)}), bf16[32,16,128]{2,1,0:T(8,128)(2,1)S(1)}, u32[]{:S(2)}, u32[]{:S(2)}) async-start(bf16[32,16,128]{2,1,0:T(8,128)(2,1)} %bitcast.29), calls=%async_computation.1 | async-start | bytes 262144 | tf_op jit(solution)/shard_map/all_to_all | solution.py:22
  70.7 13.3 %all-to-all-start.2 = ((bf16[32,16,128]{2,1,0:T(8,128)(2,1)}), bf16[32,16,128]{2,1,0:T(8,128)(2,1)S(1)}, u32[]{:S(2)}, u32[]{:S(2)}) async-start(bf16[32,16,128]{2,1,0:T(8,128)(2,1)} %bitcast.46), calls=%async_computation.2 | async-start | bytes 262144 | tf_op jit(solution)/shard_map/all_to_all | solution.py:29
  78.3 7.5 %copy-start.1 = (f32[512]{0:T(512)S(1)}, f32[512]{0:T(512)}, u32[]{:S(2)}) copy-start(f32[512]{0:T(512)} %param.9) | copy-start | bytes 6148

commit v12 on v7

--- a/solution.py
+++ b/solution.py
@@ -1,6 +1,7 @@
 import jax
 import jax.numpy as jnp
 from jax import lax
+from jax.experimental import pallas as pl
 from jax.sharding import Mesh, PartitionSpec as P
 
 HEAD_DIM = 128
@@ -73,13 +74,40 @@
     scores = jnp.where(causal[None, None], scores, jnp.float32(0.0)).astype(jnp.bfloat16)
     inner = jnp.einsum("bhqk,bkhe->bqhe", scores, value_rows, preferred_element_type=jnp.float32)
     inner = lax.optimization_barrier(inner)
-    carried_part = jnp.einsum(
-        "bqhd,bhde->bqhe", query_rows, block_start, preferred_element_type=jnp.float32
+    out = finish(
+        query_rows.reshape(group_len, local_width),
+        block_start.reshape(block_count * head_count, HEAD_DIM, HEAD_DIM),
+        inner.reshape(group_len, local_width),
+        norm_gain.reshape(1, local_width),
+        head_count,
     )
-    mixed = inner + carried_part
+    return out
+
+
+def finish_kernel(query_ref, start_ref, inner_ref, gain_ref, out_ref):
+    carried = jnp.dot(query_ref[...], start_ref[0], preferred_element_type=jnp.float32)
+    mixed = inner_ref[...] + carried
     mean_square = jnp.mean(mixed * mixed, axis=-1, keepdims=True)
-    normed = mixed * lax.rsqrt(mean_square + EPSILON) * norm_gain.reshape(head_count, HEAD_DIM)
-    return normed.reshape(group_len, local_width).astype(jnp.bfloat16)
+    normed = mixed * lax.rsqrt(mean_square + EPSILON) * gain_ref[...]
+    out_ref[...] = normed.astype(out_ref.dtype)
+
+
+def finish(query, start, inner, gain, head_count):
+    rows = query.shape[0]
+    blocks = rows // BLOCK
+    tile = pl.BlockSpec((BLOCK, HEAD_DIM), lambda b, h: (b, h))
+    return pl.pallas_call(
+        finish_kernel,
+        out_shape=jax.ShapeDtypeStruct(query.shape, jnp.bfloat16),
+        grid=(blocks, head_count),
+        in_specs=[
+            tile,
+            pl.BlockSpec((1, HEAD_DIM, HEAD_DIM), lambda b, h: (b * head_count + h, 0, 0)),
+            tile,
+            pl.BlockSpec((1, HEAD_DIM), lambda b, h: (0, h)),
+        ],
+        out_specs=tile,
+    )(query, start, inner, gain)
 
 
 def chip_split(mesh):

time: 82.6 us -> 82.7 us (level)
  waiting for transfers between devices: 14.9 us -> 8.43 us
  local copies, waits for them, and re-layouts: 5.82 us -> 10.9 us
  Pallas kernels: 0 us -> 4.01 us
  matrix products: 12.1 us -> 10.4 us
  other arithmetic: 1.14 us -> 0.18 us
    all_to_all x1, waiting for transfers between devices: 5.61 us -> 1.04 us  [exclusive_scan(): lax.all_to_all(before.reshape(pieces.shape), axis, 0, 0, tiled=True)]
    pallas_call x0 -> x1, Pallas kernels: none -> 4.01 us  [finish(): pl.pallas_call(finish_kernel, out_shape=jax.ShapeDtypeStruct(query.shape,...]
    reshape x0 -> x1, local copies, waits for them, and re-layouts: none -> 2.53 us  [body(): inner.reshape(group_len, local_width)]
    another operation x0 -> x1, local copies, waits for them, and re-layouts: none -> 2.06 us  [body(): query_rows.reshape(group_len, local_width)]
    convert_element_type x1 -> x0, local copies, waits for them, and re-layouts: 2.05 us -> none  [body(): return normed.reshape(group_len, local_width).astype(jnp.bfloat16)]
    all_to_all x1, waiting for transfers between devices: 9.26 us -> 7.39 us  [exclusive_scan(): gathered = lax.all_to_all(pieces, axis, 0, 0, tiled=True)]
    slice x0 -> x1, local copies, waits for them, and re-layouts: none -> 1.87 us  [body(): query_rows = shaped[:, :, 0]]
    dot_general x1 -> x0, matrix products: 1.75 us -> none  [body(): jnp.einsum('bqhd,bhde->bqhe', query_rows, block_start, preferred_element_...]
  transfers between devices with their start and end apart: 2 -> 2, of which waited for: 2 -> 2; matrix products, arithmetic and copies ran while one was open for 5% -> 13% of each run, Pallas kernels for 0% -> 0%
where the time goes in v12:
time: 82.7 us; the launch traced here: 81.2 us
  blocking collectives  32.4 us (39%)
  starting transfers between devices  14.9 us (18%)
  local copies, waits for them, and re-layouts  10.9 us (13%)
  matrix products  10.4 us (13%)
  waiting for transfers between devices  8.43 us (10%)
  Pallas kernels  4.01 us (5%)
    all_to_all x2, blocking collectives, spread(): return lax.all_to_all(copies, axis, 0, 0, tiled=True)  32.4 us
    all_to_all x1, starting transfers between devices, exclusive_scan(): gathered = lax.all_to_all(pieces, axis, 0, 0, tiled=True)  11 us
    all_to_all x1, waiting for transfers between devices, exclusive_scan(): gathered = lax.all_to_all(pieces, axis, 0, 0, tiled=True)  7.39 us
    pallas_call x1, Pallas kernels, finish(): pl.pallas_call(finish_kernel, out_shape=jax.ShapeDtypeStruct(query.shape,...  4.01 us
    all_to_all x1, starting transfers between devices, exclusive_scan(): lax.all_to_all(before.reshape(pieces.shape), axis, 0, 0, tiled=True)  3.87 us
    dot_general x1, matrix products, body(): jnp.einsum('bhqk,bkhe->bqhe', scores, value_rows, preferred_element_type=...  3.71 us
    unnamed x11, local copies, waits for them, and re-layouts  2.53 us
    reshape x1, local copies, waits for them, and re-layouts, body(): inner.reshape(group_len, local_width)  2.53 us
  transfers between devices with their start and end apart: 2, of which 2 were waited for; matrix products, arithmetic and copies ran while one was open for 13% of the time, Pallas kernels for 0%

profile of v12, /device:TPU:1, one launch (start us, length us, event | category | flops | bytes accessed | tf_op | source)
XLA Modules:
  0.0 81.2 jit_solution(6328526672221356834)
XLA Ops:
  0.0 0.0 copy-start
  0.0 1.3 %broadcast_in_dim.12 = bf16[4,64,3072]{2,1,0:T(8,128)(2,1)S(1)} broadcast(bf16[64,3072]{1,0:T(8,128)(2,1)} %param.5), dimensions={1,2} | broadcast | bytes 1966080 | tf_op jit(solution)/shard_map/broadcast_in_dim | solution.py:36
  1.3 24.7 %all_to_all.20 = bf16[4,64,3072]{2,1,0:T(8,128)(2,1)S(1)} all-to-all(bf16[4,64,3072]{2,1,0:T(8,128)(2,1)S(1)} %broadcast_in_dim.12), channel_id=1, replica_groups=mesh['ctx'=32,'y'=4,'core'=2] {'y'}, dimensions={0} | all-to-all | bytes 3145728 | tf_op jit(solution)/shard_map/all_to_all | solution.py:37
  26.0 0.4 broadcast_in_dim.13
  26.4 7.7 %all_to_all.21 = bf16[2,4,64,3072]{3,2,1,0:T(8,128)(2,1)S(1)} all-to-all(bf16[2,4,64,3072]{3,2,1,0:T(8,128)(2,1)S(1)} %broadcast_in_dim.13), channel_id=1, replica_groups=mesh['ctx'=32,'y'=4,'core'=2] {'core'}, dimensions={0} | all-to-all | bytes 6291456 | tf_op jit(solution)/shard_map/all_to_all | solution.py:37
  34.1 0.2 copy.14
  34.3 0.0 copy-done
  34.3 0.0 copy-start.3
  34.3 1.9 %convolution_convert_fusion.1 = bf16[512,512]{0,1:T(8,128)(2,1)S(1)} fusion(bf16[512,3072]{1,0:T(8,128)(2,1)S(1)} %bitcast.41, bf16[3072,512]{1,0:T(8,128)(2,1)S(1)} %copy-done), kind=kOutput, calls=%fused_computation.5 | convolution fusion | flops 1610874880 | bytes 6815744 | tf_op jit(solution)/shard_map/dot_general | solution.py:54
  36.2 0.0 copy-done.3
  36.2 0.0 copy-start.4
  36.2 1.8 %convolution_convert_fusion.2 = bf16[512,512]{0,1:T(8,128)(2,1)S(1)} fusion(bf16[512,3072]{1,0:T(8,128)(2,1)S(1)} %bitcast.42, bf16[3072,512]{1,0:T(8,128)(2,1)S(1)} %copy-done.3), kind=kOutput, calls=%fused_computation.6 | convolution fusion | flops 1610874880 | bytes 6815744 | tf_op jit(solution)/shard_map/dot_general | solution.py:53
  38.0 0.0 copy-done.4
  38.1 1.8 %convolution_convert_fusion.3 = bf16[512,512]{0,1:T(8,128)(2,1)S(1)} fusion(bf16[512,3072]{1,0:T(8,128)(2,1)S(1)} %bitcast.43, bf16[3072,512]{1,0:T(8,128)(2,1)S(1)} %copy-done.4), kind=kOutput, calls=%fused_computation.7 | convolution fusion | flops 1610874880 | bytes 6815744 | tf_op jit(solution)/shard_map/dot_general | solution.py:50
  39.9 0.1 pad_maximum_fusion
  40.0 0.0 copy-start.1
  40.0 1.1 %copy-done.1 = bf16[512,1536]{0,1:T(8,128)(2,1)} copy-done((bf16[512,1536]{0,1:T(8,128)(2,1)}, bf16[512,1536]{0,1:T(8,128)(2,1)S(1)}, u32[]{:S(2)}) %copy-start.1) | copy-done | bytes 1572888
  41.2 1.0 %convolution_convert_fusion.4 = bf16[4,128,128]{2,1,0:T(8,128)(2,1)} fusion(bf16[1,512,3,4,128]{1,4,3,2,0:T(8,128)(2,1)S(1)} %bitcast.44), kind=kOutput, calls=%fused_computation.8 | convolution fusion | flops 67174400 | bytes 1179648 | tf_op jit(solution)/shard_map/bshd,bshe->bhde/dot_general | solution.py:64
  42.1 11.0 %all-to-all-start.2 = ((bf16[32,16,128]{2,1,0:T(8,128)(2,1)}), bf16[32,16,128]{2,1,0:T(8,128)(2,1)S(1)}, u32[]{:S(2)}, u32[]{:S(2)}) async-start(bf16[32,16,128]{2,1,0:T(8,128)(2,1)} %bitcast.7), calls=%async_computation.2 | async-start | bytes 262144 | tf_op jit(solution)/shard_map/all_to_all | solution.py:23
  53.2 0.1 iota_compare_fusion
  53.2 1.9 %slice.12 = bf16[1,512,1,4,128]{1,4,3,2,0:T(8,128)(2,1)} slice(bf16[1,512,3,4,128]{1,4,3,2,0:T(8,128)(2,1)} %bitcast.45), slice={[0:1], [0:512], [0:1], [0:4], [0:128]} | slice | bytes 1048576 | tf_op jit(solution)/shard_map/slice | solution.py:61
  55.1 7.4 %all-to-all-done.2 = bf16[32,16,128]{2,1,0:T(8,128)(2,1)S(1)} async-done(((bf16[32,16,128]{2,1,0:T(8,128)(2,1)}), bf16[32,16,128]{2,1,0:T(8,128)(2,1)S(1)}, u32[]{:S(2)}, u32[]{:S(2)}) %all-to-all-start.2) | async-done | bytes 131104 | tf_op jit(solution)/shard_map/all_to_all | solution.py:23
  62.5 0.2 fusion.2
  62.7 0.7 copy.28
  63.4 3.9 %all-to-all-start.3 = ((bf16[32,16,128]{2,1,0:T(8,128)(2,1)}), bf16[32,16,128]{2,1,0:T(8,128)(2,1)S(1)}, u32[]{:S(2)}, u32[]{:S(2)}) async-start(bf16[32,16,128]{2,1,0:T(8,128)(2,1)} %bitcast.20), calls=%async_computation.3 | async-start | bytes 262144 | tf_op jit(solution)/shard_map/all_to_all | solution.py:30
  67.2 3.7 %fusion.1 = f32[1,512,4,128]{1,3,2,0:T(8,128)} fusion(pred[512,512]{1,0:T(8,128)(4,1)S(1)} %iota_compare_fusion, bf16[1,512,3,4,128]{1,4,3,2,0:T(8,128)(2,1)} %bitcast.46), kind=kOutput, calls=%fused_computation.4 | convolution fusion | flops 538968064 | bytes 2883584 | tf_op jit(solution)/shard_map/bhqk,bkhe->bqhe/dot_general | solution.py:75
  70.9 2.5 %copy.25.inner_ref = f32[512,512]{1,0:T(8,128)} copy(f32[512,512]{0,1:T(8,128)} %bitcast.48) | data formatting | bytes 2097152 | tf_op jit(solution)/shard_map/reshape | solution.py:80
  73.5 2.1 %copy.24.query_ref = bf16[512,512]{1,0:T(8,128)(2,1)} copy(bf16[512,512]{0,1:T(8,128)(2,1)} %bitcast.47) | data formatting | bytes 1048576 | tf_op jit(solution)/shard_map/reshape;squeeze | solution.py:78
  75.5 1.0 %all-to-all-done.3 = bf16[32,16,128]{2,1,0:T(8,128)(2,1)S(1)} async-done(((bf16[32,16,128]{2,1,0:T(8,128)(2,1)}), bf16[32,16,128]{2,1,0:T(8,128)(2,1)S(1)}, u32[]{:S(2)}, u32[]{:S(2)}) %all-to-all-start.3) | async-done | bytes 131104 | tf_op jit(solution)/shard_map/all_to_all | solution.py:30
  76.6 0.0 copy-start.2
  76.6 0.7 copy-done.2
  77.2 4.0 %shard_map.55 = bf16[512,512]{1,0:T(8,128)(2,1)} custom-call(bf16[512,512]{1,0:T(8,128)(2,1)} %copy.24.query_ref, bf16[4,128,128]{2,1,0:T(8,128)(2,1)} %bitcast.49, f32[512,512]{1,0:T(8,128)} %copy.25.inner_ref, f32[1,512]{1,0:T(1,128)} %bitcast.51), custom_call_target="tpu_custom_call" | custom-call | tf_op jit(solution)/shard_map/pallas_call | solution.py:99
Async XLA Ops:
  0.0 34.3 %copy-start = (bf16[3072,512]{1,0:T(8,128)(2,1)S(1)}, bf16[3072,512]{1,0:T(8,128)(2,1)}, u32[]{:S(2)}) copy-start(bf16[3072,512]{1,0:T(8,128)(2,1)} %param.8) | copy-start | bytes 9437188
  34.3 1.9 %copy-start.3 = (bf16[3072,512]{1,0:T(8,128)(2,1)S(1)}, bf16[3072,512]{1,0:T(8,128)(2,1)}, u32[]{:S(2)}) copy-start(bf16[3072,512]{1,0:T(8,128)(2,1)} %param.7) | copy-start | bytes 9437188
  36.2 1.9 %copy-start.4 = (bf16[3072,512]{1,0:T(8,128)(2,1)S(1)}, bf16[3072,512]{1,0:T(8,128)(2,1)}, u32[]{:S(2)}) copy-start(bf16[3072,512]{1,0:T(8,128)(2,1)} %param.6) | copy-start | bytes 9437188
  40.0 1.1 %copy-start.1 = (bf16[512,1536]{0,1:T(8,128)(2,1)}, bf16[512,1536]{0,1:T(8,128)(2,1)S(1)}, u32[]{:S(2)}) copy-start(bf16[512,1536]{0,1:T(8,128)(2,1)S(1)} %pad_maximum_fusion) | copy-start | bytes 4718596
  42.1 20.4 %all-to-all-start.2 = ((bf16[32,16,128]{2,1,0:T(8,128)(2,1)}), bf16[32,16,128]{2,1,0:T(8,128)(2,1)S(1)}, u32[]{:S(2)}, u32[]{:S(2)}) async-start(bf16[32,16,128]{2,1,0:T(8,128)(2,1)} %bitcast.7), calls=%async_computation.2 | async-start | bytes 262144 | tf_op jit(solution)/shard_map/all_to_all | solution.py:23
  63.4 13.2 %all-to-all-start.3 = ((bf16[32,16,128]{2,1,0:T(8,128)(2,1)}), bf16[32,16,128]{2,1,0:T(8,128)(2,1)S(1)}, u32[]{:S(2)}, u32[]{:S(2)}) async-start(bf16[32,16,128]{2,1,0:T(8,128)(2,1)} %bitcast.20), calls=%async_computation.3 | async-start | bytes 262144 | tf_op jit(solution)/shard_map/all_to_all | solution.py:30
  76.6 0.7 copy-start.2

commit v13 on v12

--- a/solution.py
+++ b/solution.py
@@ -85,26 +85,30 @@
 
 
 def finish_kernel(query_ref, start_ref, inner_ref, gain_ref, out_ref):
-    carried = jnp.dot(query_ref[...], start_ref[0], preferred_element_type=jnp.float32)
-    mixed = inner_ref[...] + carried
-    mean_square = jnp.mean(mixed * mixed, axis=-1, keepdims=True)
-    normed = mixed * lax.rsqrt(mean_square + EPSILON) * gain_ref[...]
-    out_ref[...] = normed.astype(out_ref.dtype)
+    for head in range(start_ref.shape[0]):
+        lanes = slice(head * HEAD_DIM, (head + 1) * HEAD_DIM)
+        carried = jnp.dot(
+            query_ref[:, lanes], start_ref[head], preferred_element_type=jnp.float32
+        )
+        mixed = inner_ref[:, lanes] + carried
+        mean_square = jnp.mean(mixed * mixed, axis=-1, keepdims=True)
+        normed = mixed * lax.rsqrt(mean_square + EPSILON) * gain_ref[:, lanes]
+        out_ref[:, lanes] = normed.astype(out_ref.dtype)
 
 
 def finish(query, start, inner, gain, head_count):
-    rows = query.shape[0]
+    rows, width = query.shape
     blocks = rows // BLOCK
-    tile = pl.BlockSpec((BLOCK, HEAD_DIM), lambda b, h: (b, h))
+    tile = pl.BlockSpec((BLOCK, width), lambda b: (b, 0))
     return pl.pallas_call(
         finish_kernel,
         out_shape=jax.ShapeDtypeStruct(query.shape, jnp.bfloat16),
-        grid=(blocks, head_count),
+        grid=(blocks,),
         in_specs=[
             tile,
-            pl.BlockSpec((1, HEAD_DIM, HEAD_DIM), lambda b, h: (b * head_count + h, 0, 0)),
+            pl.BlockSpec((head_count, HEAD_DIM, HEAD_DIM), lambda b: (b, 0, 0)),
             tile,
-            pl.BlockSpec((1, HEAD_DIM), lambda b, h: (0, h)),
+            pl.BlockSpec((1, width), lambda b: (0, 0)),
         ],
         out_specs=tile,
     )(query, start, inner, gain)

time: 82.7 us -> 81.4 us (0.984)
  Pallas kernels: 4.01 us -> 2.76 us
    pallas_call x1, Pallas kernels: 4.01 us -> 2.76 us  [finish(): pl.pallas_call(finish_kernel, out_shape=jax.ShapeDtypeStruct(query.shape,...]
where the time goes in v13:
time: 81.4 us; the launch traced here: 80 us
  blocking collectives  32.4 us (40%)
  starting transfers between devices  14.9 us (18%)
  local copies, waits for them, and re-layouts  10.9 us (13%)
  matrix products  10.4 us (13%)
  waiting for transfers between devices  8.43 us (10%)
  Pallas kernels  2.76 us (3%)
    all_to_all x2, blocking collectives, spread(): return lax.all_to_all(copies, axis, 0, 0, tiled=True)  32.4 us
    all_to_all x1, starting transfers between devices, exclusive_scan(): gathered = lax.all_to_all(pieces, axis, 0, 0, tiled=True)  11 us
    all_to_all x1, waiting for transfers between devices, exclusive_scan(): gathered = lax.all_to_all(pieces, axis, 0, 0, tiled=True)  7.39 us
    all_to_all x1, starting transfers between devices, exclusive_scan(): lax.all_to_all(before.reshape(pieces.shape), axis, 0, 0, tiled=True)  3.87 us
    dot_general x1, matrix products, body(): jnp.einsum('bhqk,bkhe->bqhe', scores, value_rows, preferred_element_type=...  3.71 us
    pallas_call x1, Pallas kernels, finish(): pl.pallas_call(finish_kernel, out_shape=jax.ShapeDtypeStruct(query.shape,...  2.76 us
    unnamed x11, local copies, waits for them, and re-layouts  2.53 us
    reshape x1, local copies, waits for them, and re-layouts, body(): inner.reshape(group_len, local_width)  2.53 us
  transfers between devices with their start and end apart: 2, of which 2 were waited for; matrix products, arithmetic and copies ran while one was open for 13% of the time, Pallas kernels for 0%

profile of v13, /device:TPU:1, one launch (start us, length us, event | category | flops | bytes accessed | tf_op | source)
XLA Modules:
  0.0 80.0 jit_solution(14946882188951571106)
XLA Ops:
  0.0 0.0 copy-start
  0.0 1.3 %broadcast_in_dim.12 = bf16[4,64,3072]{2,1,0:T(8,128)(2,1)S(1)} broadcast(bf16[64,3072]{1,0:T(8,128)(2,1)} %param.5), dimensions={1,2} | broadcast | bytes 1966080 | tf_op jit(solution)/shard_map/broadcast_in_dim | solution.py:36
  1.3 24.7 %all_to_all.20 = bf16[4,64,3072]{2,1,0:T(8,128)(2,1)S(1)} all-to-all(bf16[4,64,3072]{2,1,0:T(8,128)(2,1)S(1)} %broadcast_in_dim.12), channel_id=1, replica_groups=mesh['ctx'=32,'y'=4,'core'=2] {'y'}, dimensions={0} | all-to-all | bytes 3145728 | tf_op jit(solution)/shard_map/all_to_all | solution.py:37
  26.0 0.4 broadcast_in_dim.13
  26.4 7.7 %all_to_all.21 = bf16[2,4,64,3072]{3,2,1,0:T(8,128)(2,1)S(1)} all-to-all(bf16[2,4,64,3072]{3,2,1,0:T(8,128)(2,1)S(1)} %broadcast_in_dim.13), channel_id=1, replica_groups=mesh['ctx'=32,'y'=4,'core'=2] {'core'}, dimensions={0} | all-to-all | bytes 6291456 | tf_op jit(solution)/shard_map/all_to_all | solution.py:37
  34.1 0.2 copy.14
  34.3 0.0 copy-done
  34.3 0.0 copy-start.3
  34.3 1.9 %convolution_convert_fusion.1 = bf16[512,512]{0,1:T(8,128)(2,1)S(1)} fusion(bf16[512,3072]{1,0:T(8,128)(2,1)S(1)} %bitcast.41, bf16[3072,512]{1,0:T(8,128)(2,1)S(1)} %copy-done), kind=kOutput, calls=%fused_computation.5 | convolution fusion | flops 1610874880 | bytes 6815744 | tf_op jit(solution)/shard_map/dot_general | solution.py:54
  36.2 0.0 copy-done.3
  36.2 0.0 copy-start.4
  36.2 1.8 %convolution_convert_fusion.2 = bf16[512,512]{0,1:T(8,128)(2,1)S(1)} fusion(bf16[512,3072]{1,0:T(8,128)(2,1)S(1)} %bitcast.42, bf16[3072,512]{1,0:T(8,128)(2,1)S(1)} %copy-done.3), kind=kOutput, calls=%fused_computation.6 | convolution fusion | flops 1610874880 | bytes 6815744 | tf_op jit(solution)/shard_map/dot_general | solution.py:53
  38.0 0.0 copy-done.4
  38.1 1.8 %convolution_convert_fusion.3 = bf16[512,512]{0,1:T(8,128)(2,1)S(1)} fusion(bf16[512,3072]{1,0:T(8,128)(2,1)S(1)} %bitcast.43, bf16[3072,512]{1,0:T(8,128)(2,1)S(1)} %copy-done.4), kind=kOutput, calls=%fused_computation.7 | convolution fusion | flops 1610874880 | bytes 6815744 | tf_op jit(solution)/shard_map/dot_general | solution.py:50
  39.9 0.1 pad_maximum_fusion
  40.0 0.0 copy-start.1
  40.0 1.1 %copy-done.1 = bf16[512,1536]{0,1:T(8,128)(2,1)} copy-done((bf16[512,1536]{0,1:T(8,128)(2,1)}, bf16[512,1536]{0,1:T(8,128)(2,1)S(1)}, u32[]{:S(2)}) %copy-start.1) | copy-done | bytes 1572888
  41.2 1.0 %convolution_convert_fusion.4 = bf16[4,128,128]{2,1,0:T(8,128)(2,1)} fusion(bf16[1,512,3,4,128]{1,4,3,2,0:T(8,128)(2,1)S(1)} %bitcast.44), kind=kOutput, calls=%fused_computation.8 | convolution fusion | flops 67174400 | bytes 1179648 | tf_op jit(solution)/shard_map/bshd,bshe->bhde/dot_general | solution.py:64
  42.1 11.0 %all-to-all-start.2 = ((bf16[32,16,128]{2,1,0:T(8,128)(2,1)}), bf16[32,16,128]{2,1,0:T(8,128)(2,1)S(1)}, u32[]{:S(2)}, u32[]{:S(2)}) async-start(bf16[32,16,128]{2,1,0:T(8,128)(2,1)} %bitcast.7), calls=%async_computation.2 | async-start | bytes 262144 | tf_op jit(solution)/shard_map/all_to_all | solution.py:23
  53.2 0.1 iota_compare_fusion
  53.2 1.9 %slice.12 = bf16[1,512,1,4,128]{1,4,3,2,0:T(8,128)(2,1)} slice(bf16[1,512,3,4,128]{1,4,3,2,0:T(8,128)(2,1)} %bitcast.45), slice={[0:1], [0:512], [0:1], [0:4], [0:128]} | slice | bytes 1048576 | tf_op jit(solution)/shard_map/slice | solution.py:61
  55.1 7.4 %all-to-all-done.2 = bf16[32,16,128]{2,1,0:T(8,128)(2,1)S(1)} async-done(((bf16[32,16,128]{2,1,0:T(8,128)(2,1)}), bf16[32,16,128]{2,1,0:T(8,128)(2,1)S(1)}, u32[]{:S(2)}, u32[]{:S(2)}) %all-to-all-start.2) | async-done | bytes 131104 | tf_op jit(solution)/shard_map/all_to_all | solution.py:23
  62.5 0.2 fusion.2
  62.7 0.7 copy.28
  63.4 3.9 %all-to-all-start.3 = ((bf16[32,16,128]{2,1,0:T(8,128)(2,1)}), bf16[32,16,128]{2,1,0:T(8,128)(2,1)S(1)}, u32[]{:S(2)}, u32[]{:S(2)}) async-start(bf16[32,16,128]{2,1,0:T(8,128)(2,1)} %bitcast.20), calls=%async_computation.3 | async-start | bytes 262144 | tf_op jit(solution)/shard_map/all_to_all | solution.py:30
  67.2 3.7 %fusion.1 = f32[1,512,4,128]{1,3,2,0:T(8,128)} fusion(pred[512,512]{1,0:T(8,128)(4,1)S(1)} %iota_compare_fusion, bf16[1,512,3,4,128]{1,4,3,2,0:T(8,128)(2,1)} %bitcast.46), kind=kOutput, calls=%fused_computation.4 | convolution fusion | flops 538968064 | bytes 2883584 | tf_op jit(solution)/shard_map/bhqk,bkhe->bqhe/dot_general | solution.py:75
  70.9 2.5 %copy.25.inner_ref = f32[512,512]{1,0:T(8,128)} copy(f32[512,512]{0,1:T(8,128)} %bitcast.48) | data formatting | bytes 2097152 | tf_op jit(solution)/shard_map/reshape | solution.py:80
  73.5 2.1 %copy.24.query_ref = bf16[512,512]{1,0:T(8,128)(2,1)} copy(bf16[512,512]{0,1:T(8,128)(2,1)} %bitcast.47) | data formatting | bytes 1048576 | tf_op jit(solution)/shard_map/reshape;squeeze | solution.py:78
  75.5 1.0 %all-to-all-done.3 = bf16[32,16,128]{2,1,0:T(8,128)(2,1)S(1)} async-done(((bf16[32,16,128]{2,1,0:T(8,128)(2,1)}), bf16[32,16,128]{2,1,0:T(8,128)(2,1)S(1)}, u32[]{:S(2)}, u32[]{:S(2)}) %all-to-all-start.3) | async-done | bytes 131104 | tf_op jit(solution)/shard_map/all_to_all | solution.py:30
  76.6 0.0 copy-start.2
  76.6 0.7 copy-done.2
  77.2 2.8 %shard_map.55 = bf16[512,512]{1,0:T(8,128)(2,1)} custom-call(bf16[512,512]{1,0:T(8,128)(2,1)} %copy.24.query_ref, bf16[4,128,128]{2,1,0:T(8,128)(2,1)} %bitcast.49, f32[512,512]{1,0:T(8,128)} %copy.25.inner_ref, f32[1,512]{1,0:T(1,128)} %bitcast.51), custom_call_target="tpu_custom_call" | custom-call | tf_op jit(solution)/shard_map/pallas_call | solution.py:103
Async XLA Ops:
  0.0 34.3 %copy-start = (bf16[3072,512]{1,0:T(8,128)(2,1)S(1)}, bf16[3072,512]{1,0:T(8,128)(2,1)}, u32[]{:S(2)}) copy-start(bf16[3072,512]{1,0:T(8,128)(2,1)} %param.8) | copy-start | bytes 9437188
  34.3 1.9 %copy-start.3 = (bf16[3072,512]{1,0:T(8,128)(2,1)S(1)}, bf16[3072,512]{1,0:T(8,128)(2,1)}, u32[]{:S(2)}) copy-start(bf16[3072,512]{1,0:T(8,128)(2,1)} %param.7) | copy-start | bytes 9437188
  36.2 1.9 %copy-start.4 = (bf16[3072,512]{1,0:T(8,128)(2,1)S(1)}, bf16[3072,512]{1,0:T(8,128)(2,1)}, u32[]{:S(2)}) copy-start(bf16[3072,512]{1,0:T(8,128)(2,1)} %param.6) | copy-start | bytes 9437188
  40.0 1.1 %copy-start.1 = (bf16[512,1536]{0,1:T(8,128)(2,1)}, bf16[512,1536]{0,1:T(8,128)(2,1)S(1)}, u32[]{:S(2)}) copy-start(bf16[512,1536]{0,1:T(8,128)(2,1)S(1)} %pad_maximum_fusion) | copy-start | bytes 4718596
  42.1 20.4 %all-to-all-start.2 = ((bf16[32,16,128]{2,1,0:T(8,128)(2,1)}), bf16[32,16,128]{2,1,0:T(8,128)(2,1)S(1)}, u32[]{:S(2)}, u32[]{:S(2)}) async-start(bf16[32,16,128]{2,1,0:T(8,128)(2,1)} %bitcast.7), calls=%async_computation.2 | async-start | bytes 262144 | tf_op jit(solution)/shard_map/all_to_all | solution.py:23
  63.4 13.2 %all-to-all-start.3 = ((bf16[32,16,128]{2,1,0:T(8,128)(2,1)}), bf16[32,16,128]{2,1,0:T(8,128)(2,1)S(1)}, u32[]{:S(2)}, u32[]{:S(2)}) async-start(bf16[32,16,128]{2,1,0:T(8,128)(2,1)} %bitcast.20), calls=%async_computation.3 | async-start | bytes 262144 | tf_op jit(solution)/shard_map/all_to_all | solution.py:30
  76.6 0.7 copy-start.2

commit v14 on v13

--- a/solution.py
+++ b/solution.py
@@ -54,13 +54,12 @@
     value_part = jnp.dot(piece_rows, w_value, preferred_element_type=jnp.float32).astype(
         jnp.bfloat16
     )
-    projected = jnp.concatenate([query_part, key_part, value_part], axis=1)
-    group_len = projected.shape[0]
+    group_len = query_part.shape[0]
     block_count = group_len // BLOCK
-    shaped = projected.reshape(block_count, BLOCK, 3, head_count, HEAD_DIM)
-    query_rows = shaped[:, :, 0]
-    key_rows = shaped[:, :, 1]
-    value_rows = shaped[:, :, 2]
+    query_rows, key_rows, value_rows = (
+        part.reshape(block_count, BLOCK, head_count, HEAD_DIM)
+        for part in (query_part, key_part, value_part)
+    )
     block_states = jnp.einsum(
         "bshd,bshe->bhde", key_rows, value_rows, preferred_element_type=jnp.float32
     )

time: 81.4 us -> 82.9 us (1.018); the launches traced: 80 us -> 82.4 us
  blocking collectives: 32.4 us -> 9.16 us
  waiting for transfers between devices: 8.43 us -> 25.5 us
  starting transfers between devices: 14.9 us -> 21.4 us
  matrix products: 10.4 us -> 13.9 us
  local copies, waits for them, and re-layouts: 10.9 us -> 9.46 us
    all_to_all x2 -> x1, blocking collectives: 32.4 us -> 9.16 us  [spread(): return lax.all_to_all(copies, axis, 0, 0, tiled=True)]
    all_to_all x0 -> x1, waiting for transfers between devices: none -> 18.5 us  [spread(): return lax.all_to_all(copies, axis, 0, 0, tiled=True)]
    all_to_all x0 -> x1, starting transfers between devices: none -> 5 us  [spread(): return lax.all_to_all(copies, axis, 0, 0, tiled=True)]
    dot_general x1, matrix products: 1.83 us -> 5.46 us  [body(): jnp.dot(piece_rows, w_query, preferred_element_type=jnp.float32)]
    all_to_all x1, waiting for transfers between devices: 7.39 us -> 3.89 us  [exclusive_scan(): gathered = lax.all_to_all(pieces, axis, 0, 0, tiled=True)]
    broadcast_in_dim x2, local copies, waits for them, and re-layouts: 1.69 us -> 4.26 us  [spread(): copies = jnp.broadcast_to(value[None], (size,) + value.shape)]
    all_to_all x1, waiting for transfers between devices: 1.04 us -> 3.13 us  [exclusive_scan(): lax.all_to_all(before.reshape(pieces.shape), axis, 0, 0, tiled=True)]
    another operation x1 -> x0, local copies, waits for them, and re-layouts: 2.06 us -> none  [body(): query_rows.reshape(group_len, local_width)]
  transfers between devices with their start and end apart: 2 -> 3, of which waited for: 2 -> 3; matrix products, arithmetic and copies ran while one was open for 13% -> 14% of each run, Pallas kernels for 0% -> 0%
where the time goes in v14:
time: 82.9 us; the launch traced here: 82.4 us
  waiting for transfers between devices  25.5 us (31%)
  starting transfers between devices  21.4 us (26%)
  matrix products  13.9 us (17%)
  local copies, waits for them, and re-layouts  9.46 us (11%)
  blocking collectives  9.16 us (11%)
  Pallas kernels  2.76 us (3%)
    all_to_all x1, waiting for transfers between devices, spread(): return lax.all_to_all(copies, axis, 0, 0, tiled=True)  18.5 us
    all_to_all x1, starting transfers between devices, exclusive_scan(): gathered = lax.all_to_all(pieces, axis, 0, 0, tiled=True)  11.1 us
    all_to_all x1, blocking collectives, spread(): return lax.all_to_all(copies, axis, 0, 0, tiled=True)  9.16 us
    dot_general x1, matrix products, body(): jnp.dot(piece_rows, w_query, preferred_element_type=jnp.float32)  5.46 us
    all_to_all x1, starting transfers between devices, exclusive_scan(): lax.all_to_all(before.reshape(pieces.shape), axis, 0, 0, tiled=True)  5.32 us
    all_to_all x1, starting transfers between devices, spread(): return lax.all_to_all(copies, axis, 0, 0, tiled=True)  5 us
    broadcast_in_dim x2, local copies, waits for them, and re-layouts, spread(): copies = jnp.broadcast_to(value[None], (size,) + value.shape)  4.26 us
    all_to_all x1, waiting for transfers between devices, exclusive_scan(): gathered = lax.all_to_all(pieces, axis, 0, 0, tiled=True)  3.89 us
  transfers between devices with their start and end apart: 3, of which 3 were waited for; matrix products, arithmetic and copies ran while one was open for 14% of the time, Pallas kernels for 0%

profile of v14, /device:TPU:1, one launch (start us, length us, event | category | flops | bytes accessed | tf_op | source)
XLA Modules:
  0.0 82.4 jit_solution(8542544393028765804)
XLA Ops:
  0.0 0.0 copy-start
  0.0 2.5 %broadcast_in_dim.12 = bf16[4,64,3072]{2,1,0:T(8,128)(2,1)} broadcast(bf16[64,3072]{1,0:T(8,128)(2,1)} %param.5), dimensions={1,2} | broadcast | bytes 1966080 | tf_op jit(solution)/shard_map/broadcast_in_dim | solution.py:36
  2.5 5.0 %all-to-all-start = ((bf16[4,64,3072]{2,1,0:T(8,128)(2,1)}), bf16[4,64,3072]{2,1,0:T(8,128)(2,1)}, u32[]{:S(2)}, u32[]{:S(2)}) async-start(bf16[4,64,3072]{2,1,0:T(8,128)(2,1)} %broadcast_in_dim.12), calls=%async_computation | async-start | bytes 3145728 | tf_op jit(solution)/shard_map/all_to_all | solution.py:37
  7.5 0.1 iota_compare_fusion
  7.6 18.5 %all-to-all-done = bf16[4,64,3072]{2,1,0:T(8,128)(2,1)} async-done(((bf16[4,64,3072]{2,1,0:T(8,128)(2,1)}), bf16[4,64,3072]{2,1,0:T(8,128)(2,1)}, u32[]{:S(2)}, u32[]{:S(2)}) %all-to-all-start) | async-done | bytes 1572896 | tf_op jit(solution)/shard_map/all_to_all | solution.py:37
  26.1 1.8 %broadcast_in_dim.13 = bf16[2,4,64,3072]{3,2,1,0:T(8,128)(2,1)S(1)} broadcast(bf16[4,64,3072]{2,1,0:T(8,128)(2,1)} %all-to-all-done), dimensions={1,2,3} | broadcast | bytes 4718592 | tf_op jit(solution)/shard_map/broadcast_in_dim | solution.py:36
  27.9 9.2 %all_to_all.20 = bf16[2,4,64,3072]{3,2,1,0:T(8,128)(2,1)S(1)} all-to-all(bf16[2,4,64,3072]{3,2,1,0:T(8,128)(2,1)S(1)} %broadcast_in_dim.13), channel_id=1, replica_groups=mesh['ctx'=32,'y'=4,'core'=2] {'core'}, dimensions={0} | all-to-all | bytes 6291456 | tf_op jit(solution)/shard_map/all_to_all | solution.py:37
  37.0 0.2 copy.12
  37.2 0.0 copy-start.1
  37.2 0.0 copy-done
  37.2 0.0 copy-start.5
  37.3 1.9 %convolution_convert_fusion.2 = bf16[512,512]{0,1:T(8,128)(2,1)S(1)} fusion(bf16[512,3072]{1,0:T(8,128)(2,1)S(1)} %bitcast.39, bf16[3072,512]{1,0:T(8,128)(2,1)S(1)} %copy-done), kind=kOutput, calls=%fused_computation.5 | convolution fusion | flops 1610874880 | bytes 6815744 | tf_op jit(solution)/shard_map/dot_general | solution.py:53
  39.1 0.0 copy-done.1
  39.1 1.1 %copy-done.5 = bf16[3072,512]{1,0:T(8,128)(2,1)S(1)} copy-done((bf16[3072,512]{1,0:T(8,128)(2,1)S(1)}, bf16[3072,512]{1,0:T(8,128)(2,1)}, u32[]{:S(2)}) %copy-start.5) | copy-done | bytes 3145752
  40.3 0.0 copy-start.3
  40.3 1.8 %convolution_convert_fusion.1 = bf16[512,512]{0,1:T(8,128)(2,1)S(1)} fusion(bf16[512,3072]{1,0:T(8,128)(2,1)S(1)} %bitcast.40, bf16[3072,512]{1,0:T(8,128)(2,1)S(1)} %copy-done.5), kind=kOutput, calls=%fused_computation.4 | convolution fusion | flops 1610874880 | bytes 6815744 | tf_op jit(solution)/shard_map/dot_general | solution.py:54
  42.1 0.0 copy-start.4
  42.1 0.0 copy-done.3
  42.1 1.0 %convolution_convert_fusion.4 = bf16[4,128,128]{2,1,0:T(8,128)(2,1)} fusion(bf16[512,4,128]{0,2,1:T(8,128)(2,1)S(1)} %bitcast.44, bf16[512,4,128]{0,2,1:T(8,128)(2,1)S(1)} %bitcast.46), kind=kOutput, calls=%fused_computation.7 | convolution fusion | flops 67174400 | bytes 1179648 | tf_op jit(solution)/shard_map/bshd,bshe->bhde/dot_general | solution.py:63
  43.1 0.0 copy-done.4
  43.1 11.1 %all-to-all-start.2 = ((bf16[32,16,128]{2,1,0:T(8,128)(2,1)}), bf16[32,16,128]{2,1,0:T(8,128)(2,1)S(1)}, u32[]{:S(2)}, u32[]{:S(2)}) async-start(bf16[32,16,128]{2,1,0:T(8,128)(2,1)} %bitcast.5), calls=%async_computation.2 | async-start | bytes 262144 | tf_op jit(solution)/shard_map/all_to_all | solution.py:23
  54.2 5.5 %convolution_convert_fusion.3.query_ref = bf16[512,512]{1,0:T(8,128)(2,1)} fusion(bf16[512,3072]{1,0:T(8,128)(2,1)} %bitcast.41, bf16[3072,512]{1,0:T(8,128)(2,1)} %param.6), kind=kOutput, calls=%fused_computation.6 | convolution fusion | flops 1610874880 | bytes 6815744 | tf_op jit(solution)/shard_map/dot_general | solution.py:50
  59.6 3.9 %all-to-all-done.2 = bf16[32,16,128]{2,1,0:T(8,128)(2,1)S(1)} async-done(((bf16[32,16,128]{2,1,0:T(8,128)(2,1)}), bf16[32,16,128]{2,1,0:T(8,128)(2,1)S(1)}, u32[]{:S(2)}, u32[]{:S(2)}) %all-to-all-start.2) | async-done | bytes 131104 | tf_op jit(solution)/shard_map/all_to_all | solution.py:23
  63.5 0.2 fusion.2
  63.7 0.7 copy.24
  64.4 5.3 %all-to-all-start.3 = ((bf16[32,16,128]{2,1,0:T(8,128)(2,1)}), bf16[32,16,128]{2,1,0:T(8,128)(2,1)S(1)}, u32[]{:S(2)}, u32[]{:S(2)}) async-start(bf16[32,16,128]{2,1,0:T(8,128)(2,1)} %bitcast.17), calls=%async_computation.3 | async-start | bytes 262144 | tf_op jit(solution)/shard_map/all_to_all | solution.py:30
  69.7 3.7 %fusion.1 = f32[1,512,4,128]{1,3,2,0:T(8,128)} fusion(bf16[512,4,128]{0,2,1:T(8,128)(2,1)} %bitcast.47, bf16[512,4,128]{0,2,1:T(8,128)(2,1)} %bitcast.45, pred[512,512]{1,0:T(8,128)(4,1)S(1)} %iota_compare_fusion, bf16[512,512]{1,0:T(8,128)(2,1)} %convolution_convert_fusion.3.query_ref), kind=kOutput, calls=%fused_computation.3 | convolution fusion | flops 538968064 | bytes 2883584 | tf_op jit(solution)/shard_map/bhqk,bkhe->bqhe/dot_general | solution.py:74
  73.4 2.5 %copy.21.inner_ref = f32[512,512]{1,0:T(8,128)} copy(f32[512,512]{0,1:T(8,128)} %bitcast.42) | data formatting | bytes 2097152 | tf_op jit(solution)/shard_map/reshape | solution.py:79
  75.9 3.1 %all-to-all-done.3 = bf16[32,16,128]{2,1,0:T(8,128)(2,1)S(1)} async-done(((bf16[32,16,128]{2,1,0:T(8,128)(2,1)}), bf16[32,16,128]{2,1,0:T(8,128)(2,1)S(1)}, u32[]{:S(2)}, u32[]{:S(2)}) %all-to-all-start.3) | async-done | bytes 131104 | tf_op jit(solution)/shard_map/all_to_all | solution.py:30
  79.0 0.0 copy-start.2
  79.0 0.6 copy-done.2
  79.7 2.8 %shard_map.55 = bf16[512,512]{1,0:T(8,128)(2,1)} custom-call(bf16[512,512]{1,0:T(8,128)(2,1)} %convolution_convert_fusion.3.query_ref, bf16[4,128,128]{2,1,0:T(8,128)(2,1)} %bitcast.43, f32[512,512]{1,0:T(8,128)} %copy.21.inner_ref, f32[1,512]{1,0:T(1,128)} %bitcast.49), custom_call_target="tpu_custom_call" | custom-call | tf_op jit(solution)/shard_map/pallas_call | solution.py:102
Async XLA Ops:
  0.0 37.2 %copy-start = (bf16[3072,512]{1,0:T(8,128)(2,1)S(1)}, bf16[3072,512]{1,0:T(8,128)(2,1)}, u32[]{:S(2)}) copy-start(bf16[3072,512]{1,0:T(8,128)(2,1)} %param.7) | copy-start | bytes 9437188
  2.5 23.6 %all-to-all-start = ((bf16[4,64,3072]{2,1,0:T(8,128)(2,1)}), bf16[4,64,3072]{2,1,0:T(8,128)(2,1)}, u32[]{:S(2)}, u32[]{:S(2)}) async-start(bf16[4,64,3072]{2,1,0:T(8,128)(2,1)} %broadcast_in_dim.12), calls=%async_computation | async-start | bytes 3145728 | tf_op jit(solution)/shard_map/all_to_all | solution.py:37
  37.2 1.9 %copy-start.1 = (bf16[2,4,64,3072]{3,2,0,1:T(8,128)(2,1)}, bf16[2,4,64,3072]{3,2,0,1:T(8,128)(2,1)S(1)}, u32[]{:S(2)}) copy-start(bf16[2,4,64,3072]{3,2,0,1:T(8,128)(2,1)S(1)} %copy.12) | copy-start | bytes 9437188
  37.2 3.0 %copy-start.5 = (bf16[3072,512]{1,0:T(8,128)(2,1)S(1)}, bf16[3072,512]{1,0:T(8,128)(2,1)}, u32[]{:S(2)}) copy-start(bf16[3072,512]{1,0:T(8,128)(2,1)} %param.8) | copy-start | bytes 9437188
  40.3 1.9 %copy-start.3 = (bf16[512,512]{0,1:T(8,128)(2,1)}, bf16[512,512]{0,1:T(8,128)(2,1)S(1)}, u32[]{:S(2)}) copy-start(bf16[512,512]{0,1:T(8,128)(2,1)S(1)} %convolution_convert_fusion.2) | copy-start | bytes 1572868
  42.1 1.0 %copy-start.4 = (bf16[512,512]{0,1:T(8,128)(2,1)}, bf16[512,512]{0,1:T(8,128)(2,1)S(1)}, u32[]{:S(2)}) copy-start(bf16[512,512]{0,1:T(8,128)(2,1)S(1)} %convolution_convert_fusion.1) | copy-start | bytes 1572868
  43.1 20.4 %all-to-all-start.2 = ((bf16[32,16,128]{2,1,0:T(8,128)(2,1)}), bf16[32,16,128]{2,1,0:T(8,128)(2,1)S(1)}, u32[]{:S(2)}, u32[]{:S(2)}) async-start(bf16[32,16,128]{2,1,0:T(8,128)(2,1)} %bitcast.5), calls=%async_computation.2 | async-start | bytes 262144 | tf_op jit(solution)/shard_map/all_to_all | solution.py:23
  64.4 14.7 %all-to-all-start.3 = ((bf16[32,16,128]{2,1,0:T(8,128)(2,1)}), bf16[32,16,128]{2,1,0:T(8,128)(2,1)S(1)}, u32[]{:S(2)}, u32[]{:S(2)}) async-start(bf16[32,16,128]{2,1,0:T(8,128)(2,1)} %bitcast.17), calls=%async_computation.3 | async-start | bytes 262144 | tf_op jit(solution)/shard_map/all_to_all | solution.py:30
  79.0 0.6 copy-start.2

commit v15 on v14

--- a/solution.py
+++ b/solution.py
@@ -69,8 +69,10 @@
     earlier = jnp.concatenate([jnp.zeros_like(block_states), running[:-1]], axis=0)
     block_start = (prefix_state.astype(jnp.float32)[None] + earlier).astype(jnp.bfloat16)
     scores = jnp.einsum("bqhd,bkhd->bhqk", query_rows, key_rows, preferred_element_type=jnp.float32)
-    causal = jnp.arange(BLOCK)[:, None] >= jnp.arange(BLOCK)[None, :]
-    scores = jnp.where(causal[None, None], scores, jnp.float32(0.0)).astype(jnp.bfloat16)
+    causal = lax.broadcasted_iota(jnp.int32, scores.shape, 2) >= lax.broadcasted_iota(
+        jnp.int32, scores.shape, 3
+    )
+    scores = jnp.where(causal, scores, jnp.float32(0.0)).astype(jnp.bfloat16)
     inner = jnp.einsum("bhqk,bkhe->bqhe", scores, value_rows, preferred_element_type=jnp.float32)
     inner = lax.optimization_barrier(inner)
     out = finish(

time: 82.9 us -> 79.9 us (0.964)
  blocking collectives: 9.16 us -> 32.4 us
  waiting for transfers between devices: 25.5 us -> 7.18 us
  starting transfers between devices: 21.4 us -> 16.3 us
  local copies, waits for them, and re-layouts: 9.46 us -> 6.9 us
    all_to_all x1 -> x2, blocking collectives: 9.16 us -> 32.4 us  [spread(): return lax.all_to_all(copies, axis, 0, 0, tiled=True)]
    all_to_all x1 -> x0, waiting for transfers between devices: 18.5 us -> none  [spread(): return lax.all_to_all(copies, axis, 0, 0, tiled=True)]
    all_to_all x1 -> x0, starting transfers between devices: 5 us -> none  [spread(): return lax.all_to_all(copies, axis, 0, 0, tiled=True)]
    broadcast_in_dim x2, local copies, waits for them, and re-layouts: 4.26 us -> 1.69 us  [spread(): copies = jnp.broadcast_to(value[None], (size,) + value.shape)]
  transfers between devices with their start and end apart: 3 -> 2, of which waited for: 3 -> 2; matrix products, arithmetic and copies ran while one was open for 14% -> 15% of each run, Pallas kernels for 0% -> 0%
where the time goes in v15:
time: 79.9 us; the launch traced here: 79.4 us
  blocking collectives  32.4 us (41%)
  starting transfers between devices  16.3 us (20%)
  matrix products  13.8 us (17%)
  waiting for transfers between devices  7.18 us (9%)
  local copies, waits for them, and re-layouts  6.9 us (9%)
  Pallas kernels  2.76 us (3%)
    all_to_all x2, blocking collectives, spread(): return lax.all_to_all(copies, axis, 0, 0, tiled=True)  32.4 us
    all_to_all x1, starting transfers between devices, exclusive_scan(): gathered = lax.all_to_all(pieces, axis, 0, 0, tiled=True)  11 us
    dot_general x1, matrix products, body(): jnp.dot(piece_rows, w_query, preferred_element_type=jnp.float32)  5.43 us
    all_to_all x1, starting transfers between devices, exclusive_scan(): lax.all_to_all(before.reshape(pieces.shape), axis, 0, 0, tiled=True)  5.3 us
    all_to_all x1, waiting for transfers between devices, exclusive_scan(): gathered = lax.all_to_all(pieces, axis, 0, 0, tiled=True)  3.92 us
    dot_general x1, matrix products, body(): jnp.einsum('bhqk,bkhe->bqhe', scores, value_rows, preferred_element_type=...  3.57 us
    all_to_all x1, waiting for transfers between devices, exclusive_scan(): lax.all_to_all(before.reshape(pieces.shape), axis, 0, 0, tiled=True)  3.26 us
    pallas_call x1, Pallas kernels, finish(): pl.pallas_call(finish_kernel, out_shape=jax.ShapeDtypeStruct(query.shape,...  2.76 us
  transfers between devices with their start and end apart: 2, of which 2 were waited for; matrix products, arithmetic and copies ran while one was open for 15% of the time, Pallas kernels for 0%

profile of v15, /device:TPU:1, one launch (start us, length us, event | category | flops | bytes accessed | tf_op | source)
XLA Modules:
  0.0 79.4 jit_solution(4404179517730688062)
XLA Ops:
  0.0 0.0 copy-start
  0.0 1.3 %broadcast_in_dim.7 = bf16[4,64,3072]{2,1,0:T(8,128)(2,1)S(1)} broadcast(bf16[64,3072]{1,0:T(8,128)(2,1)} %param.5), dimensions={1,2} | broadcast | bytes 1966080 | tf_op jit(solution)/shard_map/broadcast_in_dim | solution.py:36
  1.3 24.7 %all_to_all.20 = bf16[4,64,3072]{2,1,0:T(8,128)(2,1)S(1)} all-to-all(bf16[4,64,3072]{2,1,0:T(8,128)(2,1)S(1)} %broadcast_in_dim.7), channel_id=1, replica_groups=mesh['ctx'=32,'y'=4,'core'=2] {'y'}, dimensions={0} | all-to-all | bytes 3145728 | tf_op jit(solution)/shard_map/all_to_all | solution.py:37
  26.0 0.4 broadcast_in_dim.8
  26.4 7.7 %all_to_all.21 = bf16[2,4,64,3072]{3,2,1,0:T(8,128)(2,1)S(1)} all-to-all(bf16[2,4,64,3072]{3,2,1,0:T(8,128)(2,1)S(1)} %broadcast_in_dim.8), channel_id=1, replica_groups=mesh['ctx'=32,'y'=4,'core'=2] {'core'}, dimensions={0} | all-to-all | bytes 6291456 | tf_op jit(solution)/shard_map/all_to_all | solution.py:37
  34.1 0.2 copy.12
  34.3 0.0 copy-start.1
  34.3 0.0 copy-done
  34.3 0.0 copy-start.5
  34.3 1.9 %convolution_convert_fusion.1 = bf16[512,512]{0,1:T(8,128)(2,1)S(1)} fusion(bf16[512,3072]{1,0:T(8,128)(2,1)S(1)} %bitcast.39, bf16[3072,512]{1,0:T(8,128)(2,1)S(1)} %copy-done), kind=kOutput, calls=%fused_computation.5 | convolution fusion | flops 1610874880 | bytes 6815744 | tf_op jit(solution)/shard_map/dot_general | solution.py:54
  36.2 0.0 copy-done.1
  36.2 1.1 %copy-done.5 = bf16[3072,512]{1,0:T(8,128)(2,1)S(1)} copy-done((bf16[3072,512]{1,0:T(8,128)(2,1)S(1)}, bf16[3072,512]{1,0:T(8,128)(2,1)}, u32[]{:S(2)}) %copy-start.5) | copy-done | bytes 3145752
  37.3 0.0 copy-start.3
  37.3 1.8 %convolution_convert_fusion.2 = bf16[512,512]{0,1:T(8,128)(2,1)S(1)} fusion(bf16[512,3072]{1,0:T(8,128)(2,1)S(1)} %bitcast.40, bf16[3072,512]{1,0:T(8,128)(2,1)S(1)} %copy-done.5), kind=kOutput, calls=%fused_computation.6 | convolution fusion | flops 1610874880 | bytes 6815744 | tf_op jit(solution)/shard_map/dot_general | solution.py:53
  39.2 0.0 copy-start.4
  39.2 0.0 copy-done.3
  39.2 0.9 %convolution_convert_fusion.4 = bf16[4,128,128]{2,1,0:T(8,128)(2,1)} fusion(bf16[512,4,128]{0,2,1:T(8,128)(2,1)S(1)} %bitcast.46, bf16[512,4,128]{0,2,1:T(8,128)(2,1)S(1)} %bitcast.44), kind=kOutput, calls=%fused_computation.8 | convolution fusion | flops 67174400 | bytes 1179648 | tf_op jit(solution)/shard_map/bshd,bshe->bhde/dot_general | solution.py:63
  40.1 0.0 copy-done.4
  40.1 11.0 %all-to-all-start.2 = ((bf16[32,16,128]{2,1,0:T(8,128)(2,1)}), bf16[32,16,128]{2,1,0:T(8,128)(2,1)S(1)}, u32[]{:S(2)}, u32[]{:S(2)}) async-start(bf16[32,16,128]{2,1,0:T(8,128)(2,1)} %bitcast.5), calls=%async_computation.2 | async-start | bytes 262144 | tf_op jit(solution)/shard_map/all_to_all | solution.py:23
  51.2 5.4 %convolution_convert_fusion.3.query_ref = bf16[512,512]{1,0:T(8,128)(2,1)} fusion(bf16[512,3072]{1,0:T(8,128)(2,1)} %bitcast.41, bf16[3072,512]{1,0:T(8,128)(2,1)} %param.6), kind=kOutput, calls=%fused_computation.7 | convolution fusion | flops 1610874880 | bytes 6815744 | tf_op jit(solution)/shard_map/dot_general | solution.py:50
  56.6 3.9 %all-to-all-done.2 = bf16[32,16,128]{2,1,0:T(8,128)(2,1)S(1)} async-done(((bf16[32,16,128]{2,1,0:T(8,128)(2,1)}), bf16[32,16,128]{2,1,0:T(8,128)(2,1)S(1)}, u32[]{:S(2)}, u32[]{:S(2)}) %all-to-all-start.2) | async-done | bytes 131104 | tf_op jit(solution)/shard_map/all_to_all | solution.py:23
  60.5 0.2 fusion.2
  60.7 0.7 copy.24
  61.4 5.3 %all-to-all-start.3 = ((bf16[32,16,128]{2,1,0:T(8,128)(2,1)}), bf16[32,16,128]{2,1,0:T(8,128)(2,1)S(1)}, u32[]{:S(2)}, u32[]{:S(2)}) async-start(bf16[32,16,128]{2,1,0:T(8,128)(2,1)} %bitcast.17), calls=%async_computation.3 | async-start | bytes 262144 | tf_op jit(solution)/shard_map/all_to_all | solution.py:30
  66.7 3.6 %fusion.1 = f32[1,512,4,128]{1,3,2,0:T(8,128)} fusion(bf16[512,4,128]{0,2,1:T(8,128)(2,1)} %bitcast.45, bf16[512,4,128]{0,2,1:T(8,128)(2,1)} %bitcast.47, bf16[512,512]{1,0:T(8,128)(2,1)} %convolution_convert_fusion.3.query_ref), kind=kOutput, calls=%fused_computation.4 | convolution fusion | flops 540016640 | bytes 2621440 | tf_op jit(solution)/shard_map/bhqk,bkhe->bqhe/dot_general | solution.py:76
  70.2 2.5 %copy.21.inner_ref = f32[512,512]{1,0:T(8,128)} copy(f32[512,512]{0,1:T(8,128)} %bitcast.42) | data formatting | bytes 2097152 | tf_op jit(solution)/shard_map/reshape | solution.py:81
  72.8 3.3 %all-to-all-done.3 = bf16[32,16,128]{2,1,0:T(8,128)(2,1)S(1)} async-done(((bf16[32,16,128]{2,1,0:T(8,128)(2,1)}), bf16[32,16,128]{2,1,0:T(8,128)(2,1)S(1)}, u32[]{:S(2)}, u32[]{:S(2)}) %all-to-all-start.3) | async-done | bytes 131104 | tf_op jit(solution)/shard_map/all_to_all | solution.py:30
  76.0 0.0 copy-start.2
  76.0 0.7 copy-done.2
  76.7 2.8 %shard_map.55 = bf16[512,512]{1,0:T(8,128)(2,1)} custom-call(bf16[512,512]{1,0:T(8,128)(2,1)} %convolution_convert_fusion.3.query_ref, bf16[4,128,128]{2,1,0:T(8,128)(2,1)} %bitcast.43, f32[512,512]{1,0:T(8,128)} %copy.21.inner_ref, f32[1,512]{1,0:T(1,128)} %bitcast.49), custom_call_target="tpu_custom_call" | custom-call | tf_op jit(solution)/shard_map/pallas_call | solution.py:104
Async XLA Ops:
  0.0 34.3 %copy-start = (bf16[3072,512]{1,0:T(8,128)(2,1)S(1)}, bf16[3072,512]{1,0:T(8,128)(2,1)}, u32[]{:S(2)}) copy-start(bf16[3072,512]{1,0:T(8,128)(2,1)} %param.8) | copy-start | bytes 9437188
  34.3 1.9 %copy-start.1 = (bf16[2,4,64,3072]{3,2,0,1:T(8,128)(2,1)}, bf16[2,4,64,3072]{3,2,0,1:T(8,128)(2,1)S(1)}, u32[]{:S(2)}) copy-start(bf16[2,4,64,3072]{3,2,0,1:T(8,128)(2,1)S(1)} %copy.12) | copy-start | bytes 9437188
  34.3 3.0 %copy-start.5 = (bf16[3072,512]{1,0:T(8,128)(2,1)S(1)}, bf16[3072,512]{1,0:T(8,128)(2,1)}, u32[]{:S(2)}) copy-start(bf16[3072,512]{1,0:T(8,128)(2,1)} %param.7) | copy-start | bytes 9437188
  37.3 1.9 %copy-start.3 = (bf16[512,512]{0,1:T(8,128)(2,1)}, bf16[512,512]{0,1:T(8,128)(2,1)S(1)}, u32[]{:S(2)}) copy-start(bf16[512,512]{0,1:T(8,128)(2,1)S(1)} %convolution_convert_fusion.1) | copy-start | bytes 1572868
  39.2 1.0 %copy-start.4 = (bf16[512,512]{0,1:T(8,128)(2,1)}, bf16[512,512]{0,1:T(8,128)(2,1)S(1)}, u32[]{:S(2)}) copy-start(bf16[512,512]{0,1:T(8,128)(2,1)S(1)} %convolution_convert_fusion.2) | copy-start | bytes 1572868
  40.1 20.4 %all-to-all-start.2 = ((bf16[32,16,128]{2,1,0:T(8,128)(2,1)}), bf16[32,16,128]{2,1,0:T(8,128)(2,1)S(1)}, u32[]{:S(2)}, u32[]{:S(2)}) async-start(bf16[32,16,128]{2,1,0:T(8,128)(2,1)} %bitcast.5), calls=%async_computation.2 | async-start | bytes 262144 | tf_op jit(solution)/shard_map/all_to_all | solution.py:23
  61.4 14.7 %all-to-all-start.3 = ((bf16[32,16,128]{2,1,0:T(8,128)(2,1)}), bf16[32,16,128]{2,1,0:T(8,128)(2,1)S(1)}, u32[]{:S(2)}, u32[]{:S(2)}) async-start(bf16[32,16,128]{2,1,0:T(8,128)(2,1)} %bitcast.17), calls=%async_computation.3 | async-start | bytes 262144 | tf_op jit(solution)/shard_map/all_to_all | solution.py:30
  76.0 0.7 copy-start.2

commit v16 on v15

--- a/solution.py
+++ b/solution.py
@@ -39,7 +39,10 @@
 
 def gather_rows(tokens):
     near = spread(tokens, "y")
-    both = spread(near, "core")
+    other = lax.ppermute(near, "core", [(0, 1), (1, 0)])
+    both = jnp.where(
+        lax.axis_index("core") == 0, jnp.stack([near, other]), jnp.stack([other, near])
+    )
     return both.transpose(1, 0, 2, 3).reshape(-1, tokens.shape[1])
 
 

time: 79.9 us -> 80.2 us (level)
  blocking collectives: 32.4 us -> 23.9 us
  other arithmetic: 0 us -> 3.36 us
  waiting for transfers between devices: 7.18 us -> 10.5 us
  starting transfers between devices: 16.3 us -> 19 us
    all_to_all x2 -> x1, blocking collectives: 32.4 us -> 23.9 us  [spread(): return lax.all_to_all(copies, axis, 0, 0, tiled=True)]
    ppermute x0 -> x1, waiting for transfers between devices: none -> 3.38 us  [gather_rows(): other = lax.ppermute(near, 'core', [(0, 1), (1, 0)])]
    select_n x0 -> x1, other arithmetic: none -> 3.36 us  [gather_rows(): jnp.where(lax.axis_index('core') == 0, jnp.stack([near, other]), jnp.stac...]
    ppermute x0 -> x1, starting transfers between devices: none -> 2.63 us  [gather_rows(): other = lax.ppermute(near, 'core', [(0, 1), (1, 0)])]
    broadcast_in_dim x2 -> x1, local copies, waits for them, and re-layouts: 1.69 us -> 1.31 us  [spread(): copies = jnp.broadcast_to(value[None], (size,) + value.shape)]
  transfers between devices with their start and end apart: 2 -> 3, of which waited for: 2 -> 3; matrix products, arithmetic and copies ran while one was open for 15% -> 14% of each run, Pallas kernels for 0% -> 0%
where the time goes in v16:
time: 80.2 us; the launch traced here: 79.8 us
  blocking collectives  23.9 us (30%)
  starting transfers between devices  19 us (24%)
  matrix products  13.8 us (17%)
  waiting for transfers between devices  10.5 us (13%)
  local copies, waits for them, and re-layouts  6.34 us (8%)
  other arithmetic  3.36 us (4%)
  Pallas kernels  2.76 us (3%)
    all_to_all x1, blocking collectives, spread(): return lax.all_to_all(copies, axis, 0, 0, tiled=True)  23.9 us
    all_to_all x1, starting transfers between devices, exclusive_scan(): gathered = lax.all_to_all(pieces, axis, 0, 0, tiled=True)  11 us
    dot_general x1, matrix products, body(): jnp.dot(piece_rows, w_query, preferred_element_type=jnp.float32)  5.44 us
    all_to_all x1, starting transfers between devices, exclusive_scan(): lax.all_to_all(before.reshape(pieces.shape), axis, 0, 0, tiled=True)  5.31 us
    all_to_all x1, waiting for transfers between devices, exclusive_scan(): gathered = lax.all_to_all(pieces, axis, 0, 0, tiled=True)  3.91 us
    dot_general x1, matrix products, body(): jnp.einsum('bhqk,bkhe->bqhe', scores, value_rows, preferred_element_type=...  3.56 us
    ppermute x1, waiting for transfers between devices, gather_rows(): other = lax.ppermute(near, 'core', [(0, 1), (1, 0)])  3.38 us
    select_n x1, other arithmetic, gather_rows(): jnp.where(lax.axis_index('core') == 0, jnp.stack([near, other]), jnp.stac...  3.36 us
  transfers between devices with their start and end apart: 3, of which 3 were waited for; matrix products, arithmetic and copies ran while one was open for 14% of the time, Pallas kernels for 0%

profile of v16, /device:TPU:1, one launch (start us, length us, event | category | flops | bytes accessed | tf_op | source)
XLA Modules:
  0.0 79.8 jit_solution(18281168349648474756)
XLA Ops:
  0.0 0.0 copy-start
  0.0 1.3 %broadcast_in_dim.5 = bf16[4,64,3072]{2,1,0:T(8,128)(2,1)S(1)} broadcast(bf16[64,3072]{1,0:T(8,128)(2,1)} %param.5), dimensions={1,2} | broadcast | bytes 1966080 | tf_op jit(solution)/shard_map/broadcast_in_dim | solution.py:36
  1.3 23.9 %all_to_all.15 = bf16[4,64,3072]{2,1,0:T(8,128)(2,1)} all-to-all(bf16[4,64,3072]{2,1,0:T(8,128)(2,1)S(1)} %broadcast_in_dim.5), channel_id=1, replica_groups=mesh['ctx'=32,'y'=4,'core'=2] {'y'}, dimensions={0} | all-to-all | bytes 3145728 | tf_op jit(solution)/shard_map/all_to_all | solution.py:37
  25.3 2.6 %collective-permute-start = (bf16[4,64,3072]{2,1,0:T(8,128)(2,1)}, bf16[4,64,3072]{2,1,0:T(8,128)(2,1)}, u32[]{:S(2)}, u32[]{:S(2)}) collective-permute-start(bf16[4,64,3072]{2,1,0:T(8,128)(2,1)} %all_to_all.15), channel_id=1, source_target_pairs={{0,1},{1,0},{2,3},{3,2},{4,5},{5,4},{6,7},{7,6},{8,9},{9,8},{10,11... | collective-permute-start | bytes 4718600 | tf_op jit(solution)/shard_map/ppermute | solution.py:42
  27.9 3.4 %collective-permute-done = bf16[4,64,3072]{2,1,0:T(8,128)(2,1)} collective-permute-done((bf16[4,64,3072]{2,1,0:T(8,128)(2,1)}, bf16[4,64,3072]{2,1,0:T(8,128)(2,1)}, u32[]{:S(2)}, u32[]{:S(2)}) %collective-permute-start) | collective-permute-done | bytes 1572896 | tf_op jit(solution)/shard_map/ppermute | solution.py:42
  31.3 3.4 %maximum_select_fusion = bf16[2,4,64,3072]{3,2,0,1:T(8,128)(2,1)S(1)} fusion(bf16[1,4,64,3072]{3,2,0,1:T(8,128)(2,1)} %bitcast.1, bf16[1,4,64,3072]{3,2,0,1:T(8,128)(2,1)} %bitcast, pred[]{:T(512)S(6)} %eq.3), kind=kLoop, calls=%fused_computation.2 | loop fusion | flops 4718592 | bytes 6291457 | tf_op jit(solution)/shard_map/jit(_where)/select_n | solution.py:43
  34.6 0.0 copy-start.1
  34.7 0.0 copy-done
  34.7 0.0 copy-start.5
  34.7 1.9 %convolution_convert_fusion.1 = bf16[512,512]{0,1:T(8,128)(2,1)S(1)} fusion(bf16[512,3072]{1,0:T(8,128)(2,1)S(1)} %bitcast.41, bf16[3072,512]{1,0:T(8,128)(2,1)S(1)} %copy-done), kind=kOutput, calls=%fused_computation.6 | convolution fusion | flops 1610874880 | bytes 6815744 | tf_op jit(solution)/shard_map/dot_general | solution.py:57
  36.5 0.0 copy-done.1
  36.6 1.1 %copy-done.5 = bf16[3072,512]{1,0:T(8,128)(2,1)S(1)} copy-done((bf16[3072,512]{1,0:T(8,128)(2,1)S(1)}, bf16[3072,512]{1,0:T(8,128)(2,1)}, u32[]{:S(2)}) %copy-start.5) | copy-done | bytes 3145752
  37.7 0.0 copy-start.3
  37.7 1.8 %convolution_convert_fusion.2 = bf16[512,512]{0,1:T(8,128)(2,1)S(1)} fusion(bf16[512,3072]{1,0:T(8,128)(2,1)S(1)} %bitcast.42, bf16[3072,512]{1,0:T(8,128)(2,1)S(1)} %copy-done.5), kind=kOutput, calls=%fused_computation.7 | convolution fusion | flops 1610874880 | bytes 6815744 | tf_op jit(solution)/shard_map/dot_general | solution.py:56
  39.5 0.0 copy-start.4
  39.5 0.0 copy-done.3
  39.6 0.9 %convolution_convert_fusion.4 = bf16[4,128,128]{2,1,0:T(8,128)(2,1)} fusion(bf16[512,4,128]{0,2,1:T(8,128)(2,1)S(1)} %bitcast.48, bf16[512,4,128]{0,2,1:T(8,128)(2,1)S(1)} %bitcast.46), kind=kOutput, calls=%fused_computation.9 | convolution fusion | flops 67174400 | bytes 1179648 | tf_op jit(solution)/shard_map/bshd,bshe->bhde/dot_general | solution.py:66
  40.5 0.0 copy-done.4
  40.5 11.0 %all-to-all-start.1 = ((bf16[32,16,128]{2,1,0:T(8,128)(2,1)}), bf16[32,16,128]{2,1,0:T(8,128)(2,1)S(1)}, u32[]{:S(2)}, u32[]{:S(2)}) async-start(bf16[32,16,128]{2,1,0:T(8,128)(2,1)} %bitcast.7), calls=%async_computation.1 | async-start | bytes 262144 | tf_op jit(solution)/shard_map/all_to_all | solution.py:23
  51.5 5.4 %convolution_convert_fusion.3.query_ref = bf16[512,512]{1,0:T(8,128)(2,1)} fusion(bf16[512,3072]{1,0:T(8,128)(2,1)} %bitcast.43, bf16[3072,512]{1,0:T(8,128)(2,1)} %param.6), kind=kOutput, calls=%fused_computation.8 | convolution fusion | flops 1610874880 | bytes 6815744 | tf_op jit(solution)/shard_map/dot_general | solution.py:53
  57.0 3.9 %all-to-all-done.1 = bf16[32,16,128]{2,1,0:T(8,128)(2,1)S(1)} async-done(((bf16[32,16,128]{2,1,0:T(8,128)(2,1)}), bf16[32,16,128]{2,1,0:T(8,128)(2,1)S(1)}, u32[]{:S(2)}, u32[]{:S(2)}) %all-to-all-start.1) | async-done | bytes 131104 | tf_op jit(solution)/shard_map/all_to_all | solution.py:23
  60.9 0.2 fusion.2
  61.1 0.7 copy.18
  61.7 5.3 %all-to-all-start.2 = ((bf16[32,16,128]{2,1,0:T(8,128)(2,1)}), bf16[32,16,128]{2,1,0:T(8,128)(2,1)S(1)}, u32[]{:S(2)}, u32[]{:S(2)}) async-start(bf16[32,16,128]{2,1,0:T(8,128)(2,1)} %bitcast.19), calls=%async_computation.2 | async-start | bytes 262144 | tf_op jit(solution)/shard_map/all_to_all | solution.py:30
  67.1 3.6 %fusion.1 = f32[1,512,4,128]{1,3,2,0:T(8,128)} fusion(bf16[512,4,128]{0,2,1:T(8,128)(2,1)} %bitcast.47, bf16[512,4,128]{0,2,1:T(8,128)(2,1)} %bitcast.49, bf16[512,512]{1,0:T(8,128)(2,1)} %convolution_convert_fusion.3.query_ref), kind=kOutput, calls=%fused_computation.5 | convolution fusion | flops 540016640 | bytes 2621440 | tf_op jit(solution)/shard_map/bhqk,bkhe->bqhe/dot_general | solution.py:79
  70.6 2.5 %copy.15.inner_ref = f32[512,512]{1,0:T(8,128)} copy(f32[512,512]{0,1:T(8,128)} %bitcast.44) | data formatting | bytes 2097152 | tf_op jit(solution)/shard_map/reshape | solution.py:84
  73.1 3.2 %all-to-all-done.2 = bf16[32,16,128]{2,1,0:T(8,128)(2,1)S(1)} async-done(((bf16[32,16,128]{2,1,0:T(8,128)(2,1)}), bf16[32,16,128]{2,1,0:T(8,128)(2,1)S(1)}, u32[]{:S(2)}, u32[]{:S(2)}) %all-to-all-start.2) | async-done | bytes 131104 | tf_op jit(solution)/shard_map/all_to_all | solution.py:30
  76.4 0.0 copy-start.2
  76.4 0.7 copy-done.2
  77.1 2.8 %shard_map.55 = bf16[512,512]{1,0:T(8,128)(2,1)} custom-call(bf16[512,512]{1,0:T(8,128)(2,1)} %convolution_convert_fusion.3.query_ref, bf16[4,128,128]{2,1,0:T(8,128)(2,1)} %bitcast.45, f32[512,512]{1,0:T(8,128)} %copy.15.inner_ref, f32[1,512]{1,0:T(1,128)} %bitcast.51), custom_call_target="tpu_custom_call" | custom-call | tf_op jit(solution)/shard_map/pallas_call | solution.py:107
Async XLA Ops:
  0.0 34.7 %copy-start = (bf16[3072,512]{1,0:T(8,128)(2,1)S(1)}, bf16[3072,512]{1,0:T(8,128)(2,1)}, u32[]{:S(2)}) copy-start(bf16[3072,512]{1,0:T(8,128)(2,1)} %param.8) | copy-start | bytes 9437188
  25.3 6.0 %collective-permute-start = (bf16[4,64,3072]{2,1,0:T(8,128)(2,1)}, bf16[4,64,3072]{2,1,0:T(8,128)(2,1)}, u32[]{:S(2)}, u32[]{:S(2)}) collective-permute-start(bf16[4,64,3072]{2,1,0:T(8,128)(2,1)} %all_to_all.15), channel_id=1, source_target_pairs={{0,1},{1,0},{2,3},{3,2},{4,5},{5,4},{6,7},{7,6},{8,9},{9,8},{10,11... | collective-permute-start | bytes 4718600 | tf_op jit(solution)/shard_map/ppermute | solution.py:42
  34.6 1.9 %copy-start.1 = (bf16[2,4,64,3072]{3,2,0,1:T(8,128)(2,1)}, bf16[2,4,64,3072]{3,2,0,1:T(8,128)(2,1)S(1)}, u32[]{:S(2)}) copy-start(bf16[2,4,64,3072]{3,2,0,1:T(8,128)(2,1)S(1)} %maximum_select_fusion) | copy-start | bytes 9437188
  34.7 3.0 %copy-start.5 = (bf16[3072,512]{1,0:T(8,128)(2,1)S(1)}, bf16[3072,512]{1,0:T(8,128)(2,1)}, u32[]{:S(2)}) copy-start(bf16[3072,512]{1,0:T(8,128)(2,1)} %param.7) | copy-start | bytes 9437188
  37.7 1.9 %copy-start.3 = (bf16[512,512]{0,1:T(8,128)(2,1)}, bf16[512,512]{0,1:T(8,128)(2,1)S(1)}, u32[]{:S(2)}) copy-start(bf16[512,512]{0,1:T(8,128)(2,1)S(1)} %convolution_convert_fusion.1) | copy-start | bytes 1572868
  39.5 1.0 %copy-start.4 = (bf16[512,512]{0,1:T(8,128)(2,1)}, bf16[512,512]{0,1:T(8,128)(2,1)S(1)}, u32[]{:S(2)}) copy-start(bf16[512,512]{0,1:T(8,128)(2,1)S(1)} %convolution_convert_fusion.2) | copy-start | bytes 1572868
  40.5 20.4 %all-to-all-start.1 = ((bf16[32,16,128]{2,1,0:T(8,128)(2,1)}), bf16[32,16,128]{2,1,0:T(8,128)(2,1)S(1)}, u32[]{:S(2)}, u32[]{:S(2)}) async-start(bf16[32,16,128]{2,1,0:T(8,128)(2,1)} %bitcast.7), calls=%async_computation.1 | async-start | bytes 262144 | tf_op jit(solution)/shard_map/all_to_all | solution.py:23
  61.7 14.7 %all-to-all-start.2 = ((bf16[32,16,128]{2,1,0:T(8,128)(2,1)}), bf16[32,16,128]{2,1,0:T(8,128)(2,1)S(1)}, u32[]{:S(2)}, u32[]{:S(2)}) async-start(bf16[32,16,128]{2,1,0:T(8,128)(2,1)} %bitcast.19), calls=%async_computation.2 | async-start | bytes 262144 | tf_op jit(solution)/shard_map/all_to_all | solution.py:30
  76.4 0.7 copy-start.2

commit v17 on v15

--- a/solution.py
+++ b/solution.py
@@ -100,16 +100,18 @@
 def finish(query, start, inner, gain, head_count):
     rows, width = query.shape
     blocks = rows // BLOCK
-    tile = pl.BlockSpec((BLOCK, width), lambda b: (b, 0))
+    parts = 2 if head_count % 2 == 0 else 1
+    group = head_count // parts
+    tile = pl.BlockSpec((BLOCK, group * HEAD_DIM), lambda b, p: (b, p))
     return pl.pallas_call(
         finish_kernel,
         out_shape=jax.ShapeDtypeStruct(query.shape, jnp.bfloat16),
-        grid=(blocks,),
+        grid=(blocks, parts),
         in_specs=[
             tile,
-            pl.BlockSpec((head_count, HEAD_DIM, HEAD_DIM), lambda b: (b, 0, 0)),
+            pl.BlockSpec((group, HEAD_DIM, HEAD_DIM), lambda b, p: (b * parts + p, 0, 0)),
             tile,
-            pl.BlockSpec((1, width), lambda b: (0, 0)),
+            pl.BlockSpec((1, group * HEAD_DIM), lambda b, p: (0, p)),
         ],
         out_specs=tile,
     )(query, start, inner, gain)

time: 79.9 us -> 79.7 us (level)
  no operation moved by 1% of the time
where the time goes in v17:
time: 79.7 us; the launch traced here: 79.3 us
  blocking collectives  32.4 us (41%)
  starting transfers between devices  16.3 us (20%)
  matrix products  13.8 us (17%)
  waiting for transfers between devices  7.18 us (9%)
  local copies, waits for them, and re-layouts  6.9 us (9%)
  Pallas kernels  2.64 us (3%)
    all_to_all x2, blocking collectives, spread(): return lax.all_to_all(copies, axis, 0, 0, tiled=True)  32.4 us
    all_to_all x1, starting transfers between devices, exclusive_scan(): gathered = lax.all_to_all(pieces, axis, 0, 0, tiled=True)  11 us
    dot_general x1, matrix products, body(): jnp.dot(piece_rows, w_query, preferred_element_type=jnp.float32)  5.43 us
    all_to_all x1, starting transfers between devices, exclusive_scan(): lax.all_to_all(before.reshape(pieces.shape), axis, 0, 0, tiled=True)  5.3 us
    all_to_all x1, waiting for transfers between devices, exclusive_scan(): gathered = lax.all_to_all(pieces, axis, 0, 0, tiled=True)  3.92 us
    dot_general x1, matrix products, body(): jnp.einsum('bhqk,bkhe->bqhe', scores, value_rows, preferred_element_type=...  3.57 us
    all_to_all x1, waiting for transfers between devices, exclusive_scan(): lax.all_to_all(before.reshape(pieces.shape), axis, 0, 0, tiled=True)  3.26 us
    pallas_call x1, Pallas kernels, finish(): pl.pallas_call(finish_kernel, out_shape=jax.ShapeDtypeStruct(query.shape,...  2.64 us
  transfers between devices with their start and end apart: 2, of which 2 were waited for; matrix products, arithmetic and copies ran while one was open for 15% of the time, Pallas kernels for 0%

profile of v17, /device:TPU:1, one launch (start us, length us, event | category | flops | bytes accessed | tf_op | source)
XLA Modules:
  0.0 79.3 jit_solution(14735289144245361051)
XLA Ops:
  0.0 0.0 copy-start
  0.0 1.3 %broadcast_in_dim.7 = bf16[4,64,3072]{2,1,0:T(8,128)(2,1)S(1)} broadcast(bf16[64,3072]{1,0:T(8,128)(2,1)} %param.5), dimensions={1,2} | broadcast | bytes 1966080 | tf_op jit(solution)/shard_map/broadcast_in_dim | solution.py:36
  1.3 24.7 %all_to_all.20 = bf16[4,64,3072]{2,1,0:T(8,128)(2,1)S(1)} all-to-all(bf16[4,64,3072]{2,1,0:T(8,128)(2,1)S(1)} %broadcast_in_dim.7), channel_id=1, replica_groups=mesh['ctx'=32,'y'=4,'core'=2] {'y'}, dimensions={0} | all-to-all | bytes 3145728 | tf_op jit(solution)/shard_map/all_to_all | solution.py:37
  26.0 0.4 broadcast_in_dim.8
  26.4 7.7 %all_to_all.21 = bf16[2,4,64,3072]{3,2,1,0:T(8,128)(2,1)S(1)} all-to-all(bf16[2,4,64,3072]{3,2,1,0:T(8,128)(2,1)S(1)} %broadcast_in_dim.8), channel_id=1, replica_groups=mesh['ctx'=32,'y'=4,'core'=2] {'core'}, dimensions={0} | all-to-all | bytes 6291456 | tf_op jit(solution)/shard_map/all_to_all | solution.py:37
  34.1 0.2 copy.12
  34.3 0.0 copy-start.1
  34.3 0.0 copy-done
  34.3 0.0 copy-start.5
  34.3 1.9 %convolution_convert_fusion.1 = bf16[512,512]{0,1:T(8,128)(2,1)S(1)} fusion(bf16[512,3072]{1,0:T(8,128)(2,1)S(1)} %bitcast.39, bf16[3072,512]{1,0:T(8,128)(2,1)S(1)} %copy-done), kind=kOutput, calls=%fused_computation.5 | convolution fusion | flops 1610874880 | bytes 6815744 | tf_op jit(solution)/shard_map/dot_general | solution.py:54
  36.2 0.0 copy-done.1
  36.2 1.1 %copy-done.5 = bf16[3072,512]{1,0:T(8,128)(2,1)S(1)} copy-done((bf16[3072,512]{1,0:T(8,128)(2,1)S(1)}, bf16[3072,512]{1,0:T(8,128)(2,1)}, u32[]{:S(2)}) %copy-start.5) | copy-done | bytes 3145752
  37.3 0.0 copy-start.3
  37.3 1.8 %convolution_convert_fusion.2 = bf16[512,512]{0,1:T(8,128)(2,1)S(1)} fusion(bf16[512,3072]{1,0:T(8,128)(2,1)S(1)} %bitcast.40, bf16[3072,512]{1,0:T(8,128)(2,1)S(1)} %copy-done.5), kind=kOutput, calls=%fused_computation.6 | convolution fusion | flops 1610874880 | bytes 6815744 | tf_op jit(solution)/shard_map/dot_general | solution.py:53
  39.2 0.0 copy-start.4
  39.2 0.0 copy-done.3
  39.2 0.9 %convolution_convert_fusion.4 = bf16[4,128,128]{2,1,0:T(8,128)(2,1)} fusion(bf16[512,4,128]{0,2,1:T(8,128)(2,1)S(1)} %bitcast.46, bf16[512,4,128]{0,2,1:T(8,128)(2,1)S(1)} %bitcast.44), kind=kOutput, calls=%fused_computation.8 | convolution fusion | flops 67174400 | bytes 1179648 | tf_op jit(solution)/shard_map/bshd,bshe->bhde/dot_general | solution.py:63
  40.1 0.0 copy-done.4
  40.1 11.0 %all-to-all-start.2 = ((bf16[32,16,128]{2,1,0:T(8,128)(2,1)}), bf16[32,16,128]{2,1,0:T(8,128)(2,1)S(1)}, u32[]{:S(2)}, u32[]{:S(2)}) async-start(bf16[32,16,128]{2,1,0:T(8,128)(2,1)} %bitcast.5), calls=%async_computation.2 | async-start | bytes 262144 | tf_op jit(solution)/shard_map/all_to_all | solution.py:23
  51.2 5.4 %convolution_convert_fusion.3.query_ref = bf16[512,512]{1,0:T(8,128)(2,1)} fusion(bf16[512,3072]{1,0:T(8,128)(2,1)} %bitcast.41, bf16[3072,512]{1,0:T(8,128)(2,1)} %param.6), kind=kOutput, calls=%fused_computation.7 | convolution fusion | flops 1610874880 | bytes 6815744 | tf_op jit(solution)/shard_map/dot_general | solution.py:50
  56.6 3.9 %all-to-all-done.2 = bf16[32,16,128]{2,1,0:T(8,128)(2,1)S(1)} async-done(((bf16[32,16,128]{2,1,0:T(8,128)(2,1)}), bf16[32,16,128]{2,1,0:T(8,128)(2,1)S(1)}, u32[]{:S(2)}, u32[]{:S(2)}) %all-to-all-start.2) | async-done | bytes 131104 | tf_op jit(solution)/shard_map/all_to_all | solution.py:23
  60.5 0.2 fusion.2
  60.7 0.7 copy.24
  61.4 5.3 %all-to-all-start.3 = ((bf16[32,16,128]{2,1,0:T(8,128)(2,1)}), bf16[32,16,128]{2,1,0:T(8,128)(2,1)S(1)}, u32[]{:S(2)}, u32[]{:S(2)}) async-start(bf16[32,16,128]{2,1,0:T(8,128)(2,1)} %bitcast.17), calls=%async_computation.3 | async-start | bytes 262144 | tf_op jit(solution)/shard_map/all_to_all | solution.py:30
  66.7 3.6 %fusion.1 = f32[1,512,4,128]{1,3,2,0:T(8,128)} fusion(bf16[512,4,128]{0,2,1:T(8,128)(2,1)} %bitcast.45, bf16[512,4,128]{0,2,1:T(8,128)(2,1)} %bitcast.47, bf16[512,512]{1,0:T(8,128)(2,1)} %convolution_convert_fusion.3.query_ref), kind=kOutput, calls=%fused_computation.4 | convolution fusion | flops 540016640 | bytes 2621440 | tf_op jit(solution)/shard_map/bhqk,bkhe->bqhe/dot_general | solution.py:76
  70.2 2.5 %copy.21.inner_ref = f32[512,512]{1,0:T(8,128)} copy(f32[512,512]{0,1:T(8,128)} %bitcast.42) | data formatting | bytes 2097152 | tf_op jit(solution)/shard_map/reshape | solution.py:81
  72.8 3.3 %all-to-all-done.3 = bf16[32,16,128]{2,1,0:T(8,128)(2,1)S(1)} async-done(((bf16[32,16,128]{2,1,0:T(8,128)(2,1)}), bf16[32,16,128]{2,1,0:T(8,128)(2,1)S(1)}, u32[]{:S(2)}, u32[]{:S(2)}) %all-to-all-start.3) | async-done | bytes 131104 | tf_op jit(solution)/shard_map/all_to_all | solution.py:30
  76.0 0.0 copy-start.2
  76.0 0.7 copy-done.2
  76.7 2.6 %shard_map.55 = bf16[512,512]{1,0:T(8,128)(2,1)} custom-call(bf16[512,512]{1,0:T(8,128)(2,1)} %convolution_convert_fusion.3.query_ref, bf16[4,128,128]{2,1,0:T(8,128)(2,1)} %bitcast.43, f32[512,512]{1,0:T(8,128)} %copy.21.inner_ref, f32[1,512]{1,0:T(1,128)} %bitcast.49), custom_call_target="tpu_custom_call" | custom-call | tf_op jit(solution)/shard_map/pallas_call | solution.py:106
Async XLA Ops:
  0.0 34.3 %copy-start = (bf16[3072,512]{1,0:T(8,128)(2,1)S(1)}, bf16[3072,512]{1,0:T(8,128)(2,1)}, u32[]{:S(2)}) copy-start(bf16[3072,512]{1,0:T(8,128)(2,1)} %param.8) | copy-start | bytes 9437188
  34.3 1.9 %copy-start.1 = (bf16[2,4,64,3072]{3,2,0,1:T(8,128)(2,1)}, bf16[2,4,64,3072]{3,2,0,1:T(8,128)(2,1)S(1)}, u32[]{:S(2)}) copy-start(bf16[2,4,64,3072]{3,2,0,1:T(8,128)(2,1)S(1)} %copy.12) | copy-start | bytes 9437188
  34.3 3.0 %copy-start.5 = (bf16[3072,512]{1,0:T(8,128)(2,1)S(1)}, bf16[3072,512]{1,0:T(8,128)(2,1)}, u32[]{:S(2)}) copy-start(bf16[3072,512]{1,0:T(8,128)(2,1)} %param.7) | copy-start | bytes 9437188
  37.3 1.9 %copy-start.3 = (bf16[512,512]{0,1:T(8,128)(2,1)}, bf16[512,512]{0,1:T(8,128)(2,1)S(1)}, u32[]{:S(2)}) copy-start(bf16[512,512]{0,1:T(8,128)(2,1)S(1)} %convolution_convert_fusion.1) | copy-start | bytes 1572868
  39.2 1.0 %copy-start.4 = (bf16[512,512]{0,1:T(8,128)(2,1)}, bf16[512,512]{0,1:T(8,128)(2,1)S(1)}, u32[]{:S(2)}) copy-start(bf16[512,512]{0,1:T(8,128)(2,1)S(1)} %convolution_convert_fusion.2) | copy-start | bytes 1572868
  40.1 20.4 %all-to-all-start.2 = ((bf16[32,16,128]{2,1,0:T(8,128)(2,1)}), bf16[32,16,128]{2,1,0:T(8,128)(2,1)S(1)}, u32[]{:S(2)}, u32[]{:S(2)}) async-start(bf16[32,16,128]{2,1,0:T(8,128)(2,1)} %bitcast.5), calls=%async_computation.2 | async-start | bytes 262144 | tf_op jit(solution)/shard_map/all_to_all | solution.py:23
  61.4 14.7 %all-to-all-start.3 = ((bf16[32,16,128]{2,1,0:T(8,128)(2,1)}), bf16[32,16,128]{2,1,0:T(8,128)(2,1)S(1)}, u32[]{:S(2)}, u32[]{:S(2)}) async-start(bf16[32,16,128]{2,1,0:T(8,128)(2,1)} %bitcast.17), calls=%async_computation.3 | async-start | bytes 262144 | tf_op jit(solution)/shard_map/all_to_all | solution.py:30
  76.0 0.7 copy-start.2

commit v18 on v15

--- a/solution.py
+++ b/solution.py
@@ -64,6 +64,7 @@
         "bshd,bshe->bhde", key_rows, value_rows, preferred_element_type=jnp.float32
     )
     local_state = jnp.sum(block_states, axis=0)
+    local_state, query_rows = lax.optimization_barrier((local_state, query_rows))
     prefix_state = exclusive_scan(local_state, "ctx")
     running = jnp.cumsum(block_states, axis=0)
     earlier = jnp.concatenate([jnp.zeros_like(block_states), running[:-1]], axis=0)

time: 79.9 us -> 79.9 us (level)
  blocking collectives: 32.4 us -> 52.5 us
  starting transfers between devices: 16.3 us -> 3.87 us
  waiting for transfers between devices: 7.18 us -> 1.11 us
  matrix products: 13.8 us -> 10.4 us
  local copies, waits for them, and re-layouts: 6.9 us -> 7.87 us
    all_to_all x0 -> x1, blocking collectives: none -> 20.2 us  [exclusive_scan(): gathered = lax.all_to_all(pieces, axis, 0, 0, tiled=True)]
    all_to_all x1 -> x0, starting transfers between devices: 11 us -> none  [exclusive_scan(): gathered = lax.all_to_all(pieces, axis, 0, 0, tiled=True)]
    all_to_all x1 -> x0, waiting for transfers between devices: 3.92 us -> none  [exclusive_scan(): gathered = lax.all_to_all(pieces, axis, 0, 0, tiled=True)]
    dot_general x1, matrix products: 5.43 us -> 2.67 us  [body(): jnp.dot(piece_rows, w_query, preferred_element_type=jnp.float32)]
    all_to_all x1, waiting for transfers between devices: 3.26 us -> 1.11 us  [exclusive_scan(): lax.all_to_all(before.reshape(pieces.shape), axis, 0, 0, tiled=True)]
    reshape x0 -> x1, local copies, waits for them, and re-layouts: none -> 2.07 us  [body(): query_rows.reshape(group_len, local_width)]
    all_to_all x1, starting transfers between devices: 5.3 us -> 3.87 us  [exclusive_scan(): lax.all_to_all(before.reshape(pieces.shape), axis, 0, 0, tiled=True)]
    unnamed x13, local copies, waits for them, and re-layouts: 2.49 us -> 1.38 us
  transfers between devices with their start and end apart: 2 -> 1, of which waited for: 2 -> 1; matrix products, arithmetic and copies ran while one was open for 15% -> 10% of each run, Pallas kernels for 0% -> 0%
where the time goes in v18:
time: 79.9 us; the launch traced here: 78.7 us
  blocking collectives  52.5 us (66%)
  matrix products  10.4 us (13%)
  local copies, waits for them, and re-layouts  7.87 us (10%)
  starting transfers between devices  3.87 us (5%)
  Pallas kernels  2.76 us (3%)
  waiting for transfers between devices  1.11 us (1%)
    all_to_all x2, blocking collectives, spread(): return lax.all_to_all(copies, axis, 0, 0, tiled=True)  32.4 us
    all_to_all x1, blocking collectives, exclusive_scan(): gathered = lax.all_to_all(pieces, axis, 0, 0, tiled=True)  20.2 us
    all_to_all x1, starting transfers between devices, exclusive_scan(): lax.all_to_all(before.reshape(pieces.shape), axis, 0, 0, tiled=True)  3.87 us
    dot_general x1, matrix products, body(): jnp.einsum('bhqk,bkhe->bqhe', scores, value_rows, preferred_element_type=...  3.64 us
    pallas_call x1, Pallas kernels, finish(): pl.pallas_call(finish_kernel, out_shape=jax.ShapeDtypeStruct(query.shape,...  2.76 us
    dot_general x1, matrix products, body(): jnp.dot(piece_rows, w_query, preferred_element_type=jnp.float32)  2.67 us
    reshape x1, local copies, waits for them, and re-layouts, body(): inner.reshape(group_len, local_width)  2.53 us
    reshape x1, local copies, waits for them, and re-layouts, body(): query_rows.reshape(group_len, local_width)  2.07 us
  transfers between devices with their start and end apart: 1, of which 1 were waited for; matrix products, arithmetic and copies ran while one was open for 10% of the time, Pallas kernels for 0%

profile of v18, /device:TPU:1, one launch (start us, length us, event | category | flops | bytes accessed | tf_op | source)
XLA Modules:
  0.0 78.7 jit_solution(8295682749530002737)
XLA Ops:
  0.0 0.0 copy-start
  0.0 1.3 %broadcast_in_dim.7 = bf16[4,64,3072]{2,1,0:T(8,128)(2,1)S(1)} broadcast(bf16[64,3072]{1,0:T(8,128)(2,1)} %param.5), dimensions={1,2} | broadcast | bytes 1966080 | tf_op jit(solution)/shard_map/broadcast_in_dim | solution.py:36
  1.3 24.7 %all_to_all.20 = bf16[4,64,3072]{2,1,0:T(8,128)(2,1)S(1)} all-to-all(bf16[4,64,3072]{2,1,0:T(8,128)(2,1)S(1)} %broadcast_in_dim.7), channel_id=1, replica_groups=mesh['ctx'=32,'y'=4,'core'=2] {'y'}, dimensions={0} | all-to-all | bytes 3145728 | tf_op jit(solution)/shard_map/all_to_all | solution.py:37
  26.0 0.4 broadcast_in_dim.8
  26.4 7.7 %all_to_all.21 = bf16[2,4,64,3072]{3,2,1,0:T(8,128)(2,1)S(1)} all-to-all(bf16[2,4,64,3072]{3,2,1,0:T(8,128)(2,1)S(1)} %broadcast_in_dim.8), channel_id=1, replica_groups=mesh['ctx'=32,'y'=4,'core'=2] {'core'}, dimensions={0} | all-to-all | bytes 6291456 | tf_op jit(solution)/shard_map/all_to_all | solution.py:37
  34.1 0.2 copy.12
  34.3 0.0 copy-done
  34.3 0.0 copy-start.4
  34.3 2.7 %convolution_convert_fusion.1 = bf16[512,512]{0,1:T(8,128)(2,1)} fusion(bf16[512,3072]{1,0:T(8,128)(2,1)S(1)} %bitcast.37, bf16[3072,512]{1,0:T(8,128)(2,1)S(1)} %copy-done), kind=kOutput, calls=%fused_computation.5 | convolution fusion | flops 1610874880 | bytes 6815744 | tf_op jit(solution)/shard_map/dot_general | solution.py:50
  37.0 0.0 copy-done.4
  37.0 0.0 copy-start.5
  37.0 1.8 %convolution_convert_fusion.2 = bf16[512,512]{0,1:T(8,128)(2,1)S(1)} fusion(bf16[512,3072]{1,0:T(8,128)(2,1)S(1)} %bitcast.38, bf16[3072,512]{1,0:T(8,128)(2,1)S(1)} %copy-done.4), kind=kOutput, calls=%fused_computation.6 | convolution fusion | flops 1610874880 | bytes 6815744 | tf_op jit(solution)/shard_map/dot_general | solution.py:54
  38.8 0.0 copy-done.5
  38.9 0.0 copy-start.2
  38.9 1.8 %convolution_convert_fusion.3 = bf16[512,512]{0,1:T(8,128)(2,1)S(1)} fusion(bf16[512,3072]{1,0:T(8,128)(2,1)S(1)} %bitcast.39, bf16[3072,512]{1,0:T(8,128)(2,1)S(1)} %copy-done.5), kind=kOutput, calls=%fused_computation.7 | convolution fusion | flops 1610874880 | bytes 6815744 | tf_op jit(solution)/shard_map/dot_general | solution.py:53
  40.7 0.0 copy-start.3
  40.7 0.0 copy-done.2
  40.7 0.3 fusion.8
  41.0 20.2 %all_to_all.22 = bf16[32,16,128]{2,1,0:T(8,128)(2,1)S(1)} all-to-all(bf16[32,16,128]{2,1,0:T(8,128)(2,1)S(1)} %bitcast.42), channel_id=1, replica_groups=mesh['ctx'=32,'y'=4,'core'=2] {'ctx'}, dimensions={0} | all-to-all | bytes 262144 | tf_op jit(solution)/shard_map/all_to_all | solution.py:23
  61.2 0.0 copy-done.3
  61.2 0.2 fusion.2
  61.4 0.7 copy.23
  62.0 3.9 %all-to-all-start.3 = ((bf16[32,16,128]{2,1,0:T(8,128)(2,1)}), bf16[32,16,128]{2,1,0:T(8,128)(2,1)S(1)}, u32[]{:S(2)}, u32[]{:S(2)}) async-start(bf16[32,16,128]{2,1,0:T(8,128)(2,1)} %bitcast.19), calls=%async_computation.3 | async-start | bytes 262144 | tf_op jit(solution)/shard_map/all_to_all | solution.py:30
  65.9 3.6 %fusion.1 = f32[1,512,4,128]{1,3,2,0:T(8,128)} fusion(bf16[512,4,128]{0,2,1:T(8,128)(2,1)} %bitcast.45, bf16[512,4,128]{0,2,1:T(8,128)(2,1)} %bitcast.47, bf16[1,512,4,128]{1,3,2,0:T(8,128)(2,1)} %bitcast.43), kind=kOutput, calls=%fused_computation.4 | convolution fusion | flops 540016640 | bytes 2621440 | tf_op jit(solution)/shard_map/bhqk,bkhe->bqhe/dot_general | solution.py:77
  69.6 2.5 %copy.21.inner_ref = f32[512,512]{1,0:T(8,128)} copy(f32[512,512]{0,1:T(8,128)} %bitcast.40) | data formatting | bytes 2097152 | tf_op jit(solution)/shard_map/reshape | solution.py:82
  72.1 2.1 %copy.20.query_ref = bf16[512,512]{1,0:T(8,128)(2,1)} copy(bf16[512,512]{0,1:T(8,128)(2,1)} %convolution_convert_fusion.1) | data formatting | bytes 1048576 | tf_op jit(solution)/shard_map/reshape | solution.py:80
  74.2 1.1 %all-to-all-done.3 = bf16[32,16,128]{2,1,0:T(8,128)(2,1)S(1)} async-done(((bf16[32,16,128]{2,1,0:T(8,128)(2,1)}), bf16[32,16,128]{2,1,0:T(8,128)(2,1)S(1)}, u32[]{:S(2)}, u32[]{:S(2)}) %all-to-all-start.3) | async-done | bytes 131104 | tf_op jit(solution)/shard_map/all_to_all | solution.py:30
  75.3 0.0 copy-start.1
  75.3 0.6 copy-done.1
  75.9 2.8 %shard_map.55 = bf16[512,512]{1,0:T(8,128)(2,1)} custom-call(bf16[512,512]{1,0:T(8,128)(2,1)} %copy.20.query_ref, bf16[4,128,128]{2,1,0:T(8,128)(2,1)} %bitcast.41, f32[512,512]{1,0:T(8,128)} %copy.21.inner_ref, f32[1,512]{1,0:T(1,128)} %bitcast.49), custom_call_target="tpu_custom_call" | custom-call | tf_op jit(solution)/shard_map/pallas_call | solution.py:105
Async XLA Ops:
  0.0 34.3 %copy-start = (bf16[3072,512]{1,0:T(8,128)(2,1)S(1)}, bf16[3072,512]{1,0:T(8,128)(2,1)}, u32[]{:S(2)}) copy-start(bf16[3072,512]{1,0:T(8,128)(2,1)} %param.6) | copy-start | bytes 9437188
  34.3 2.7 %copy-start.4 = (bf16[3072,512]{1,0:T(8,128)(2,1)S(1)}, bf16[3072,512]{1,0:T(8,128)(2,1)}, u32[]{:S(2)}) copy-start(bf16[3072,512]{1,0:T(8,128)(2,1)} %param.8) | copy-start | bytes 9437188
  37.0 1.9 %copy-start.5 = (bf16[3072,512]{1,0:T(8,128)(2,1)S(1)}, bf16[3072,512]{1,0:T(8,128)(2,1)}, u32[]{:S(2)}) copy-start(bf16[3072,512]{1,0:T(8,128)(2,1)} %param.7) | copy-start | bytes 9437188
  38.9 1.9 %copy-start.2 = (bf16[512,512]{0,1:T(8,128)(2,1)}, bf16[512,512]{0,1:T(8,128)(2,1)S(1)}, u32[]{:S(2)}) copy-start(bf16[512,512]{0,1:T(8,128)(2,1)S(1)} %convolution_convert_fusion.2) | copy-start | bytes 1572868
  40.7 20.5 %copy-start.3 = (bf16[512,512]{0,1:T(8,128)(2,1)}, bf16[512,512]{0,1:T(8,128)(2,1)S(1)}, u32[]{:S(2)}) copy-start(bf16[512,512]{0,1:T(8,128)(2,1)S(1)} %convolution_convert_fusion.3) | copy-start | bytes 1572868
  62.0 13.2 %all-to-all-start.3 = ((bf16[32,16,128]{2,1,0:T(8,128)(2,1)}), bf16[32,16,128]{2,1,0:T(8,128)(2,1)S(1)}, u32[]{:S(2)}, u32[]{:S(2)}) async-start(bf16[32,16,128]{2,1,0:T(8,128)(2,1)} %bitcast.19), calls=%async_computation.3 | async-start | bytes 262144 | tf_op jit(solution)/shard_map/all_to_all | solution.py:30
  75.3 0.7 copy-start.1

commit v19 on v17

--- a/solution.py
+++ b/solution.py
@@ -100,18 +100,17 @@
 def finish(query, start, inner, gain, head_count):
     rows, width = query.shape
     blocks = rows // BLOCK
-    parts = 2 if head_count % 2 == 0 else 1
-    group = head_count // parts
-    tile = pl.BlockSpec((BLOCK, group * HEAD_DIM), lambda b, p: (b, p))
+    parts = 2
+    tile = pl.BlockSpec((BLOCK // parts, width), lambda b, p: (b * parts + p, 0))
     return pl.pallas_call(
         finish_kernel,
         out_shape=jax.ShapeDtypeStruct(query.shape, jnp.bfloat16),
         grid=(blocks, parts),
         in_specs=[
             tile,
-            pl.BlockSpec((group, HEAD_DIM, HEAD_DIM), lambda b, p: (b * parts + p, 0, 0)),
+            pl.BlockSpec((head_count, HEAD_DIM, HEAD_DIM), lambda b, p: (b, 0, 0)),
             tile,
-            pl.BlockSpec((1, group * HEAD_DIM), lambda b, p: (0, p)),
+            pl.BlockSpec((1, width), lambda b, p: (0, 0)),
         ],
         out_specs=tile,
     )(query, start, inner, gain)

time: 79.7 us -> 79.7 us (level)
  no operation moved by 1% of the time
where the time goes in v19:
time: 79.7 us; the launch traced here: 79.3 us
  blocking collectives  32.4 us (41%)
  starting transfers between devices  16.3 us (20%)
  matrix products  13.8 us (17%)
  waiting for transfers between devices  7.18 us (9%)
  local copies, waits for them, and re-layouts  6.9 us (9%)
  Pallas kernels  2.62 us (3%)
    all_to_all x2, blocking collectives, spread(): return lax.all_to_all(copies, axis, 0, 0, tiled=True)  32.4 us
    all_to_all x1, starting transfers between devices, exclusive_scan(): gathered = lax.all_to_all(pieces, axis, 0, 0, tiled=True)  11 us
    dot_general x1, matrix products, body(): jnp.dot(piece_rows, w_query, preferred_element_type=jnp.float32)  5.43 us
    all_to_all x1, starting transfers between devices, exclusive_scan(): lax.all_to_all(before.reshape(pieces.shape), axis, 0, 0, tiled=True)  5.3 us
    all_to_all x1, waiting for transfers between devices, exclusive_scan(): gathered = lax.all_to_all(pieces, axis, 0, 0, tiled=True)  3.92 us
    dot_general x1, matrix products, body(): jnp.einsum('bhqk,bkhe->bqhe', scores, value_rows, preferred_element_type=...  3.57 us
    all_to_all x1, waiting for transfers between devices, exclusive_scan(): lax.all_to_all(before.reshape(pieces.shape), axis, 0, 0, tiled=True)  3.26 us
    pallas_call x1, Pallas kernels, finish(): pl.pallas_call(finish_kernel, out_shape=jax.ShapeDtypeStruct(query.shape,...  2.62 us
  transfers between devices with their start and end apart: 2, of which 2 were waited for; matrix products, arithmetic and copies ran while one was open for 15% of the time, Pallas kernels for 0%

profile of v19, /device:TPU:1, one launch (start us, length us, event | category | flops | bytes accessed | tf_op | source)
XLA Modules:
  0.0 79.3 jit_solution(15887778105593932055)
XLA Ops:
  0.0 0.0 copy-start
  0.0 1.3 %broadcast_in_dim.7 = bf16[4,64,3072]{2,1,0:T(8,128)(2,1)S(1)} broadcast(bf16[64,3072]{1,0:T(8,128)(2,1)} %param.5), dimensions={1,2} | broadcast | bytes 1966080 | tf_op jit(solution)/shard_map/broadcast_in_dim | solution.py:36
  1.3 24.7 %all_to_all.20 = bf16[4,64,3072]{2,1,0:T(8,128)(2,1)S(1)} all-to-all(bf16[4,64,3072]{2,1,0:T(8,128)(2,1)S(1)} %broadcast_in_dim.7), channel_id=1, replica_groups=mesh['ctx'=32,'y'=4,'core'=2] {'y'}, dimensions={0} | all-to-all | bytes 3145728 | tf_op jit(solution)/shard_map/all_to_all | solution.py:37
  26.0 0.4 broadcast_in_dim.8
  26.4 7.7 %all_to_all.21 = bf16[2,4,64,3072]{3,2,1,0:T(8,128)(2,1)S(1)} all-to-all(bf16[2,4,64,3072]{3,2,1,0:T(8,128)(2,1)S(1)} %broadcast_in_dim.8), channel_id=1, replica_groups=mesh['ctx'=32,'y'=4,'core'=2] {'core'}, dimensions={0} | all-to-all | bytes 6291456 | tf_op jit(solution)/shard_map/all_to_all | solution.py:37
  34.1 0.2 copy.12
  34.3 0.0 copy-start.1
  34.3 0.0 copy-done
  34.3 0.0 copy-start.5
  34.3 1.9 %convolution_convert_fusion.1 = bf16[512,512]{0,1:T(8,128)(2,1)S(1)} fusion(bf16[512,3072]{1,0:T(8,128)(2,1)S(1)} %bitcast.39, bf16[3072,512]{1,0:T(8,128)(2,1)S(1)} %copy-done), kind=kOutput, calls=%fused_computation.5 | convolution fusion | flops 1610874880 | bytes 6815744 | tf_op jit(solution)/shard_map/dot_general | solution.py:54
  36.2 0.0 copy-done.1
  36.2 1.1 %copy-done.5 = bf16[3072,512]{1,0:T(8,128)(2,1)S(1)} copy-done((bf16[3072,512]{1,0:T(8,128)(2,1)S(1)}, bf16[3072,512]{1,0:T(8,128)(2,1)}, u32[]{:S(2)}) %copy-start.5) | copy-done | bytes 3145752
  37.3 0.0 copy-start.3
  37.3 1.8 %convolution_convert_fusion.2 = bf16[512,512]{0,1:T(8,128)(2,1)S(1)} fusion(bf16[512,3072]{1,0:T(8,128)(2,1)S(1)} %bitcast.40, bf16[3072,512]{1,0:T(8,128)(2,1)S(1)} %copy-done.5), kind=kOutput, calls=%fused_computation.6 | convolution fusion | flops 1610874880 | bytes 6815744 | tf_op jit(solution)/shard_map/dot_general | solution.py:53
  39.2 0.0 copy-start.4
  39.2 0.0 copy-done.3
  39.2 0.9 %convolution_convert_fusion.4 = bf16[4,128,128]{2,1,0:T(8,128)(2,1)} fusion(bf16[512,4,128]{0,2,1:T(8,128)(2,1)S(1)} %bitcast.46, bf16[512,4,128]{0,2,1:T(8,128)(2,1)S(1)} %bitcast.44), kind=kOutput, calls=%fused_computation.8 | convolution fusion | flops 67174400 | bytes 1179648 | tf_op jit(solution)/shard_map/bshd,bshe->bhde/dot_general | solution.py:63
  40.1 0.0 copy-done.4
  40.1 11.0 %all-to-all-start.2 = ((bf16[32,16,128]{2,1,0:T(8,128)(2,1)}), bf16[32,16,128]{2,1,0:T(8,128)(2,1)S(1)}, u32[]{:S(2)}, u32[]{:S(2)}) async-start(bf16[32,16,128]{2,1,0:T(8,128)(2,1)} %bitcast.5), calls=%async_computation.2 | async-start | bytes 262144 | tf_op jit(solution)/shard_map/all_to_all | solution.py:23
  51.2 5.4 %convolution_convert_fusion.3.query_ref = bf16[512,512]{1,0:T(8,128)(2,1)} fusion(bf16[512,3072]{1,0:T(8,128)(2,1)} %bitcast.41, bf16[3072,512]{1,0:T(8,128)(2,1)} %param.6), kind=kOutput, calls=%fused_computation.7 | convolution fusion | flops 1610874880 | bytes 6815744 | tf_op jit(solution)/shard_map/dot_general | solution.py:50
  56.6 3.9 %all-to-all-done.2 = bf16[32,16,128]{2,1,0:T(8,128)(2,1)S(1)} async-done(((bf16[32,16,128]{2,1,0:T(8,128)(2,1)}), bf16[32,16,128]{2,1,0:T(8,128)(2,1)S(1)}, u32[]{:S(2)}, u32[]{:S(2)}) %all-to-all-start.2) | async-done | bytes 131104 | tf_op jit(solution)/shard_map/all_to_all | solution.py:23
  60.5 0.2 fusion.2
  60.7 0.7 copy.24
  61.4 5.3 %all-to-all-start.3 = ((bf16[32,16,128]{2,1,0:T(8,128)(2,1)}), bf16[32,16,128]{2,1,0:T(8,128)(2,1)S(1)}, u32[]{:S(2)}, u32[]{:S(2)}) async-start(bf16[32,16,128]{2,1,0:T(8,128)(2,1)} %bitcast.17), calls=%async_computation.3 | async-start | bytes 262144 | tf_op jit(solution)/shard_map/all_to_all | solution.py:30
  66.7 3.6 %fusion.1 = f32[1,512,4,128]{1,3,2,0:T(8,128)} fusion(bf16[512,4,128]{0,2,1:T(8,128)(2,1)} %bitcast.45, bf16[512,4,128]{0,2,1:T(8,128)(2,1)} %bitcast.47, bf16[512,512]{1,0:T(8,128)(2,1)} %convolution_convert_fusion.3.query_ref), kind=kOutput, calls=%fused_computation.4 | convolution fusion | flops 540016640 | bytes 2621440 | tf_op jit(solution)/shard_map/bhqk,bkhe->bqhe/dot_general | solution.py:76
  70.2 2.5 %copy.21.inner_ref = f32[512,512]{1,0:T(8,128)} copy(f32[512,512]{0,1:T(8,128)} %bitcast.42) | data formatting | bytes 2097152 | tf_op jit(solution)/shard_map/reshape | solution.py:81
  72.8 3.3 %all-to-all-done.3 = bf16[32,16,128]{2,1,0:T(8,128)(2,1)S(1)} async-done(((bf16[32,16,128]{2,1,0:T(8,128)(2,1)}), bf16[32,16,128]{2,1,0:T(8,128)(2,1)S(1)}, u32[]{:S(2)}, u32[]{:S(2)}) %all-to-all-start.3) | async-done | bytes 131104 | tf_op jit(solution)/shard_map/all_to_all | solution.py:30
  76.0 0.0 copy-start.2
  76.0 0.7 copy-done.2
  76.7 2.6 %shard_map.55 = bf16[512,512]{1,0:T(8,128)(2,1)} custom-call(bf16[512,512]{1,0:T(8,128)(2,1)} %convolution_convert_fusion.3.query_ref, bf16[4,128,128]{2,1,0:T(8,128)(2,1)} %bitcast.43, f32[512,512]{1,0:T(8,128)} %copy.21.inner_ref, f32[1,512]{1,0:T(1,128)} %bitcast.49), custom_call_target="tpu_custom_call" | custom-call | tf_op jit(solution)/shard_map/pallas_call | solution.py:105
Async XLA Ops:
  0.0 34.3 %copy-start = (bf16[3072,512]{1,0:T(8,128)(2,1)S(1)}, bf16[3072,512]{1,0:T(8,128)(2,1)}, u32[]{:S(2)}) copy-start(bf16[3072,512]{1,0:T(8,128)(2,1)} %param.8) | copy-start | bytes 9437188
  34.3 1.9 %copy-start.1 = (bf16[2,4,64,3072]{3,2,0,1:T(8,128)(2,1)}, bf16[2,4,64,3072]{3,2,0,1:T(8,128)(2,1)S(1)}, u32[]{:S(2)}) copy-start(bf16[2,4,64,3072]{3,2,0,1:T(8,128)(2,1)S(1)} %copy.12) | copy-start | bytes 9437188
  34.3 3.0 %copy-start.5 = (bf16[3072,512]{1,0:T(8,128)(2,1)S(1)}, bf16[3072,512]{1,0:T(8,128)(2,1)}, u32[]{:S(2)}) copy-start(bf16[3072,512]{1,0:T(8,128)(2,1)} %param.7) | copy-start | bytes 9437188
  37.3 1.9 %copy-start.3 = (bf16[512,512]{0,1:T(8,128)(2,1)}, bf16[512,512]{0,1:T(8,128)(2,1)S(1)}, u32[]{:S(2)}) copy-start(bf16[512,512]{0,1:T(8,128)(2,1)S(1)} %convolution_convert_fusion.1) | copy-start | bytes 1572868
  39.2 1.0 %copy-start.4 = (bf16[512,512]{0,1:T(8,128)(2,1)}, bf16[512,512]{0,1:T(8,128)(2,1)S(1)}, u32[]{:S(2)}) copy-start(bf16[512,512]{0,1:T(8,128)(2,1)S(1)} %convolution_convert_fusion.2) | copy-start | bytes 1572868
  40.1 20.4 %all-to-all-start.2 = ((bf16[32,16,128]{2,1,0:T(8,128)(2,1)}), bf16[32,16,128]{2,1,0:T(8,128)(2,1)S(1)}, u32[]{:S(2)}, u32[]{:S(2)}) async-start(bf16[32,16,128]{2,1,0:T(8,128)(2,1)} %bitcast.5), calls=%async_computation.2 | async-start | bytes 262144 | tf_op jit(solution)/shard_map/all_to_all | solution.py:23
  61.4 14.7 %all-to-all-start.3 = ((bf16[32,16,128]{2,1,0:T(8,128)(2,1)}), bf16[32,16,128]{2,1,0:T(8,128)(2,1)S(1)}, u32[]{:S(2)}, u32[]{:S(2)}) async-start(bf16[32,16,128]{2,1,0:T(8,128)(2,1)} %bitcast.17), calls=%async_computation.3 | async-start | bytes 262144 | tf_op jit(solution)/shard_map/all_to_all | solution.py:30
  76.0 0.7 copy-start.2

commit v20 on v19

--- a/solution.py
+++ b/solution.py
@@ -100,7 +100,7 @@
 def finish(query, start, inner, gain, head_count):
     rows, width = query.shape
     blocks = rows // BLOCK
-    parts = 2
+    parts = 4
     tile = pl.BlockSpec((BLOCK // parts, width), lambda b, p: (b * parts + p, 0))
     return pl.pallas_call(
         finish_kernel,

time: 79.7 us -> 81.1 us (1.018)
  Pallas kernels: 2.62 us -> 4 us
    pallas_call x1, Pallas kernels: 2.62 us -> 4 us  [finish(): pl.pallas_call(finish_kernel, out_shape=jax.ShapeDtypeStruct(query.shape,...]
  transfers between devices with their start and end apart: 2 -> 2, of which waited for: 2 -> 2; matrix products, arithmetic and copies ran while one was open for 15% -> 14% of each run, Pallas kernels for 0% -> 0%
where the time goes in v20:
time: 81.1 us; the launch traced here: 80.7 us
  blocking collectives  32.4 us (40%)
  starting transfers between devices  16.3 us (20%)
  matrix products  13.8 us (17%)
  waiting for transfers between devices  7.18 us (9%)
  local copies, waits for them, and re-layouts  6.9 us (9%)
  Pallas kernels  4 us (5%)
    all_to_all x2, blocking collectives, spread(): return lax.all_to_all(copies, axis, 0, 0, tiled=True)  32.4 us
    all_to_all x1, starting transfers between devices, exclusive_scan(): gathered = lax.all_to_all(pieces, axis, 0, 0, tiled=True)  11 us
    dot_general x1, matrix products, body(): jnp.dot(piece_rows, w_query, preferred_element_type=jnp.float32)  5.43 us
    all_to_all x1, starting transfers between devices, exclusive_scan(): lax.all_to_all(before.reshape(pieces.shape), axis, 0, 0, tiled=True)  5.3 us
    pallas_call x1, Pallas kernels, finish(): pl.pallas_call(finish_kernel, out_shape=jax.ShapeDtypeStruct(query.shape,...  4 us
    all_to_all x1, waiting for transfers between devices, exclusive_scan(): gathered = lax.all_to_all(pieces, axis, 0, 0, tiled=True)  3.92 us
    dot_general x1, matrix products, body(): jnp.einsum('bhqk,bkhe->bqhe', scores, value_rows, preferred_element_type=...  3.57 us
    all_to_all x1, waiting for transfers between devices, exclusive_scan(): lax.all_to_all(before.reshape(pieces.shape), axis, 0, 0, tiled=True)  3.26 us
  transfers between devices with their start and end apart: 2, of which 2 were waited for; matrix products, arithmetic and copies ran while one was open for 14% of the time, Pallas kernels for 0%

profile of v20, /device:TPU:1, one launch (start us, length us, event | category | flops | bytes accessed | tf_op | source)
XLA Modules:
  0.0 80.7 jit_solution(1834226032919549525)
XLA Ops:
  0.0 0.0 copy-start
  0.0 1.3 %broadcast_in_dim.7 = bf16[4,64,3072]{2,1,0:T(8,128)(2,1)S(1)} broadcast(bf16[64,3072]{1,0:T(8,128)(2,1)} %param.5), dimensions={1,2} | broadcast | bytes 1966080 | tf_op jit(solution)/shard_map/broadcast_in_dim | solution.py:36
  1.3 24.7 %all_to_all.20 = bf16[4,64,3072]{2,1,0:T(8,128)(2,1)S(1)} all-to-all(bf16[4,64,3072]{2,1,0:T(8,128)(2,1)S(1)} %broadcast_in_dim.7), channel_id=1, replica_groups=mesh['ctx'=32,'y'=4,'core'=2] {'y'}, dimensions={0} | all-to-all | bytes 3145728 | tf_op jit(solution)/shard_map/all_to_all | solution.py:37
  26.0 0.4 broadcast_in_dim.8
  26.4 7.7 %all_to_all.21 = bf16[2,4,64,3072]{3,2,1,0:T(8,128)(2,1)S(1)} all-to-all(bf16[2,4,64,3072]{3,2,1,0:T(8,128)(2,1)S(1)} %broadcast_in_dim.8), channel_id=1, replica_groups=mesh['ctx'=32,'y'=4,'core'=2] {'core'}, dimensions={0} | all-to-all | bytes 6291456 | tf_op jit(solution)/shard_map/all_to_all | solution.py:37
  34.1 0.2 copy.12
  34.3 0.0 copy-start.1
  34.3 0.0 copy-done
  34.3 0.0 copy-start.5
  34.3 1.9 %convolution_convert_fusion.1 = bf16[512,512]{0,1:T(8,128)(2,1)S(1)} fusion(bf16[512,3072]{1,0:T(8,128)(2,1)S(1)} %bitcast.39, bf16[3072,512]{1,0:T(8,128)(2,1)S(1)} %copy-done), kind=kOutput, calls=%fused_computation.5 | convolution fusion | flops 1610874880 | bytes 6815744 | tf_op jit(solution)/shard_map/dot_general | solution.py:54
  36.2 0.0 copy-done.1
  36.2 1.1 %copy-done.5 = bf16[3072,512]{1,0:T(8,128)(2,1)S(1)} copy-done((bf16[3072,512]{1,0:T(8,128)(2,1)S(1)}, bf16[3072,512]{1,0:T(8,128)(2,1)}, u32[]{:S(2)}) %copy-start.5) | copy-done | bytes 3145752
  37.3 0.0 copy-start.3
  37.3 1.8 %convolution_convert_fusion.2 = bf16[512,512]{0,1:T(8,128)(2,1)S(1)} fusion(bf16[512,3072]{1,0:T(8,128)(2,1)S(1)} %bitcast.40, bf16[3072,512]{1,0:T(8,128)(2,1)S(1)} %copy-done.5), kind=kOutput, calls=%fused_computation.6 | convolution fusion | flops 1610874880 | bytes 6815744 | tf_op jit(solution)/shard_map/dot_general | solution.py:53
  39.2 0.0 copy-start.4
  39.2 0.0 copy-done.3
  39.2 0.9 %convolution_convert_fusion.4 = bf16[4,128,128]{2,1,0:T(8,128)(2,1)} fusion(bf16[512,4,128]{0,2,1:T(8,128)(2,1)S(1)} %bitcast.46, bf16[512,4,128]{0,2,1:T(8,128)(2,1)S(1)} %bitcast.44), kind=kOutput, calls=%fused_computation.8 | convolution fusion | flops 67174400 | bytes 1179648 | tf_op jit(solution)/shard_map/bshd,bshe->bhde/dot_general | solution.py:63
  40.1 0.0 copy-done.4
  40.1 11.0 %all-to-all-start.2 = ((bf16[32,16,128]{2,1,0:T(8,128)(2,1)}), bf16[32,16,128]{2,1,0:T(8,128)(2,1)S(1)}, u32[]{:S(2)}, u32[]{:S(2)}) async-start(bf16[32,16,128]{2,1,0:T(8,128)(2,1)} %bitcast.5), calls=%async_computation.2 | async-start | bytes 262144 | tf_op jit(solution)/shard_map/all_to_all | solution.py:23
  51.2 5.4 %convolution_convert_fusion.3.query_ref = bf16[512,512]{1,0:T(8,128)(2,1)} fusion(bf16[512,3072]{1,0:T(8,128)(2,1)} %bitcast.41, bf16[3072,512]{1,0:T(8,128)(2,1)} %param.6), kind=kOutput, calls=%fused_computation.7 | convolution fusion | flops 1610874880 | bytes 6815744 | tf_op jit(solution)/shard_map/dot_general | solution.py:50
  56.6 3.9 %all-to-all-done.2 = bf16[32,16,128]{2,1,0:T(8,128)(2,1)S(1)} async-done(((bf16[32,16,128]{2,1,0:T(8,128)(2,1)}), bf16[32,16,128]{2,1,0:T(8,128)(2,1)S(1)}, u32[]{:S(2)}, u32[]{:S(2)}) %all-to-all-start.2) | async-done | bytes 131104 | tf_op jit(solution)/shard_map/all_to_all | solution.py:23
  60.5 0.2 fusion.2
  60.7 0.7 copy.24
  61.4 5.3 %all-to-all-start.3 = ((bf16[32,16,128]{2,1,0:T(8,128)(2,1)}), bf16[32,16,128]{2,1,0:T(8,128)(2,1)S(1)}, u32[]{:S(2)}, u32[]{:S(2)}) async-start(bf16[32,16,128]{2,1,0:T(8,128)(2,1)} %bitcast.17), calls=%async_computation.3 | async-start | bytes 262144 | tf_op jit(solution)/shard_map/all_to_all | solution.py:30
  66.7 3.6 %fusion.1 = f32[1,512,4,128]{1,3,2,0:T(8,128)} fusion(bf16[512,4,128]{0,2,1:T(8,128)(2,1)} %bitcast.45, bf16[512,4,128]{0,2,1:T(8,128)(2,1)} %bitcast.47, bf16[512,512]{1,0:T(8,128)(2,1)} %convolution_convert_fusion.3.query_ref), kind=kOutput, calls=%fused_computation.4 | convolution fusion | flops 540016640 | bytes 2621440 | tf_op jit(solution)/shard_map/bhqk,bkhe->bqhe/dot_general | solution.py:76
  70.2 2.5 %copy.21.inner_ref = f32[512,512]{1,0:T(8,128)} copy(f32[512,512]{0,1:T(8,128)} %bitcast.42) | data formatting | bytes 2097152 | tf_op jit(solution)/shard_map/reshape | solution.py:81
  72.8 3.3 %all-to-all-done.3 = bf16[32,16,128]{2,1,0:T(8,128)(2,1)S(1)} async-done(((bf16[32,16,128]{2,1,0:T(8,128)(2,1)}), bf16[32,16,128]{2,1,0:T(8,128)(2,1)S(1)}, u32[]{:S(2)}, u32[]{:S(2)}) %all-to-all-start.3) | async-done | bytes 131104 | tf_op jit(solution)/shard_map/all_to_all | solution.py:30
  76.0 0.0 copy-start.2
  76.0 0.7 copy-done.2
  76.7 4.0 %shard_map.55 = bf16[512,512]{1,0:T(8,128)(2,1)} custom-call(bf16[512,512]{1,0:T(8,128)(2,1)} %convolution_convert_fusion.3.query_ref, bf16[4,128,128]{2,1,0:T(8,128)(2,1)} %bitcast.43, f32[512,512]{1,0:T(8,128)} %copy.21.inner_ref, f32[1,512]{1,0:T(1,128)} %bitcast.49), custom_call_target="tpu_custom_call" | custom-call | tf_op jit(solution)/shard_map/pallas_call | solution.py:105
Async XLA Ops:
  0.0 34.3 %copy-start = (bf16[3072,512]{1,0:T(8,128)(2,1)S(1)}, bf16[3072,512]{1,0:T(8,128)(2,1)}, u32[]{:S(2)}) copy-start(bf16[3072,512]{1,0:T(8,128)(2,1)} %param.8) | copy-start | bytes 9437188
  34.3 1.9 %copy-start.1 = (bf16[2,4,64,3072]{3,2,0,1:T(8,128)(2,1)}, bf16[2,4,64,3072]{3,2,0,1:T(8,128)(2,1)S(1)}, u32[]{:S(2)}) copy-start(bf16[2,4,64,3072]{3,2,0,1:T(8,128)(2,1)S(1)} %copy.12) | copy-start | bytes 9437188
  34.3 3.0 %copy-start.5 = (bf16[3072,512]{1,0:T(8,128)(2,1)S(1)}, bf16[3072,512]{1,0:T(8,128)(2,1)}, u32[]{:S(2)}) copy-start(bf16[3072,512]{1,0:T(8,128)(2,1)} %param.7) | copy-start | bytes 9437188
  37.3 1.9 %copy-start.3 = (bf16[512,512]{0,1:T(8,128)(2,1)}, bf16[512,512]{0,1:T(8,128)(2,1)S(1)}, u32[]{:S(2)}) copy-start(bf16[512,512]{0,1:T(8,128)(2,1)S(1)} %convolution_convert_fusion.1) | copy-start | bytes 1572868
  39.2 1.0 %copy-start.4 = (bf16[512,512]{0,1:T(8,128)(2,1)}, bf16[512,512]{0,1:T(8,128)(2,1)S(1)}, u32[]{:S(2)}) copy-start(bf16[512,512]{0,1:T(8,128)(2,1)S(1)} %convolution_convert_fusion.2) | copy-start | bytes 1572868
  40.1 20.4 %all-to-all-start.2 = ((bf16[32,16,128]{2,1,0:T(8,128)(2,1)}), bf16[32,16,128]{2,1,0:T(8,128)(2,1)S(1)}, u32[]{:S(2)}, u32[]{:S(2)}) async-start(bf16[32,16,128]{2,1,0:T(8,128)(2,1)} %bitcast.5), calls=%async_computation.2 | async-start | bytes 262144 | tf_op jit(solution)/shard_map/all_to_all | solution.py:23
  61.4 14.7 %all-to-all-start.3 = ((bf16[32,16,128]{2,1,0:T(8,128)(2,1)}), bf16[32,16,128]{2,1,0:T(8,128)(2,1)S(1)}, u32[]{:S(2)}, u32[]{:S(2)}) async-start(bf16[32,16,128]{2,1,0:T(8,128)(2,1)} %bitcast.17), calls=%async_computation.3 | async-start | bytes 262144 | tf_op jit(solution)/shard_map/all_to_all | solution.py:30
  76.0 0.7 copy-start.2
